TPU v7x, 128 devices: a whole 4x4x4 slice. The times are simulated.
128 devices in a mesh: dp: 8 (over x_hi, z), row: 4 (over x_lo, core), col: 4 (over y).
Axes of the slice: x: 4 (x_hi: 2, x_lo: 2; x = x_hi * 2 + x_lo), y: 4, z: 4, core: 2. Of those that a mesh axis runs over, the one named last changes fastest.
Arguments:
- hidden_acts: bfloat16 [4096, 29568], P('dp', ('row', 'col')), may hold values from -6 to 6
- out_cotangent: bfloat16 [4096, 1024], P('dp'), may hold values from -6 to 6
- is_paraphrase: int32 [4096], P('dp'), may hold values 0 or 1
- token_edit: int32 [4096], P('dp'), may hold values from 0 to 511
- edit_weight: float32 [512], replicated, may hold values from 0.5 to 2
- inverse_gram: bfloat16 [29568, 29568], P(('row', 'col'), 'dp'), may hold values from -1 to 3
- edit_keys: bfloat16 [29568, 512], P('dp'), may hold values from -0.03125 to 0.03125
- edit_slots: int32 [512], replicated, may hold values from 0 to 511, each once
Outputs:
- edit_shift_grads: float32 [512, 1024], P('dp', ('row', 'col'))
Inputs may be any that keep to these rules, and one draw needn't show every extreme that they name: `edit_slots`: every edit number appears in exactly one slot.
All inputs are finite; a program needn't handle non-finite values. No bound on the sum of `is_paraphrase` on one device may be relied on, other than what follows from the above.
Results may differ from a plain program's by a relative error of at most 0.024.
Values may be sent and summed in bfloat16 or wider, within the bound.
No kernel may reach another device: no remote copies, remote signals or barrier semaphores. Data moves between devices by JAX's collectives and lax.ppermute only.
A program may use at most 128 MiB of HBM per device.

v0:
```python
import jax
import jax.numpy as jnp
from jax import lax
from jax.sharding import PartitionSpec as P


def body(
    hidden_acts,
    out_cotangent,
    is_paraphrase,
    token_edit,
    edit_weight,
    inverse_gram,
    edit_keys,
    edit_slots,
):
    tokens = hidden_acts.shape[0] * lax.axis_size("dp")
    edits = edit_weight.shape[0]
    match = token_edit[:, None] == jnp.arange(edits, dtype=jnp.int32)[None, :]
    looked = jnp.sum(jnp.where(match, edit_weight[None, :], jnp.float32(0.0)), axis=1)
    weight = jnp.where(is_paraphrase == 1, looked, jnp.float32(1.0)) / jnp.sqrt(jnp.float32(tokens))
    scaled = (out_cotangent.astype(jnp.float32) * weight[:, None]).astype(jnp.bfloat16)
    partial_grad = lax.dot_general(
        scaled, hidden_acts, (((0,), (0,)), ((), ())), preferred_element_type=jnp.float32
    )
    grad_shift = lax.psum(partial_grad, "dp").astype(jnp.bfloat16)
    pushed_rows = lax.psum_scatter(
        jnp.dot(grad_shift, inverse_gram, preferred_element_type=jnp.float32),
        ("row", "col"),
        scatter_dimension=0,
        tiled=True,
    ).astype(jnp.bfloat16)
    keys = jnp.take(edit_keys, edit_slots, axis=1)
    return lax.psum_scatter(
        lax.dot_general(
            keys, pushed_rows, (((0,), (1,)), ((), ())), preferred_element_type=jnp.float32
        ),
        "dp",
        scatter_dimension=0,
        tiled=True,
    )


def solution(mesh):
    return jax.shard_map(
        body,
        mesh=mesh,
        in_specs=(
            P("dp", ("row", "col")),
            P("dp", None),
            P("dp"),
            P("dp"),
            P(),
            P(("row", "col"), "dp"),
            P("dp", None),
            P(),
        ),
        out_specs=P("dp", ("row", "col")),
        check_vma=False,
    )
```

profile of v0, /device:TPU:0, one launch (start us, length us, event | category | flops | bytes accessed | tf_op | source)
XLA Modules:
  0.0 448.5 jit_solution(1394385368685526929)
XLA Ops:
  6.5 0.0 copy-start
  6.5 0.0 reduce-scatter.3.cloned.1.call-start
  6.5 1.1 select_reduce_fusion
  7.6 0.7 select_multiply_fusion
  8.3 0.0 copy-done
  8.3 6.9 %fusion.6 = f32[1024,1848]{1,0:T(8,128)} fusion(bf16[512,1848]{0,1:T(8,128)(2,1)S(1)} %copy-done, bf16[512,1024]{1,0:T(8,128)(2,1)} %param.9, f32[512]{0:T(512)S(1)} %select_multiply_fusion), kind=kOutput, calls=%fused_computation.8 | convolution fusion | flops 1939341312 | bytes 10512384 | tf_op jit(solution)/shard_map/dot_general | solution.py:23
  15.2 165.8 %all-reduce.1 = bf16[1024,1848]{1,0:T(8,128)(2,1)} all-reduce(f32[1024,1848]{1,0:T(8,128)} %fusion.6), channel_id=1, replica_groups=mesh['dp'=8,'row'=4,'col'=4] {'dp'}, use_global_device_ids=true, to_apply=%region_1.2 | all-reduce | flops 1892352 | bytes 11354112 | tf_op jit(solution)/shard_map/psum | solution.py:26
  181.0 22.5 %fusion.10 = f32[1024,3696]{1,0:T(8,128)} fusion(bf16[1024,1848]{1,0:T(8,128)(2,1)} %all-reduce.1, bf16[1848,3696]{1,0:T(8,128)(2,1)} %param.13), kind=kOutput, calls=%fused_computation.18 | convolution fusion | flops 13988265984 | bytes 32583936 | tf_op jit(solution)/shard_map/dot_general | solution.py:28
  203.5 0.0 reduce-scatter.3.cloned.1.call-update
  203.5 0.0 copy-start.1
  203.5 0.2 reduce-scatter.5.cloned.1.call-start
  203.8 6.2 %copy.10 = bf16[3696,512]{0,1:T(8,128)(2,1)} copy(bf16[3696,512]{1,0:T(8,128)(2,1)} %param.14) | data formatting | bytes 7569408 | tf_op args[6]
  209.9 0.0 copy-done.1
  209.9 10.8 %gather_fusion = bf16[512,3696]{1,0:T(8,128)(2,1)} fusion(bf16[3696,512]{0,1:T(8,128)(2,1)} %copy.10, s32[1024]{0:T(1024)S(1)} %pad_clamp_fusion), kind=kCustom, calls=%fused_computation | custom fusion | bytes 7571456 | tf_op jit(solution)/shard_map/jit(_take)/gather | solution.py:33
  220.7 144.9 %reduce-scatter.3.cloned.1.call-done = f32[64,3696]{1,0:T(8,128)} async-done(((f32[1024,3696]{1,0:T(8,128)}), f32[64,3696]{1,0:T(8,128)}) %reduce-scatter.3.cloned.1.call-update) | async-done | bytes 946192 | tf_op jit(solution)/shard_map/reduce_scatter | solution.py:27
  365.6 4.2 fusion.2
  369.8 0.0 reduce-scatter.5.cloned.1.call-update
  369.9 71.8 %reduce-scatter.5.cloned.1.call-done = f32[64,64]{1,0:T(8,128)} async-done(((f32[512,64]{1,0:T(8,128)}), f32[64,64]{1,0:T(8,128)}) %reduce-scatter.5.cloned.1.call-update) | async-done | bytes 16400 | tf_op jit(solution)/shard_map/reduce_scatter | solution.py:34
  (3 shorter events, 0.0 us)
Async XLA Ops:
  6.5 1.8 copy-start
  6.5 359.1 %reduce-scatter.3.cloned.1.call-start = ((), (), s32[]{:S(2)}) async-start(), calls=%async_computation.2 | async-start | bytes 16154624 | tf_op jit(solution)/shard_map/reduce_scatter | solution.py:27
  203.5 6.4 %copy-start.1 = (s32[512]{0:T(512)S(1)}, s32[512]{0:T(512)}, u32[]{:S(2)}) copy-start(s32[512]{0:T(512)} %param.15) | copy-start | bytes 6148
  203.5 238.1 %reduce-scatter.5.cloned.1.call-start = ((), (), s32[]{:S(2)}) async-start(), calls=%async_computation.3 | async-start | bytes 294912 | tf_op jit(solution)/shard_map/reduce_scatter | solution.py:34
Sparse Core Ops, SparseCore 0:
  203.6 161.9 reduce-scatter.2
  370.0 71.6 reduce-scatter.4
where the time goes:
time: 449 us
  waiting for transfers between devices  217 us (48%)
  blocking collectives  166 us (37%)
  matrix products  33.7 us (8%)
  local copies, waits for them, and re-layouts  17 us (4%)
  between operations  13.4 us (3%)
    psum x1, blocking collectives, body(): grad_shift = lax.psum(partial_grad, 'dp').astype(jnp.bfloat16)  166 us
    reduce_scatter x1, waiting for transfers between devices, body(): lax.psum_scatter(jnp.dot(grad_shift, inverse_gram, preferred_element_type...  145 us
    reduce_scatter x1, waiting for transfers between devices, body(): lax.psum_scatter(lax.dot_general(keys, pushed_rows, (((0,), (1,)), ((), (...  71.8 us
    dot_general x1, matrix products, body(): jnp.dot(grad_shift, inverse_gram, preferred_element_type=jnp.float32)  22.5 us
    gather x1, local copies, waits for them, and re-layouts, body(): keys = jnp.take(edit_keys, edit_slots, axis=1)  10.8 us
  transfers between devices with their start and end apart: 2, of which 2 were waited for; matrix products, arithmetic and copies ran while one was open for 4% of the time, Pallas kernels for 0%

commit v1 on v0

--- a/solution.py
+++ b/solution.py
@@ -20,25 +20,23 @@
     looked = jnp.sum(jnp.where(match, edit_weight[None, :], jnp.float32(0.0)), axis=1)
     weight = jnp.where(is_paraphrase == 1, looked, jnp.float32(1.0)) / jnp.sqrt(jnp.float32(tokens))
     scaled = (out_cotangent.astype(jnp.float32) * weight[:, None]).astype(jnp.bfloat16)
-    partial_grad = lax.dot_general(
-        scaled, hidden_acts, (((0,), (0,)), ((), ())), preferred_element_type=jnp.float32
+
+    gram_keys = jnp.dot(inverse_gram, edit_keys, preferred_element_type=jnp.float32)
+    gram_keys = lax.psum(gram_keys, "dp").astype(jnp.bfloat16)
+    acts_keys = jnp.dot(hidden_acts, gram_keys, preferred_element_type=jnp.float32)
+    acts_keys = lax.psum(acts_keys, ("row", "col"))
+    rows = out_cotangent.shape[1] // (lax.axis_size("row") * lax.axis_size("col"))
+    block = lax.axis_index("row") * lax.axis_size("col") + lax.axis_index("col")
+    scaled_rows = lax.dynamic_slice_in_dim(scaled, block * rows, rows, axis=1)
+    partial = lax.dot_general(
+        acts_keys,
+        scaled_rows.astype(jnp.float32),
+        (((0,), (0,)), ((), ())),
+        precision=lax.Precision.HIGHEST,
+        preferred_element_type=jnp.float32,
     )
-    grad_shift = lax.psum(partial_grad, "dp").astype(jnp.bfloat16)
-    pushed_rows = lax.psum_scatter(
-        jnp.dot(grad_shift, inverse_gram, preferred_element_type=jnp.float32),
-        ("row", "col"),
-        scatter_dimension=0,
-        tiled=True,
-    ).astype(jnp.bfloat16)
-    keys = jnp.take(edit_keys, edit_slots, axis=1)
-    return lax.psum_scatter(
-        lax.dot_general(
-            keys, pushed_rows, (((0,), (1,)), ((), ())), preferred_element_type=jnp.float32
-        ),
-        "dp",
-        scatter_dimension=0,
-        tiled=True,
-    )
+    partial = jnp.take(partial, edit_slots, axis=0)
+    return lax.psum_scatter(partial, "dp", scatter_dimension=0, tiled=True)
 
 
 def solution(mesh):

time: 449 us -> 322 us (0.72)
  blocking collectives: 166 us -> 96 us
  waiting for transfers between devices: 217 us -> 191 us
  local copies, waits for them, and re-layouts: 17 us -> 1.06 us
  matrix products: 33.7 us -> 18.9 us
    reduce_scatter x2 -> x1, waiting for transfers between devices: 217 us -> 71.5 us  [body(): return lax.psum_scatter(partial, 'dp', scatter_dimension=0, tiled=True)]
    psum x0 -> x1, waiting for transfers between devices: none -> 120 us  [body(): acts_keys = lax.psum(acts_keys, ('row', 'col'))]
    psum x1, blocking collectives: 166 us -> 96 us  [body(): gram_keys = lax.psum(gram_keys, 'dp').astype(jnp.bfloat16)]
    dot_general x3, matrix products: 33.7 us -> 18.9 us  [the longest x1 13.1 us: body(): jnp.dot(inverse_gram, edit_keys, preferred_element_type=jnp.float32)]
    gather x1, local copies, waits for them, and re-layouts: 10.8 us -> 1.04 us  [body(): partial = jnp.take(partial, edit_slots, axis=0)]
    unnamed x5 -> x10, local copies, waits for them, and re-layouts: 6.17 us -> 0.02 us
  transfers between devices with their start and end apart: 2 -> 2, of which waited for: 2 -> 2; matrix products, arithmetic and copies ran while one was open for 4% -> 0% of each run, Pallas kernels for 0% -> 0%
where the time goes in v1:
time: 322 us
  waiting for transfers between devices  191 us (59%)
  blocking collectives  96 us (30%)
  matrix products  18.9 us (6%)
  between operations  13.5 us (4%)
    psum x1, waiting for transfers between devices, body(): acts_keys = lax.psum(acts_keys, ('row', 'col'))  120 us
    psum x1, blocking collectives, body(): gram_keys = lax.psum(gram_keys, 'dp').astype(jnp.bfloat16)  96 us
    reduce_scatter x1, waiting for transfers between devices, body(): return lax.psum_scatter(partial, 'dp', scatter_dimension=0, tiled=True)  71.5 us
    dot_general x1, matrix products, body(): jnp.dot(inverse_gram, edit_keys, preferred_element_type=jnp.float32)  13.1 us
  transfers between devices with their start and end apart: 2, of which 2 were waited for; matrix products, arithmetic and copies ran while one was open for 0% of the time, Pallas kernels for 0%

profile of v1, /device:TPU:0, one launch (start us, length us, event | category | flops | bytes accessed | tf_op | source)
XLA Modules:
  0.0 321.6 jit_solution(8364792604882470710)
XLA Ops:
  6.5 0.0 copy-start
  6.5 0.0 all-reduce.3.cloned.1.call-start
  6.5 13.1 %fusion.9 = f32[1848,512]{1,0:T(8,128)} fusion(bf16[1848,3696]{1,0:T(8,128)(2,1)} %param.13, bf16[3696,512]{1,0:T(8,128)(2,1)} %param.14), kind=kOutput, calls=%fused_computation.16 | convolution fusion | flops 6994132992 | bytes 21229824 | tf_op jit(solution)/shard_map/dot_general | solution.py:24
  19.6 96.0 %all-reduce.4 = bf16[1848,512]{1,0:T(8,128)(2,1)} all-reduce(f32[1848,512]{1,0:T(8,128)} %fusion.9), channel_id=1, replica_groups=mesh['dp'=8,'row'=4,'col'=4] {'dp'}, use_global_device_ids=true, to_apply=%region_0.1 | all-reduce | flops 946176 | bytes 5677056 | tf_op jit(solution)/shard_map/psum | solution.py:25
  115.6 0.0 copy-done
  115.6 0.0 copy-start.1
  115.6 0.0 copy-start.2
  115.6 0.0 copy-start.3
  115.6 0.0 copy-start.4
  115.6 3.8 %fusion.2 = f32[512,512]{0,1:T(8,128)} fusion(bf16[512,1848]{0,1:T(8,128)(2,1)S(1)} %copy-done, bf16[1848,512]{1,0:T(8,128)(2,1)} %all-reduce.4), kind=kOutput, calls=%fused_computation.3 | convolution fusion | flops 968884224 | bytes 4833280 | tf_op jit(solution)/shard_map/dot_general | solution.py:26
  119.5 0.0 all-reduce.3.cloned.1.call-update
  119.5 0.0 reduce-scatter.2.cloned.1.call-start
  119.6 0.0 copy-done.1
  119.6 0.0 copy-done.2
  119.6 0.0 copy-done.3
  119.6 0.2 select_reduce_fusion
  119.9 0.0 copy-done.4
  119.9 119.5 %all-reduce.3.cloned.1.call-done = f32[512,512]{0,1:T(8,128)} async-done(((f32[512,512]{0,1:T(8,128)}), f32[512,512]{0,1:T(8,128)}) %all-reduce.3.cloned.1.call-update) | async-done | bytes 1048592 | tf_op jit(solution)/shard_map/psum | solution.py:27
  239.4 1.9 fusion.5
  241.4 1.0 gather_fusion
  242.4 0.8 broadcast_select_fusion
  243.2 0.0 reduce-scatter.2.cloned.1.call-update
  243.3 71.5 %reduce-scatter.2.cloned.1.call-done = f32[64,64]{1,0:T(8,128)} async-done(((f32[512,64]{1,0:T(8,128)}), f32[64,64]{1,0:T(8,128)}) %reduce-scatter.2.cloned.1.call-update) | async-done | bytes 16400 | tf_op jit(solution)/shard_map/reduce_scatter | solution.py:39
  (4 shorter events, 0.0 us)
Async XLA Ops:
  6.5 109.1 %copy-start = (bf16[512,1848]{0,1:T(8,128)(2,1)S(1)}, bf16[512,1848]{0,1:T(8,128)(2,1)}, u32[]{:S(2)}) copy-start(bf16[512,1848]{0,1:T(8,128)(2,1)} %param.8) | copy-start | bytes 5677060
  6.5 232.9 %all-reduce.3.cloned.1.call-start = ((), (), s32[]{:S(2)}) async-start(), calls=%async_computation.1 | async-start | bytes 2097152 | tf_op jit(solution)/shard_map/psum | solution.py:27
  115.6 3.9 %copy-start.1 = (s32[512]{0:T(512)S(1)}, s32[512]{0:T(512)}, u32[]{:S(2)}) copy-start(s32[512]{0:T(512)} %param.15) | copy-start | bytes 6148
  115.6 4.0 %copy-start.2 = (f32[512]{0:T(512)S(1)}, f32[512]{0:T(512)}, u32[]{:S(2)}) copy-start(f32[512]{0:T(512)} %param.12) | copy-start | bytes 6148
  115.6 4.0 %copy-start.3 = (s32[512]{0:T(512)S(1)}, s32[512]{0:T(512)}, u32[]{:S(2)}) copy-start(s32[512]{0:T(512)} %param.11) | copy-start | bytes 6148
  115.6 4.2 %copy-start.4 = (s32[512]{0:T(512)S(1)}, s32[512]{0:T(512)}, u32[]{:S(2)}) copy-start(s32[512]{0:T(512)} %param.10) | copy-start | bytes 6148
  119.5 195.2 %reduce-scatter.2.cloned.1.call-start = ((), (), s32[]{:S(2)}) async-start(), calls=%async_computation.2 | async-start | bytes 294912 | tf_op jit(solution)/shard_map/reduce_scatter | solution.py:39
Sparse Core Ops, SparseCore 0:
  119.6 119.7 all-reduce.2
  243.4 71.3 reduce-scatter.1

commit v2 on v1

v2 whole, which is shorter than its diff:
```python
import jax
import jax.numpy as jnp
from jax import lax
from jax.sharding import PartitionSpec as P


def reduce_scatter(x, axis, parts):
    pieces = x.reshape((parts, x.shape[0] // parts) + x.shape[1:])
    got = lax.all_to_all(pieces, axis, 0, 0)
    return jnp.sum(got.astype(jnp.float32), axis=0)


def all_gather(x, axis, parts):
    pieces = jnp.broadcast_to(x[None], (parts,) + x.shape)
    got = lax.all_to_all(pieces, axis, 0, 0)
    return got.reshape((parts * x.shape[0],) + x.shape[1:])


def body(
    hidden_acts,
    out_cotangent,
    is_paraphrase,
    token_edit,
    edit_weight,
    inverse_gram,
    edit_keys,
    edit_slots,
):
    n_dp = lax.axis_size("dp")
    n_rc = lax.axis_size("row") * lax.axis_size("col")
    tokens = hidden_acts.shape[0] * n_dp
    edits = edit_weight.shape[0]
    match = token_edit[:, None] == jnp.arange(edits, dtype=jnp.int32)[None, :]
    looked = jnp.sum(jnp.where(match, edit_weight[None, :], jnp.float32(0.0)), axis=1)
    weight = jnp.where(is_paraphrase == 1, looked, jnp.float32(1.0)) / jnp.sqrt(jnp.float32(tokens))
    scaled = (out_cotangent.astype(jnp.float32) * weight[:, None]).astype(jnp.bfloat16)

    gram_keys = jnp.dot(inverse_gram, edit_keys, preferred_element_type=jnp.float32)
    gram_keys = reduce_scatter(gram_keys.astype(jnp.bfloat16), "dp", n_dp)
    gram_keys = all_gather(gram_keys.astype(jnp.bfloat16), "dp", n_dp)
    acts_keys = jnp.dot(hidden_acts, gram_keys, preferred_element_type=jnp.float32)
    acts_keys = reduce_scatter(acts_keys.astype(jnp.bfloat16), ("row", "col"), n_rc)
    acts_keys = all_gather(acts_keys.astype(jnp.bfloat16), ("row", "col"), n_rc)
    rows = out_cotangent.shape[1] // n_rc
    block = lax.axis_index("row") * lax.axis_size("col") + lax.axis_index("col")
    scaled_rows = lax.dynamic_slice_in_dim(scaled, block * rows, rows, axis=1)
    partial = lax.dot_general(
        acts_keys, scaled_rows, (((0,), (0,)), ((), ())), preferred_element_type=jnp.float32
    )
    partial = jnp.take(partial, edit_slots, axis=0)
    return reduce_scatter(partial, "dp", n_dp)


def solution(mesh):
    return jax.shard_map(
        body,
        mesh=mesh,
        in_specs=(
            P("dp", ("row", "col")),
            P("dp", None),
            P("dp"),
            P("dp"),
            P(),
            P(("row", "col"), "dp"),
            P("dp", None),
            P(),
        ),
        out_specs=P("dp", ("row", "col")),
        check_vma=False,
    )
```

time: 322 us -> 135 us (0.42)
  waiting for transfers between devices: 191 us -> 20.8 us
  blocking collectives: 96 us -> 73.6 us
  between operations: 13.5 us -> 0.13 us
  starting transfers between devices: 0.04 us -> 8.72 us
  local copies, waits for them, and re-layouts: 1.06 us -> 9.59 us
    psum x1 -> x0, waiting for transfers between devices: 120 us -> none  [body(): acts_keys = lax.psum(acts_keys, ('row', 'col'))]
    psum x1 -> x0, blocking collectives: 96 us -> none  [body(): gram_keys = lax.psum(gram_keys, 'dp').astype(jnp.bfloat16)]
    all_to_all x0 -> x3, blocking collectives: none -> 73.6 us  [the longest x2 45.4 us: reduce_scatter(): got = lax.all_to_all(pieces, axis, 0, 0)]
    reduce_scatter x1 -> x0, waiting for transfers between devices: 71.5 us -> none  [body(): return lax.psum_scatter(partial, 'dp', scatter_dimension=0, tiled=True)]
    all_to_all x0 -> x2, waiting for transfers between devices: none -> 20.8 us  [the longest x1 10.6 us: reduce_scatter(): got = lax.all_to_all(pieces, axis, 0, 0)]
    all_to_all x0 -> x2, starting transfers between devices: none -> 8.72 us  [the longest x1 5.14 us: reduce_scatter(): got = lax.all_to_all(pieces, axis, 0, 0)]
    reshape x0 -> x2, local copies, waits for them, and re-layouts: none -> 6.69 us  [the longest x1 3.36 us: reduce_scatter(): pieces = x.reshape((parts, x.shape[0] // parts) + x.shape[1:])]
where the time goes in v2:
time: 135 us
  blocking collectives  73.6 us (55%)
  waiting for transfers between devices  20.8 us (15%)
  matrix products  17.8 us (13%)
  local copies, waits for them, and re-layouts  9.59 us (7%)
  starting transfers between devices  8.72 us (6%)
  other arithmetic  3.93 us (3%)
    all_to_all x2, blocking collectives, reduce_scatter(): got = lax.all_to_all(pieces, axis, 0, 0)  45.4 us
    all_to_all x1, blocking collectives, all_gather(): got = lax.all_to_all(pieces, axis, 0, 0)  28.3 us
    dot_general x1, matrix products, body(): jnp.dot(inverse_gram, edit_keys, preferred_element_type=jnp.float32)  12.8 us
    all_to_all x1, waiting for transfers between devices, reduce_scatter(): got = lax.all_to_all(pieces, axis, 0, 0)  10.6 us
    all_to_all x1, waiting for transfers between devices, all_gather(): got = lax.all_to_all(pieces, axis, 0, 0)  10.2 us
    all_to_all x1, starting transfers between devices, reduce_scatter(): got = lax.all_to_all(pieces, axis, 0, 0)  5.14 us
    dot_general x1, matrix products, body(): jnp.dot(hidden_acts, gram_keys, preferred_element_type=jnp.float32)  3.62 us
    all_to_all x1, starting transfers between devices, all_gather(): got = lax.all_to_all(pieces, axis, 0, 0)  3.57 us
  transfers between devices with their start and end apart: 2, of which 2 were waited for; matrix products, arithmetic and copies ran while one was open for 0% of the time, Pallas kernels for 0%

profile of v2, /device:TPU:0, one launch (start us, length us, event | category | flops | bytes accessed | tf_op | source)
XLA Modules:
  0.0 134.5 jit_solution(4184084246598543934)
XLA Ops:
  0.0 0.0 copy-start
  0.0 12.8 %convolution_convert_fusion = bf16[1848,512]{1,0:T(8,128)(2,1)} fusion(bf16[1848,3696]{1,0:T(8,128)(2,1)} %param.13, bf16[3696,512]{1,0:T(8,128)(2,1)} %param.14), kind=kOutput, calls=%fused_computation.1 | convolution fusion | flops 6995079168 | bytes 19337472 | tf_op jit(solution)/shard_map/dot_general | solution.py:38
  12.8 3.4 %reshape.29 = bf16[8,231,512]{2,1,0:T(8,128)(2,1)} reshape(bf16[1848,512]{1,0:T(8,128)(2,1)} %convolution_convert_fusion) | data formatting | bytes 3784704 | tf_op jit(solution)/shard_map/reshape | solution.py:8
  16.1 34.4 %all_to_all.25 = bf16[8,231,512]{2,1,0:T(8,128)(2,1)} all-to-all(bf16[8,231,512]{2,1,0:T(8,128)(2,1)} %reshape.29), channel_id=1, replica_groups=mesh['dp'=8,'row'=4,'col'=4] {'dp'}, dimensions={0} | all-to-all | bytes 3784704 | tf_op jit(solution)/shard_map/all_to_all | solution.py:9
  50.6 1.8 %reduce_sum.42 = bf16[231,512]{1,0:T(8,128)(2,1)S(1)} reduce(bf16[8,231,512]{2,1,0:T(8,128)(2,1)} %all_to_all.25, bf16[]{:T(256)} %constant.13.clone.1), dimensions={0}, to_apply=%region_0.1 | reduce | flops 827904 | bytes 2128898 | tf_op jit(solution)/shard_map/reduce_sum | solution.py:10
  52.4 0.1 broadcast_in_dim.48
  52.6 28.3 %all_to_all.26 = bf16[8,231,512]{2,1,0:T(8,128)(2,1)} all-to-all(bf16[8,231,512]{2,1,0:T(8,128)(2,1)S(1)} %broadcast_in_dim.48), channel_id=1, replica_groups=mesh['dp'=8,'row'=4,'col'=4] {'dp'}, dimensions={0} | all-to-all | bytes 3784704 | tf_op jit(solution)/shard_map/all_to_all | solution.py:15
  80.8 3.3 %reshape.30 = bf16[1848,512]{1,0:T(8,128)(2,1)} reshape(bf16[8,231,512]{2,1,0:T(8,128)(2,1)} %all_to_all.26) | data formatting | bytes 3784704 | tf_op jit(solution)/shard_map/reshape | solution.py:16
  84.2 0.0 copy-done
  84.2 0.0 copy-start.1
  84.2 3.6 %convolution_convert_fusion.1 = bf16[512,512]{0,1:T(8,128)(2,1)} fusion(bf16[1848,512]{1,0:T(8,128)(2,1)} %reshape.30, bf16[512,1848]{0,1:T(8,128)(2,1)S(1)} %copy-done), kind=kOutput, calls=%fused_computation.2 | convolution fusion | flops 969146368 | bytes 4308992 | tf_op jit(solution)/shard_map/dot_general | solution.py:41
  87.8 0.0 copy-start.2
  87.8 0.0 copy-start.3
  87.8 0.0 copy-start.4
  87.8 5.1 %all-to-all-start.2 = ((bf16[16,32,512]{2,1,0:T(8,128)(2,1)}), bf16[16,32,512]{2,1,0:T(8,128)(2,1)S(1)}, u32[]{:S(2)}, u32[]{:S(2)}) async-start(bf16[16,32,512]{2,1,0:T(8,128)(2,1)} %bitcast.1), calls=%async_computation.2 | async-start | bytes 1048576 | tf_op jit(solution)/shard_map/all_to_all | solution.py:9
  92.9 0.0 copy-done.1
  93.0 10.6 %all-to-all-done.2 = bf16[16,32,512]{2,1,0:T(8,128)(2,1)S(1)} async-done(((bf16[16,32,512]{2,1,0:T(8,128)(2,1)}), bf16[16,32,512]{2,1,0:T(8,128)(2,1)S(1)}, u32[]{:S(2)}, u32[]{:S(2)}) %all-to-all-start.2) | async-done | bytes 524320 | tf_op jit(solution)/shard_map/all_to_all | solution.py:9
  103.6 0.1 reduce_sum.43
  103.6 0.8 broadcast_in_dim.49
  104.5 3.6 %all-to-all-start.3 = ((bf16[16,32,512]{2,1,0:T(8,128)(2,1)}), bf16[16,32,512]{2,1,0:T(8,128)(2,1)S(1)}, u32[]{:S(2)}, u32[]{:S(2)}) async-start(bf16[16,32,512]{2,1,0:T(8,128)(2,1)} %broadcast_in_dim.49), calls=%async_computation.3 | async-start | bytes 1048576 | tf_op jit(solution)/shard_map/all_to_all | solution.py:15
  108.1 0.1 broadcast_in_dim.46
  108.2 0.0 copy-done.2
  108.2 0.0 copy-done.3
  108.2 0.2 select_reduce_fusion
  108.4 0.0 copy-done.4
  108.5 10.2 %all-to-all-done.3 = bf16[16,32,512]{2,1,0:T(8,128)(2,1)S(1)} async-done(((bf16[16,32,512]{2,1,0:T(8,128)(2,1)}), bf16[16,32,512]{2,1,0:T(8,128)(2,1)S(1)}, u32[]{:S(2)}, u32[]{:S(2)}) %all-to-all-start.3) | async-done | bytes 524320 | tf_op jit(solution)/shard_map/all_to_all | solution.py:15
  118.7 1.4 %fusion = f32[512,64]{1,0:T(8,128)S(1)} fusion(bf16[512,512]{1,0:T(8,128)(2,1)S(1)} %bitcast.10, f32[512]{0:T(512)S(1)} %select_multiply_fusion, bf16[512,1024]{1,0:T(8,128)(2,1)} %param.9, s32[]{:T(128)S(6)} %select_n.24), kind=kOutput, calls=%fused_computation.6 | convolution fusion | flops 33652736 | bytes 788484 | tf_op jit(solution)/shard_map/dot_general | solution.py:47
  120.0 1.0 gather_fusion
  121.1 0.1 broadcast_select_fusion
  121.2 0.2 reshape.42
  121.4 10.9 %all_to_all.27 = f32[8,1,4096]{2,1,0:T(1,128)S(1)} all-to-all(f32[8,1,4096]{2,1,0:T(1,128)S(1)} %reshape.42), channel_id=1, replica_groups=mesh['dp'=8,'row'=4,'col'=4] {'dp'}, dimensions={0} | all-to-all | bytes 262144 | tf_op jit(solution)/shard_map/all_to_all | solution.py:9
  132.3 0.5 broadcast.15
  132.8 1.0 reduce.2
  133.8 0.1 reshape.43
  133.9 0.6 reduce_sum.45
  (4 shorter events, 0.0 us)
Async XLA Ops:
  0.0 84.2 %copy-start = (bf16[512,1848]{0,1:T(8,128)(2,1)S(1)}, bf16[512,1848]{0,1:T(8,128)(2,1)}, u32[]{:S(2)}) copy-start(bf16[512,1848]{0,1:T(8,128)(2,1)} %param.8) | copy-start | bytes 5677060
  84.2 8.8 %copy-start.1 = (s32[512]{0:T(512)S(1)}, s32[512]{0:T(512)}, u32[]{:S(2)}) copy-start(s32[512]{0:T(512)} %param.15) | copy-start | bytes 6148
  87.8 20.4 %copy-start.2 = (f32[512]{0:T(512)S(1)}, f32[512]{0:T(512)}, u32[]{:S(2)}) copy-start(f32[512]{0:T(512)} %param.12) | copy-start | bytes 6148
  87.8 20.4 %copy-start.3 = (s32[512]{0:T(512)S(1)}, s32[512]{0:T(512)}, u32[]{:S(2)}) copy-start(s32[512]{0:T(512)} %param.11) | copy-start | bytes 6148
  87.8 20.7 %copy-start.4 = (s32[512]{0:T(512)S(1)}, s32[512]{0:T(512)}, u32[]{:S(2)}) copy-start(s32[512]{0:T(512)} %param.10) | copy-start | bytes 6148
  87.8 15.8 %all-to-all-start.2 = ((bf16[16,32,512]{2,1,0:T(8,128)(2,1)}), bf16[16,32,512]{2,1,0:T(8,128)(2,1)S(1)}, u32[]{:S(2)}, u32[]{:S(2)}) async-start(bf16[16,32,512]{2,1,0:T(8,128)(2,1)} %bitcast.1), calls=%async_computation.2 | async-start | bytes 1048576 | tf_op jit(solution)/shard_map/all_to_all | solution.py:9
  104.5 14.2 %all-to-all-start.3 = ((bf16[16,32,512]{2,1,0:T(8,128)(2,1)}), bf16[16,32,512]{2,1,0:T(8,128)(2,1)S(1)}, u32[]{:S(2)}, u32[]{:S(2)}) async-start(bf16[16,32,512]{2,1,0:T(8,128)(2,1)} %broadcast_in_dim.49), calls=%async_computation.3 | async-start | bytes 1048576 | tf_op jit(solution)/shard_map/all_to_all | solution.py:15

commit v3 on v2

--- a/solution.py
+++ b/solution.py
@@ -39,15 +39,15 @@
     gram_keys = reduce_scatter(gram_keys.astype(jnp.bfloat16), "dp", n_dp)
     gram_keys = all_gather(gram_keys.astype(jnp.bfloat16), "dp", n_dp)
     acts_keys = jnp.dot(hidden_acts, gram_keys, preferred_element_type=jnp.float32)
-    acts_keys = reduce_scatter(acts_keys.astype(jnp.bfloat16), ("row", "col"), n_rc)
-    acts_keys = all_gather(acts_keys.astype(jnp.bfloat16), ("row", "col"), n_rc)
-    rows = out_cotangent.shape[1] // n_rc
-    block = lax.axis_index("row") * lax.axis_size("col") + lax.axis_index("col")
-    scaled_rows = lax.dynamic_slice_in_dim(scaled, block * rows, rows, axis=1)
     partial = lax.dot_general(
-        acts_keys, scaled_rows, (((0,), (0,)), ((), ())), preferred_element_type=jnp.float32
+        scaled,
+        acts_keys,
+        (((0,), (0,)), ((), ())),
+        precision=lax.Precision.HIGH,
+        preferred_element_type=jnp.float32,
     )
-    partial = jnp.take(partial, edit_slots, axis=0)
+    partial = reduce_scatter(partial.astype(jnp.bfloat16), ("row", "col"), n_rc)
+    partial = jnp.take(partial.T, edit_slots, axis=0)
     return reduce_scatter(partial, "dp", n_dp)
 
 

time: 135 us -> 129 us (0.956)
  blocking collectives: 73.6 us -> 47.7 us
  waiting for transfers between devices: 20.8 us -> 38.8 us
    all_to_all x1 -> x0, blocking collectives: 28.3 us -> none  [all_gather(): got = lax.all_to_all(pieces, axis, 0, 0)]
    all_to_all x1, waiting for transfers between devices: 10.2 us -> 22.6 us  [all_gather(): got = lax.all_to_all(pieces, axis, 0, 0)]
    all_to_all x1, waiting for transfers between devices: 10.6 us -> 16.1 us  [reduce_scatter(): got = lax.all_to_all(pieces, axis, 0, 0)]
    all_to_all x2, blocking collectives: 45.4 us -> 47.7 us  [reduce_scatter(): got = lax.all_to_all(pieces, axis, 0, 0)]
    dot_general x1, matrix products: 1.36 us -> 2.72 us  [body(): lax.dot_general(scaled, acts_keys, (((0,), (0,)), ((), ())), precision=la...]
where the time goes in v3:
time: 129 us; the launch traced here: 128 us
  blocking collectives  47.7 us (37%)
  waiting for transfers between devices  38.8 us (30%)
  matrix products  18.4 us (14%)
  local copies, waits for them, and re-layouts  10.1 us (8%)
  starting transfers between devices  9.29 us (7%)
  other arithmetic  4 us (3%)
    all_to_all x2, blocking collectives, reduce_scatter(): got = lax.all_to_all(pieces, axis, 0, 0)  47.7 us
    all_to_all x1, waiting for transfers between devices, all_gather(): got = lax.all_to_all(pieces, axis, 0, 0)  22.6 us
    all_to_all x1, waiting for transfers between devices, reduce_scatter(): got = lax.all_to_all(pieces, axis, 0, 0)  16.1 us
    dot_general x1, matrix products, body(): jnp.dot(inverse_gram, edit_keys, preferred_element_type=jnp.float32)  12.8 us
    all_to_all x1, starting transfers between devices, reduce_scatter(): got = lax.all_to_all(pieces, axis, 0, 0)  4.84 us
    all_to_all x1, starting transfers between devices, all_gather(): got = lax.all_to_all(pieces, axis, 0, 0)  4.45 us
    reshape x1, local copies, waits for them, and re-layouts, reduce_scatter(): pieces = x.reshape((parts, x.shape[0] // parts) + x.shape[1:])  3.36 us
    reshape x1, local copies, waits for them, and re-layouts, all_gather(): return got.reshape((parts * x.shape[0],) + x.shape[1:])  3.33 us
  transfers between devices with their start and end apart: 2, of which 2 were waited for; matrix products, arithmetic and copies ran while one was open for 0% of the time, Pallas kernels for 0%

profile of v3, /device:TPU:0, one launch (start us, length us, event | category | flops | bytes accessed | tf_op | source)
XLA Modules:
  0.0 128.4 jit_solution(9549349988721896461)
XLA Ops:
  0.0 0.0 copy-start
  0.0 12.8 %convolution_convert_fusion = bf16[1848,512]{1,0:T(8,128)(2,1)} fusion(bf16[1848,3696]{1,0:T(8,128)(2,1)} %param.13, bf16[3696,512]{1,0:T(8,128)(2,1)} %param.14), kind=kOutput, calls=%fused_computation.1 | convolution fusion | flops 6995079168 | bytes 19337472 | tf_op jit(solution)/shard_map/dot_general | solution.py:38
  12.8 3.4 %reshape.25 = bf16[8,231,512]{2,1,0:T(8,128)(2,1)} reshape(bf16[1848,512]{1,0:T(8,128)(2,1)} %convolution_convert_fusion) | data formatting | bytes 3784704 | tf_op jit(solution)/shard_map/reshape | solution.py:8
  16.1 34.4 %all_to_all.20 = bf16[8,231,512]{2,1,0:T(8,128)(2,1)} all-to-all(bf16[8,231,512]{2,1,0:T(8,128)(2,1)} %reshape.25), channel_id=1, replica_groups=mesh['dp'=8,'row'=4,'col'=4] {'dp'}, dimensions={0} | all-to-all | bytes 3784704 | tf_op jit(solution)/shard_map/all_to_all | solution.py:9
  50.6 1.8 %reduce_sum.40 = bf16[231,512]{1,0:T(8,128)(2,1)S(1)} reduce(bf16[8,231,512]{2,1,0:T(8,128)(2,1)} %all_to_all.20, bf16[]{:T(256)} %constant.25.clone.1), dimensions={0}, to_apply=%region_1.2 | reduce | flops 827904 | bytes 2128898 | tf_op jit(solution)/shard_map/reduce_sum | solution.py:10
  52.4 1.4 %broadcast_in_dim.45 = bf16[8,231,512]{2,1,0:T(8,128)(2,1)} broadcast(bf16[231,512]{1,0:T(8,128)(2,1)S(1)} %reduce_sum.40), dimensions={1,2} | broadcast | bytes 2128896 | tf_op jit(solution)/shard_map/broadcast_in_dim | solution.py:14
  53.8 0.0 copy-start.3
  53.8 0.0 copy-start.4
  53.8 0.0 copy-start.5
  53.8 4.4 %all-to-all-start.1 = ((bf16[8,231,512]{2,1,0:T(8,128)(2,1)}), bf16[8,231,512]{2,1,0:T(8,128)(2,1)}, u32[]{:S(2)}, u32[]{:S(2)}) async-start(bf16[8,231,512]{2,1,0:T(8,128)(2,1)} %broadcast_in_dim.45), calls=%async_computation.1 | async-start | bytes 3801088 | tf_op jit(solution)/shard_map/all_to_all | solution.py:15
  58.3 0.0 copy-done.3
  58.3 0.0 copy-done.4
  58.3 0.2 select_reduce_fusion
  58.5 0.0 copy-done.5
  58.6 22.6 %all-to-all-done.1 = bf16[8,231,512]{2,1,0:T(8,128)(2,1)} async-done(((bf16[8,231,512]{2,1,0:T(8,128)(2,1)}), bf16[8,231,512]{2,1,0:T(8,128)(2,1)}, u32[]{:S(2)}, u32[]{:S(2)}) %all-to-all-start.1) | async-done | bytes 1892384 | tf_op jit(solution)/shard_map/all_to_all | solution.py:15
  81.2 3.3 %reshape.26 = bf16[1848,512]{1,0:T(8,128)(2,1)} reshape(bf16[8,231,512]{2,1,0:T(8,128)(2,1)} %all-to-all-done.1) | data formatting | bytes 3784704 | tf_op jit(solution)/shard_map/reshape | solution.py:16
  84.5 0.0 copy-done
  84.5 0.0 copy-start.1
  84.5 2.9 %fusion.1 = f32[512,512]{1,0:T(8,128)S(1)} fusion(bf16[1848,512]{1,0:T(8,128)(2,1)} %reshape.26, bf16[512,1848]{0,1:T(8,128)(2,1)S(1)} %copy-done), kind=kOutput, calls=%fused_computation.13 | convolution fusion | flops 968884224 | bytes 4833280 | tf_op jit(solution)/shard_map/dot_general | solution.py:41
  87.4 0.0 copy-done.1
  87.4 0.0 copy-start.2
  87.4 2.7 %convolution_convert_fusion.1 = bf16[1024,512]{1,0:T(8,128)(2,1)} fusion(f32[512,512]{1,0:T(8,128)S(1)} %fusion.1, bf16[512,1024]{1,0:T(8,128)(2,1)S(1)} %copy-done.1, f32[512]{0:T(512)S(1)} %select_multiply_fusion), kind=kOutput, calls=%fused_computation.4 | convolution fusion | flops 1612709888 | bytes 3147776 | tf_op jit(solution)/shard_map/dot_general | solution.py:42
  90.2 4.8 %all-to-all-start.2 = ((bf16[16,64,512]{2,1,0:T(8,128)(2,1)}), bf16[16,64,512]{2,1,0:T(8,128)(2,1)S(1)}, u32[]{:S(2)}, u32[]{:S(2)}) async-start(bf16[16,64,512]{2,1,0:T(8,128)(2,1)} %bitcast.9), calls=%async_computation.2 | async-start | bytes 2097152 | tf_op jit(solution)/shard_map/all_to_all | solution.py:9
  95.0 0.0 copy-done.2
  95.0 0.1 broadcast_in_dim.40
  95.1 16.1 %all-to-all-done.2 = bf16[16,64,512]{2,1,0:T(8,128)(2,1)S(1)} async-done(((bf16[16,64,512]{2,1,0:T(8,128)(2,1)}), bf16[16,64,512]{2,1,0:T(8,128)(2,1)S(1)}, u32[]{:S(2)}, u32[]{:S(2)}) %all-to-all-start.2) | async-done | bytes 1048608 | tf_op jit(solution)/shard_map/all_to_all | solution.py:9
  111.3 0.1 convert_reduce_fusion
  111.4 0.1 copy.10
  111.5 1.0 gather_fusion
  112.6 0.1 broadcast_select_fusion
  112.7 0.2 reshape.37
  112.9 13.3 %all_to_all.21 = f32[8,1,4096]{2,1,0:T(1,128)S(1)} all-to-all(f32[8,1,4096]{2,1,0:T(1,128)S(1)} %reshape.37), channel_id=1, replica_groups=mesh['dp'=8,'row'=4,'col'=4] {'dp'}, dimensions={0} | all-to-all | bytes 262144 | tf_op jit(solution)/shard_map/all_to_all | solution.py:9
  126.2 0.5 broadcast.14
  126.7 1.0 reduce.1
  127.7 0.1 reshape.38
  127.8 0.6 reduce_sum.42
  (4 shorter events, 0.0 us)
Async XLA Ops:
  0.0 84.5 %copy-start = (bf16[512,1848]{0,1:T(8,128)(2,1)S(1)}, bf16[512,1848]{0,1:T(8,128)(2,1)}, u32[]{:S(2)}) copy-start(bf16[512,1848]{0,1:T(8,128)(2,1)} %param.8) | copy-start | bytes 5677060
  53.8 4.5 %copy-start.3 = (f32[512]{0:T(512)S(1)}, f32[512]{0:T(512)}, u32[]{:S(2)}) copy-start(f32[512]{0:T(512)} %param.12) | copy-start | bytes 6148
  53.8 4.5 %copy-start.4 = (s32[512]{0:T(512)S(1)}, s32[512]{0:T(512)}, u32[]{:S(2)}) copy-start(s32[512]{0:T(512)} %param.11) | copy-start | bytes 6148
  53.8 4.7 %copy-start.5 = (s32[512]{0:T(512)S(1)}, s32[512]{0:T(512)}, u32[]{:S(2)}) copy-start(s32[512]{0:T(512)} %param.10) | copy-start | bytes 6148
  53.8 27.4 %all-to-all-start.1 = ((bf16[8,231,512]{2,1,0:T(8,128)(2,1)}), bf16[8,231,512]{2,1,0:T(8,128)(2,1)}, u32[]{:S(2)}, u32[]{:S(2)}) async-start(bf16[8,231,512]{2,1,0:T(8,128)(2,1)} %broadcast_in_dim.45), calls=%async_computation.1 | async-start | bytes 3801088 | tf_op jit(solution)/shard_map/all_to_all | solution.py:15
  84.5 2.9 %copy-start.1 = (bf16[512,1024]{1,0:T(8,128)(2,1)S(1)}, bf16[512,1024]{1,0:T(8,128)(2,1)}, u32[]{:S(2)}) copy-start(bf16[512,1024]{1,0:T(8,128)(2,1)} %param.9) | copy-start | bytes 3145732
  87.4 7.6 %copy-start.2 = (s32[512]{0:T(512)S(1)}, s32[512]{0:T(512)}, u32[]{:S(2)}) copy-start(s32[512]{0:T(512)} %param.15) | copy-start | bytes 6148
  90.2 21.1 %all-to-all-start.2 = ((bf16[16,64,512]{2,1,0:T(8,128)(2,1)}), bf16[16,64,512]{2,1,0:T(8,128)(2,1)S(1)}, u32[]{:S(2)}, u32[]{:S(2)}) async-start(bf16[16,64,512]{2,1,0:T(8,128)(2,1)} %bitcast.9), calls=%async_computation.2 | async-start | bytes 2097152 | tf_op jit(solution)/shard_map/all_to_all | solution.py:9

commit v4 on v3

--- a/solution.py
+++ b/solution.py
@@ -35,18 +35,25 @@
     weight = jnp.where(is_paraphrase == 1, looked, jnp.float32(1.0)) / jnp.sqrt(jnp.float32(tokens))
     scaled = (out_cotangent.astype(jnp.float32) * weight[:, None]).astype(jnp.bfloat16)
 
-    gram_keys = jnp.dot(inverse_gram, edit_keys, preferred_element_type=jnp.float32)
-    gram_keys = reduce_scatter(gram_keys.astype(jnp.bfloat16), "dp", n_dp)
-    gram_keys = all_gather(gram_keys.astype(jnp.bfloat16), "dp", n_dp)
-    acts_keys = jnp.dot(hidden_acts, gram_keys, preferred_element_type=jnp.float32)
-    partial = lax.dot_general(
-        scaled,
-        acts_keys,
-        (((0,), (0,)), ((), ())),
-        precision=lax.Precision.HIGH,
-        preferred_element_type=jnp.float32,
-    )
-    partial = reduce_scatter(partial.astype(jnp.bfloat16), ("row", "col"), n_rc)
+    rows = out_cotangent.shape[1] // n_rc
+    halves = 2
+    width = edits // halves
+    pieces = []
+    for h in range(halves):
+        keys = edit_keys[:, h * width:(h + 1) * width]
+        gram_keys = jnp.dot(inverse_gram, keys, preferred_element_type=jnp.float32)
+        gram_keys = reduce_scatter(gram_keys.astype(jnp.bfloat16), "dp", n_dp)
+        gram_keys = all_gather(gram_keys.astype(jnp.bfloat16), "dp", n_dp)
+        acts_keys = jnp.dot(hidden_acts, gram_keys, preferred_element_type=jnp.float32)
+        partial = lax.dot_general(
+            scaled,
+            acts_keys,
+            (((0,), (0,)), ((), ())),
+            precision=lax.Precision.HIGH,
+            preferred_element_type=jnp.float32,
+        )
+        pieces.append(reduce_scatter(partial.astype(jnp.bfloat16), ("row", "col"), n_rc))
+    partial = jnp.concatenate(pieces, axis=1)
     partial = jnp.take(partial.T, edit_slots, axis=0)
     return reduce_scatter(partial, "dp", n_dp)
 

time: 129 us -> 139 us (1.078)
  blocking collectives: 47.7 us -> 12.4 us
  starting transfers between devices: 9.29 us -> 28.3 us
  waiting for transfers between devices: 38.8 us -> 55.4 us
  matrix products: 18.4 us -> 24.6 us
  local copies, waits for them, and re-layouts: 10.1 us -> 12.7 us
    all_to_all x2 -> x1, blocking collectives: 47.7 us -> 12.4 us  [reduce_scatter(): got = lax.all_to_all(pieces, axis, 0, 0)]
    all_to_all x1 -> x4, waiting for transfers between devices: 16.1 us -> 32.1 us  [reduce_scatter(): got = lax.all_to_all(pieces, axis, 0, 0)]
    all_to_all x1 -> x4, starting transfers between devices: 4.84 us -> 20 us  [reduce_scatter(): got = lax.all_to_all(pieces, axis, 0, 0)]
    dot_general x1 -> x2, matrix products: 12.8 us -> 17 us  [body(): gram_keys = jnp.dot(inverse_gram, keys, preferred_element_type=jnp.float32)]
    all_to_all x1 -> x2, starting transfers between devices: 4.45 us -> 8.23 us  [all_gather(): got = lax.all_to_all(pieces, axis, 0, 0)]
    dot_general x1 -> x2, matrix products: 2.88 us -> 3.9 us  [body(): jnp.dot(hidden_acts, gram_keys, preferred_element_type=jnp.float32)]
    dot_general x1 -> x2, matrix products: 2.72 us -> 3.69 us  [body(): lax.dot_general(scaled, acts_keys, (((0,), (0,)), ((), ())), precision=la...]
    reduce_sum x3 -> x5, other arithmetic: 2.63 us -> 3.46 us  [reduce_scatter(): return jnp.sum(got.astype(jnp.float32), axis=0)]
  transfers between devices with their start and end apart: 2 -> 6, of which waited for: 2 -> 6; matrix products, arithmetic and copies ran while one was open for 0% -> 19% of each run, Pallas kernels for 0% -> 0%
where the time goes in v4:
time: 139 us; the launch traced here: 138 us
  waiting for transfers between devices  55.4 us (40%)
  starting transfers between devices  28.3 us (20%)
  matrix products  24.6 us (18%)
  local copies, waits for them, and re-layouts  12.7 us (9%)
  blocking collectives  12.4 us (9%)
  other arithmetic  4.85 us (3%)
    all_to_all x4, waiting for transfers between devices, reduce_scatter(): got = lax.all_to_all(pieces, axis, 0, 0)  32.1 us
    all_to_all x2, waiting for transfers between devices, all_gather(): got = lax.all_to_all(pieces, axis, 0, 0)  23.3 us
    all_to_all x4, starting transfers between devices, reduce_scatter(): got = lax.all_to_all(pieces, axis, 0, 0)  20 us
    dot_general x2, matrix products, body(): gram_keys = jnp.dot(inverse_gram, keys, preferred_element_type=jnp.float32)  17 us
    all_to_all x1, blocking collectives, reduce_scatter(): got = lax.all_to_all(pieces, axis, 0, 0)  12.4 us
    all_to_all x2, starting transfers between devices, all_gather(): got = lax.all_to_all(pieces, axis, 0, 0)  8.23 us
    dot_general x2, matrix products, body(): jnp.dot(hidden_acts, gram_keys, preferred_element_type=jnp.float32)  3.9 us
    dot_general x2, matrix products, body(): lax.dot_general(scaled, acts_keys, (((0,), (0,)), ((), ())), precision=la...  3.69 us
  transfers between devices with their start and end apart: 6, of which 6 were waited for; matrix products, arithmetic and copies ran while one was open for 19% of the time, Pallas kernels for 0%

profile of v4, /device:TPU:0, one launch (start us, length us, event | category | flops | bytes accessed | tf_op | source)
XLA Modules:
  0.0 138.5 jit_solution(16248449647738270082)
XLA Ops:
  0.0 0.0 copy-start
  0.0 8.2 %convolution_convert_fusion.1 = bf16[1848,256]{1,0:T(8,128)(2,1)S(1)} fusion(bf16[1848,3696]{1,0:T(8,128)(2,1)} %param.13, bf16[3696,512]{1,0:T(8,128)(2,1)} %param.14), kind=kOutput, calls=%fused_computation.2 | convolution fusion | flops 3497539584 | bytes 16558080 | tf_op jit(solution)/shard_map/dot_general | solution.py:44
  8.2 1.2 reshape.35
  9.4 7.9 %all-to-all-start = ((bf16[8,231,256]{2,1,0:T(8,128)(2,1)}), bf16[8,231,256]{2,1,0:T(8,128)(2,1)S(1)}, u32[]{:S(2)}, u32[]{:S(2)}) async-start(bf16[8,231,256]{2,1,0:T(8,128)(2,1)} %reshape.35), calls=%async_computation | async-start | bytes 1900544 | tf_op jit(solution)/shard_map/all_to_all | solution.py:9
  17.3 8.9 %convolution_convert_fusion = bf16[1848,256]{1,0:T(8,128)(2,1)} fusion(bf16[1848,3696]{1,0:T(8,128)(2,1)} %param.13, bf16[3696,512]{1,0:T(8,128)(2,1)} %param.14), kind=kOutput, calls=%fused_computation.1 | convolution fusion | flops 3497539584 | bytes 16558080 | tf_op jit(solution)/shard_map/dot_general | solution.py:44
  26.2 2.4 %reshape.38 = bf16[8,231,256]{2,1,0:T(8,128)(2,1)} reshape(bf16[1848,256]{1,0:T(8,128)(2,1)} %convolution_convert_fusion) | data formatting | bytes 1892352 | tf_op jit(solution)/shard_map/reshape | solution.py:8
  28.6 3.7 %all-to-all-done = bf16[8,231,256]{2,1,0:T(8,128)(2,1)S(1)} async-done(((bf16[8,231,256]{2,1,0:T(8,128)(2,1)}), bf16[8,231,256]{2,1,0:T(8,128)(2,1)S(1)}, u32[]{:S(2)}, u32[]{:S(2)}) %all-to-all-start) | async-done | bytes 946208 | tf_op jit(solution)/shard_map/all_to_all | solution.py:9
  32.2 1.0 copy-done.3
  33.2 4.0 %all-to-all-start.3 = ((bf16[8,231,256]{2,1,0:T(8,128)(2,1)}), bf16[8,231,256]{2,1,0:T(8,128)(2,1)S(1)}, u32[]{:S(2)}, u32[]{:S(2)}) async-start(bf16[8,231,256]{2,1,0:T(8,128)(2,1)} %reshape.38), calls=%async_computation.3 | async-start | bytes 1900544 | tf_op jit(solution)/shard_map/all_to_all | solution.py:9
  37.2 1.3 reduce_sum.61
  38.5 13.7 %all-to-all-done.3 = bf16[8,231,256]{2,1,0:T(8,128)(2,1)S(1)} async-done(((bf16[8,231,256]{2,1,0:T(8,128)(2,1)}), bf16[8,231,256]{2,1,0:T(8,128)(2,1)S(1)}, u32[]{:S(2)}, u32[]{:S(2)}) %all-to-all-start.3) | async-done | bytes 946208 | tf_op jit(solution)/shard_map/all_to_all | solution.py:9
  52.2 1.1 broadcast_in_dim.51
  53.3 0.2 copy-done.2
  53.5 4.0 %all-to-all-start.1 = ((bf16[8,231,256]{2,1,0:T(8,128)(2,1)}), bf16[8,231,256]{2,1,0:T(8,128)(2,1)S(1)}, u32[]{:S(2)}, u32[]{:S(2)}) async-start(bf16[8,231,256]{2,1,0:T(8,128)(2,1)} %broadcast_in_dim.51), calls=%async_computation.1 | async-start | bytes 1900544 | tf_op jit(solution)/shard_map/all_to_all | solution.py:15
  57.5 0.0 copy-start.6
  57.5 0.0 copy-start.7
  57.5 1.3 reduce_sum.63
  58.9 13.7 %all-to-all-done.1 = bf16[8,231,256]{2,1,0:T(8,128)(2,1)S(1)} async-done(((bf16[8,231,256]{2,1,0:T(8,128)(2,1)}), bf16[8,231,256]{2,1,0:T(8,128)(2,1)S(1)}, u32[]{:S(2)}, u32[]{:S(2)}) %all-to-all-start.1) | async-done | bytes 946208 | tf_op jit(solution)/shard_map/all_to_all | solution.py:15
  72.6 1.0 broadcast_in_dim.52
  73.6 4.2 %all-to-all-start.4 = ((bf16[8,231,256]{2,1,0:T(8,128)(2,1)}), bf16[8,231,256]{2,1,0:T(8,128)(2,1)}, u32[]{:S(2)}, u32[]{:S(2)}) async-start(bf16[8,231,256]{2,1,0:T(8,128)(2,1)} %broadcast_in_dim.52), calls=%async_computation.4 | async-start | bytes 1900544 | tf_op jit(solution)/shard_map/all_to_all | solution.py:15
  77.8 0.0 copy-done.5
  77.8 0.0 copy-done.6
  77.8 0.2 select_reduce_fusion
  78.1 1.2 reshape.36
  79.4 2.0 %fusion.2 = f32[256,512]{1,0:T(8,128)S(1)} fusion(bf16[1848,256]{1,0:T(8,128)(2,1)} %reshape.36, bf16[512,1848]{0,1:T(8,128)(2,1)S(1)} %copy-done), kind=kOutput, calls=%fused_computation.18 | convolution fusion | flops 484442112 | bytes 3362816 | tf_op jit(solution)/shard_map/dot_general | solution.py:47
  81.4 1.9 %convolution_convert_fusion.3 = bf16[1024,256]{1,0:T(8,128)(2,1)} fusion(f32[256,512]{1,0:T(8,128)S(1)} %fusion.2, bf16[512,1024]{1,0:T(8,128)(2,1)S(1)} %copy-done.1, f32[512]{0:T(512)S(1)} %select_multiply_fusion), kind=kOutput, calls=%fused_computation.7 | convolution fusion | flops 807141376 | bytes 2099200 | tf_op jit(solution)/shard_map/dot_general | solution.py:48
  83.2 9.6 %all-to-all-done.4 = bf16[8,231,256]{2,1,0:T(8,128)(2,1)} async-done(((bf16[8,231,256]{2,1,0:T(8,128)(2,1)}), bf16[8,231,256]{2,1,0:T(8,128)(2,1)}, u32[]{:S(2)}, u32[]{:S(2)}) %all-to-all-start.4) | async-done | bytes 946208 | tf_op jit(solution)/shard_map/all_to_all | solution.py:15
  92.8 4.6 %all-to-all-start.2 = ((bf16[16,64,256]{2,1,0:T(8,128)(2,1)}), bf16[16,64,256]{2,1,0:T(8,128)(2,1)S(1)}, u32[]{:S(2)}, u32[]{:S(2)}) async-start(bf16[16,64,256]{2,1,0:T(8,128)(2,1)} %bitcast), calls=%async_computation.2 | async-start | bytes 1048576 | tf_op jit(solution)/shard_map/all_to_all | solution.py:9
  97.4 2.4 %reshape.39 = bf16[1848,256]{1,0:T(8,128)(2,1)} reshape(bf16[8,231,256]{2,1,0:T(8,128)(2,1)} %all-to-all-done.4) | data formatting | bytes 1892352 | tf_op jit(solution)/shard_map/reshape | solution.py:16
  99.9 1.9 %fusion.3 = f32[256,512]{1,0:T(8,128)S(1)} fusion(bf16[1848,256]{1,0:T(8,128)(2,1)} %reshape.39, bf16[512,1848]{0,1:T(8,128)(2,1)S(1)} %copy-done), kind=kOutput, calls=%fused_computation.19 | convolution fusion | flops 484442112 | bytes 3362816 | tf_op jit(solution)/shard_map/dot_general | solution.py:47
  101.8 0.0 copy-start.4
  101.8 1.8 %convolution_convert_fusion.2 = bf16[1024,256]{1,0:T(8,128)(2,1)} fusion(f32[256,512]{1,0:T(8,128)S(1)} %fusion.3, bf16[512,1024]{1,0:T(8,128)(2,1)S(1)} %copy-done.1, f32[512]{0:T(512)S(1)} %select_multiply_fusion), kind=kOutput, calls=%fused_computation.6 | convolution fusion | flops 807141376 | bytes 2099200 | tf_op jit(solution)/shard_map/dot_general | solution.py:48
  103.6 4.4 %all-to-all-done.2 = bf16[16,64,256]{2,1,0:T(8,128)(2,1)S(1)} async-done(((bf16[16,64,256]{2,1,0:T(8,128)(2,1)}), bf16[16,64,256]{2,1,0:T(8,128)(2,1)S(1)}, u32[]{:S(2)}, u32[]{:S(2)}) %all-to-all-start.2) | async-done | bytes 524320 | tf_op jit(solution)/shard_map/all_to_all | solution.py:9
  108.1 3.6 %all-to-all-start.5 = ((bf16[16,64,256]{2,1,0:T(8,128)(2,1)}), bf16[16,64,256]{2,1,0:T(8,128)(2,1)S(1)}, u32[]{:S(2)}, u32[]{:S(2)}) async-start(bf16[16,64,256]{2,1,0:T(8,128)(2,1)} %bitcast.1), calls=%async_computation.5 | async-start | bytes 1048576 | tf_op jit(solution)/shard_map/all_to_all | solution.py:9
  111.7 0.1 broadcast_in_dim.46
  111.8 0.1 convert_reduce_fusion.1
  111.8 0.1 copy.11
  111.9 10.3 %all-to-all-done.5 = bf16[16,64,256]{2,1,0:T(8,128)(2,1)S(1)} async-done(((bf16[16,64,256]{2,1,0:T(8,128)(2,1)}), bf16[16,64,256]{2,1,0:T(8,128)(2,1)S(1)}, u32[]{:S(2)}, u32[]{:S(2)}) %all-to-all-start.5) | async-done | bytes 524320 | tf_op jit(solution)/shard_map/all_to_all | solution.py:9
  122.2 0.1 convert_reduce_fusion
  122.3 0.1 copy.12
  122.4 1.0 gather_fusion
  123.5 0.1 broadcast_select_fusion
  123.6 0.2 reshape.50
  123.8 12.4 %all_to_all.35 = f32[8,1,4096]{2,1,0:T(1,128)S(1)} all-to-all(f32[8,1,4096]{2,1,0:T(1,128)S(1)} %reshape.50), channel_id=1, replica_groups=mesh['dp'=8,'row'=4,'col'=4] {'dp'}, dimensions={0} | all-to-all | bytes 262144 | tf_op jit(solution)/shard_map/all_to_all | solution.py:9
  136.2 0.5 broadcast.15
  136.8 1.0 reduce.2
  137.7 0.1 reshape.51
  137.8 0.6 reduce_sum.65
  (13 shorter events, 0.1 us)
Async XLA Ops:
  0.0 79.4 %copy-start = (bf16[512,1848]{0,1:T(8,128)(2,1)S(1)}, bf16[512,1848]{0,1:T(8,128)(2,1)}, u32[]{:S(2)}) copy-start(bf16[512,1848]{0,1:T(8,128)(2,1)} %param.8) | copy-start | bytes 5677060
  9.4 22.8 %all-to-all-start = ((bf16[8,231,256]{2,1,0:T(8,128)(2,1)}), bf16[8,231,256]{2,1,0:T(8,128)(2,1)S(1)}, u32[]{:S(2)}, u32[]{:S(2)}) async-start(bf16[8,231,256]{2,1,0:T(8,128)(2,1)} %reshape.35), calls=%async_computation | async-start | bytes 1900544 | tf_op jit(solution)/shard_map/all_to_all | solution.py:9
  32.2 1.0 copy-start.3
  33.2 19.0 %all-to-all-start.3 = ((bf16[8,231,256]{2,1,0:T(8,128)(2,1)}), bf16[8,231,256]{2,1,0:T(8,128)(2,1)S(1)}, u32[]{:S(2)}, u32[]{:S(2)}) async-start(bf16[8,231,256]{2,1,0:T(8,128)(2,1)} %reshape.38), calls=%async_computation.3 | async-start | bytes 1900544 | tf_op jit(solution)/shard_map/all_to_all | solution.py:9
  52.2 1.3 copy-start.2
  53.5 19.1 %all-to-all-start.1 = ((bf16[8,231,256]{2,1,0:T(8,128)(2,1)}), bf16[8,231,256]{2,1,0:T(8,128)(2,1)S(1)}, u32[]{:S(2)}, u32[]{:S(2)}) async-start(bf16[8,231,256]{2,1,0:T(8,128)(2,1)} %broadcast_in_dim.51), calls=%async_computation.1 | async-start | bytes 1900544 | tf_op jit(solution)/shard_map/all_to_all | solution.py:15
  57.5 20.3 %copy-start.5 = (f32[512]{0:T(512)S(1)}, f32[512]{0:T(512)}, u32[]{:S(2)}) copy-start(f32[512]{0:T(512)} %param.12) | copy-start | bytes 6148
  57.5 20.3 %copy-start.6 = (s32[512]{0:T(512)S(1)}, s32[512]{0:T(512)}, u32[]{:S(2)}) copy-start(s32[512]{0:T(512)} %param.11) | copy-start | bytes 6148
  57.5 20.6 %copy-start.7 = (s32[512]{0:T(512)S(1)}, s32[512]{0:T(512)}, u32[]{:S(2)}) copy-start(s32[512]{0:T(512)} %param.10) | copy-start | bytes 6148
  73.6 19.2 %all-to-all-start.4 = ((bf16[8,231,256]{2,1,0:T(8,128)(2,1)}), bf16[8,231,256]{2,1,0:T(8,128)(2,1)}, u32[]{:S(2)}, u32[]{:S(2)}) async-start(bf16[8,231,256]{2,1,0:T(8,128)(2,1)} %broadcast_in_dim.52), calls=%async_computation.4 | async-start | bytes 1900544 | tf_op jit(solution)/shard_map/all_to_all | solution.py:15
  79.4 2.0 %copy-start.1 = (bf16[512,1024]{1,0:T(8,128)(2,1)S(1)}, bf16[512,1024]{1,0:T(8,128)(2,1)}, u32[]{:S(2)}) copy-start(bf16[512,1024]{1,0:T(8,128)(2,1)} %param.9) | copy-start | bytes 3145732
  92.8 15.2 %all-to-all-start.2 = ((bf16[16,64,256]{2,1,0:T(8,128)(2,1)}), bf16[16,64,256]{2,1,0:T(8,128)(2,1)S(1)}, u32[]{:S(2)}, u32[]{:S(2)}) async-start(bf16[16,64,256]{2,1,0:T(8,128)(2,1)} %bitcast), calls=%async_computation.2 | async-start | bytes 1048576 | tf_op jit(solution)/shard_map/all_to_all | solution.py:9
  101.8 9.9 %copy-start.4 = (s32[512]{0:T(512)S(1)}, s32[512]{0:T(512)}, u32[]{:S(2)}) copy-start(s32[512]{0:T(512)} %param.15) | copy-start | bytes 6148
  108.1 14.2 %all-to-all-start.5 = ((bf16[16,64,256]{2,1,0:T(8,128)(2,1)}), bf16[16,64,256]{2,1,0:T(8,128)(2,1)S(1)}, u32[]{:S(2)}, u32[]{:S(2)}) async-start(bf16[16,64,256]{2,1,0:T(8,128)(2,1)} %bitcast.1), calls=%async_computation.5 | async-start | bytes 1048576 | tf_op jit(solution)/shard_map/all_to_all | solution.py:9

commit v5 on v3

--- a/solution.py
+++ b/solution.py
@@ -40,15 +40,17 @@
     gram_keys = all_gather(gram_keys.astype(jnp.bfloat16), "dp", n_dp)
     acts_keys = jnp.dot(hidden_acts, gram_keys, preferred_element_type=jnp.float32)
     partial = lax.dot_general(
+        acts_keys,
         scaled,
-        acts_keys,
         (((0,), (0,)), ((), ())),
         precision=lax.Precision.HIGH,
         preferred_element_type=jnp.float32,
     )
-    partial = reduce_scatter(partial.astype(jnp.bfloat16), ("row", "col"), n_rc)
-    partial = jnp.take(partial.T, edit_slots, axis=0)
-    return reduce_scatter(partial, "dp", n_dp)
+    partial = jnp.take(partial.astype(jnp.bfloat16), edit_slots, axis=0)
+    slots, cols = partial.shape
+    blocks = partial.reshape(n_dp, slots // n_dp, n_rc, cols // n_rc).transpose(0, 2, 1, 3)
+    blocks = blocks.reshape(n_dp * n_rc, slots // n_dp, cols // n_rc)
+    return reduce_scatter(blocks.reshape(n_dp * n_rc * (slots // n_dp), cols // n_rc), ("dp", "row", "col"), n_dp * n_rc)
 
 
 def solution(mesh):

time: 129 us -> 138 us (1.070)
  waiting for transfers between devices: 38.8 us -> 22.5 us
  blocking collectives: 47.7 us -> 61.4 us
  local copies, waits for them, and re-layouts: 10.1 us -> 23.7 us
  starting transfers between devices: 9.29 us -> 4.46 us
  other arithmetic: 4 us -> 8.19 us
  matrix products: 18.4 us -> 17 us
    all_to_all x1 -> x0, waiting for transfers between devices: 16.1 us -> none  [reduce_scatter(): got = lax.all_to_all(pieces, axis, 0, 0)]
    all_to_all x2, blocking collectives: 47.7 us -> 61.4 us  [reduce_scatter(): got = lax.all_to_all(pieces, axis, 0, 0)]
    unnamed x14, local copies, waits for them, and re-layouts: 0.31 us -> 8.76 us
    gather x1 -> x2, local copies, waits for them, and re-layouts: 1.04 us -> 6.85 us  [body(): partial = jnp.take(partial.astype(jnp.bfloat16), edit_slots, axis=0)]
    all_to_all x1 -> x0, starting transfers between devices: 4.84 us -> none  [reduce_scatter(): got = lax.all_to_all(pieces, axis, 0, 0)]
    select_n x2, other arithmetic: 0.14 us -> 3.4 us  [body(): partial = jnp.take(partial.astype(jnp.bfloat16), edit_slots, axis=0)]
    reduce_sum x3 -> x2, other arithmetic: 2.63 us -> 4.52 us  [reduce_scatter(): return jnp.sum(got.astype(jnp.float32), axis=0)]
  transfers between devices with their start and end apart: 2 -> 1, of which waited for: 2 -> 1; matrix products, arithmetic and copies ran while one was open for 0% -> 0% of each run, Pallas kernels for 0% -> 0%
where the time goes in v5:
time: 138 us; the launch traced here: 137 us
  blocking collectives  61.4 us (44%)
  local copies, waits for them, and re-layouts  23.7 us (17%)
  waiting for transfers between devices  22.5 us (16%)
  matrix products  17 us (12%)
  other arithmetic  8.19 us (6%)
  starting transfers between devices  4.46 us (3%)
    all_to_all x2, blocking collectives, reduce_scatter(): got = lax.all_to_all(pieces, axis, 0, 0)  61.4 us
    all_to_all x1, waiting for transfers between devices, all_gather(): got = lax.all_to_all(pieces, axis, 0, 0)  22.5 us
    dot_general x1, matrix products, body(): jnp.dot(inverse_gram, edit_keys, preferred_element_type=jnp.float32)  12.8 us
    unnamed x14, local copies, waits for them, and re-layouts  8.76 us
    gather x2, local copies, waits for them, and re-layouts, body(): partial = jnp.take(partial.astype(jnp.bfloat16), edit_slots, axis=0)  6.85 us
    reduce_sum x2, other arithmetic, reduce_scatter(): return jnp.sum(got.astype(jnp.float32), axis=0)  4.52 us
    all_to_all x1, starting transfers between devices, all_gather(): got = lax.all_to_all(pieces, axis, 0, 0)  4.46 us
    select_n x2, other arithmetic, body(): partial = jnp.take(partial.astype(jnp.bfloat16), edit_slots, axis=0)  3.4 us
  transfers between devices with their start and end apart: 1, of which 1 were waited for; matrix products, arithmetic and copies ran while one was open for 0% of the time, Pallas kernels for 0%

profile of v5, /device:TPU:0, one launch (start us, length us, event | category | flops | bytes accessed | tf_op | source)
XLA Modules:
  0.0 137.4 jit_solution(11767364592955275658)
XLA Ops:
  0.0 0.0 copy-start
  0.0 12.8 %convolution_convert_fusion = bf16[1848,512]{1,0:T(8,128)(2,1)} fusion(bf16[1848,3696]{1,0:T(8,128)(2,1)} %param.13, bf16[3696,512]{1,0:T(8,128)(2,1)} %param.14), kind=kOutput, calls=%fused_computation.2 | convolution fusion | flops 6995079168 | bytes 19337472 | tf_op jit(solution)/shard_map/dot_general | solution.py:38
  12.8 3.4 %reshape.22 = bf16[8,231,512]{2,1,0:T(8,128)(2,1)} reshape(bf16[1848,512]{1,0:T(8,128)(2,1)} %convolution_convert_fusion) | data formatting | bytes 3784704 | tf_op jit(solution)/shard_map/reshape | solution.py:8
  16.1 34.4 %all_to_all.15 = bf16[8,231,512]{2,1,0:T(8,128)(2,1)} all-to-all(bf16[8,231,512]{2,1,0:T(8,128)(2,1)} %reshape.22), channel_id=1, replica_groups=mesh['dp'=8,'row'=4,'col'=4] {'dp'}, dimensions={0} | all-to-all | bytes 3784704 | tf_op jit(solution)/shard_map/all_to_all | solution.py:9
  50.6 1.8 %reduce_sum.30 = bf16[231,512]{1,0:T(8,128)(2,1)S(1)} reduce(bf16[8,231,512]{2,1,0:T(8,128)(2,1)} %all_to_all.15, bf16[]{:T(256)} %constant.21.clone.1), dimensions={0}, to_apply=%region_0.1 | reduce | flops 827904 | bytes 2128898 | tf_op jit(solution)/shard_map/reduce_sum | solution.py:10
  52.4 1.4 broadcast_in_dim.42
  53.8 0.0 copy-start.2
  53.8 0.0 copy-start.3
  53.8 0.0 copy-start.4
  53.8 0.0 copy-start.5
  53.8 4.5 %all-to-all-start.1 = ((bf16[8,231,512]{2,1,0:T(8,128)(2,1)}), bf16[8,231,512]{2,1,0:T(8,128)(2,1)}, u32[]{:S(2)}, u32[]{:S(2)}) async-start(bf16[8,231,512]{2,1,0:T(8,128)(2,1)} %broadcast_in_dim.42), calls=%async_computation.1 | async-start | bytes 3801088 | tf_op jit(solution)/shard_map/all_to_all | solution.py:15
  58.3 0.0 copy-done.2
  58.3 0.1 broadcast_in_dim.40
  58.4 0.0 copy-done.3
  58.4 0.0 copy-done.4
  58.4 0.2 select_reduce_fusion
  58.7 0.0 copy-done.5
  58.7 22.5 %all-to-all-done.1 = bf16[8,231,512]{2,1,0:T(8,128)(2,1)} async-done(((bf16[8,231,512]{2,1,0:T(8,128)(2,1)}), bf16[8,231,512]{2,1,0:T(8,128)(2,1)}, u32[]{:S(2)}, u32[]{:S(2)}) %all-to-all-start.1) | async-done | bytes 1892384 | tf_op jit(solution)/shard_map/all_to_all | solution.py:15
  81.2 3.3 %reshape.23 = bf16[1848,512]{1,0:T(8,128)(2,1)} reshape(bf16[8,231,512]{2,1,0:T(8,128)(2,1)} %all-to-all-done.1) | data formatting | bytes 3784704 | tf_op jit(solution)/shard_map/reshape | solution.py:16
  84.5 0.0 copy-done
  84.5 0.0 copy-start.1
  84.5 2.9 %fusion.1 = f32[512,512]{1,0:T(8,128)S(1)} fusion(bf16[1848,512]{1,0:T(8,128)(2,1)} %reshape.23, bf16[512,1848]{0,1:T(8,128)(2,1)S(1)} %copy-done), kind=kOutput, calls=%fused_computation.13 | convolution fusion | flops 968884224 | bytes 4833280 | tf_op jit(solution)/shard_map/dot_general | solution.py:41
  87.4 0.0 copy-done.1
  87.4 1.3 convolution_convert_fusion.1
  88.8 2.8 %gather_fusion = bf16[512,1024]{1,0:T(8,128)(2,1)} fusion(bf16[512,1024]{1,0:T(8,128)(2,1)S(1)} %convolution_convert_fusion.1, s32[1024]{0:T(1024)S(1)} %pad_clamp_fusion), kind=kCustom, calls=%fused_computation | custom fusion | bytes 2099200 | tf_op jit(solution)/shard_map/jit(_take)/gather | solution.py:49
  91.6 4.1 %gather.7 = bf16[8,64,16,64]{3,2,1,0:T(8,128)(2,1)} reshape(bf16[512,1024]{1,0:T(8,128)(2,1)} %gather_fusion) | data formatting | bytes 2097152 | tf_op jit(solution)/shard_map/jit(_take)/gather | solution.py:49
  95.6 3.4 %copy_select_fusion = bf16[8,64,16,64]{3,1,2,0:T(8,128)(2,1)} fusion(bf16[8,64,16,64]{3,2,1,0:T(8,128)(2,1)} %gather.7, pred[8,64]{1,0:T(8,128)(4,1)S(1)} %broadcast_in_dim.40), kind=kLoop, calls=%fused_computation.3 | loop fusion | flops 524288 | bytes 2097664 | tf_op jit(solution)/shard_map/jit(_take)/select_n | solution.py:49
  99.0 3.9 %reshape.33 = bf16[128,2,2048]{2,1,0:T(2,128)(2,1)S(1)} reshape(bf16[128,64,64]{2,1,0:T(8,128)(2,1)} %bitcast.8) | data formatting | bytes 2097152
  103.0 27.0 %all_to_all.16 = bf16[128,2,2048]{2,1,0:T(2,128)(2,1)} all-to-all(bf16[128,2,2048]{2,1,0:T(2,128)(2,1)S(1)} %reshape.33), channel_id=1, replica_groups=mesh['dp'=8,'row'=4,'col'=4] {'dp','row','col'}, dimensions={0} | all-to-all | bytes 2097152 | tf_op jit(solution)/shard_map/all_to_all | solution.py:9
  129.9 4.8 %reshape.34 = bf16[128,64,64]{2,1,0:T(8,128)(2,1)} reshape(bf16[128,2,2048]{2,1,0:T(2,128)(2,1)} %all_to_all.16) | data formatting | bytes 2097152
  134.7 2.7 %convert_reduce_fusion = f32[64,64]{1,0:T(8,128)} fusion(bf16[128,64,64]{2,1,0:T(8,128)(2,1)} %reshape.34), kind=kLoop, calls=%fused_computation.1 | loop fusion | flops 1044480 | bytes 1064960 | tf_op jit(solution)/shard_map/reduce_sum | solution.py:10
  (4 shorter events, 0.0 us)
Async XLA Ops:
  0.0 84.5 %copy-start = (bf16[512,1848]{0,1:T(8,128)(2,1)S(1)}, bf16[512,1848]{0,1:T(8,128)(2,1)}, u32[]{:S(2)}) copy-start(bf16[512,1848]{0,1:T(8,128)(2,1)} %param.8) | copy-start | bytes 5677060
  53.8 4.5 %copy-start.2 = (s32[512]{0:T(512)S(1)}, s32[512]{0:T(512)}, u32[]{:S(2)}) copy-start(s32[512]{0:T(512)} %param.15) | copy-start | bytes 6148
  53.8 4.6 %copy-start.3 = (f32[512]{0:T(512)S(1)}, f32[512]{0:T(512)}, u32[]{:S(2)}) copy-start(f32[512]{0:T(512)} %param.12) | copy-start | bytes 6148
  53.8 4.6 %copy-start.4 = (s32[512]{0:T(512)S(1)}, s32[512]{0:T(512)}, u32[]{:S(2)}) copy-start(s32[512]{0:T(512)} %param.11) | copy-start | bytes 6148
  53.8 4.9 %copy-start.5 = (s32[512]{0:T(512)S(1)}, s32[512]{0:T(512)}, u32[]{:S(2)}) copy-start(s32[512]{0:T(512)} %param.10) | copy-start | bytes 6148
  53.8 27.4 %all-to-all-start.1 = ((bf16[8,231,512]{2,1,0:T(8,128)(2,1)}), bf16[8,231,512]{2,1,0:T(8,128)(2,1)}, u32[]{:S(2)}, u32[]{:S(2)}) async-start(bf16[8,231,512]{2,1,0:T(8,128)(2,1)} %broadcast_in_dim.42), calls=%async_computation.1 | async-start | bytes 3801088 | tf_op jit(solution)/shard_map/all_to_all | solution.py:15
  84.5 2.9 %copy-start.1 = (bf16[512,1024]{1,0:T(8,128)(2,1)S(1)}, bf16[512,1024]{1,0:T(8,128)(2,1)}, u32[]{:S(2)}) copy-start(bf16[512,1024]{1,0:T(8,128)(2,1)} %param.9) | copy-start | bytes 3145732

commit v6 on v5

--- a/solution.py
+++ b/solution.py
@@ -38,6 +38,8 @@
     gram_keys = jnp.dot(inverse_gram, edit_keys, preferred_element_type=jnp.float32)
     gram_keys = reduce_scatter(gram_keys.astype(jnp.bfloat16), "dp", n_dp)
     gram_keys = all_gather(gram_keys.astype(jnp.bfloat16), "dp", n_dp)
+    order = (jnp.arange(edits, dtype=jnp.int32)[:, None] == edit_slots[None, :]).astype(jnp.bfloat16)
+    gram_keys = jnp.dot(gram_keys, order, preferred_element_type=jnp.float32).astype(jnp.bfloat16)
     acts_keys = jnp.dot(hidden_acts, gram_keys, preferred_element_type=jnp.float32)
     partial = lax.dot_general(
         acts_keys,
@@ -46,11 +48,13 @@
         precision=lax.Precision.HIGH,
         preferred_element_type=jnp.float32,
     )
-    partial = jnp.take(partial.astype(jnp.bfloat16), edit_slots, axis=0)
+    partial = partial.astype(jnp.bfloat16)
     slots, cols = partial.shape
     blocks = partial.reshape(n_dp, slots // n_dp, n_rc, cols // n_rc).transpose(0, 2, 1, 3)
-    blocks = blocks.reshape(n_dp * n_rc, slots // n_dp, cols // n_rc)
-    return reduce_scatter(blocks.reshape(n_dp * n_rc * (slots // n_dp), cols // n_rc), ("dp", "row", "col"), n_dp * n_rc)
+    blocks = blocks.reshape(n_dp * n_rc, (slots // n_dp) * (cols // n_rc))
+    got = lax.all_to_all(blocks, ("dp", "row", "col"), 0, 0)
+    total = jnp.sum(got.astype(jnp.float32), axis=0)
+    return total.reshape(slots // n_dp, cols // n_rc)
 
 
 def solution(mesh):

time: 138 us -> 152 us (1.10)
  other arithmetic: 8.19 us -> 14.5 us
  local copies, waits for them, and re-layouts: 23.7 us -> 28.2 us
  matrix products: 17 us -> 20.5 us
    all_to_all x0 -> x1, blocking collectives: none -> 27.1 us  [body(): got = lax.all_to_all(blocks, ('dp', 'row', 'col'), 0, 0)]
    all_to_all x2 -> x1, blocking collectives: 61.4 us -> 34.4 us  [reduce_scatter(): got = lax.all_to_all(pieces, axis, 0, 0)]
    all_to_all x0 -> x2, local copies, waits for them, and re-layouts: none -> 8.55 us  [body(): got = lax.all_to_all(blocks, ('dp', 'row', 'col'), 0, 0)]
    all_to_all x0 -> x1, other arithmetic: none -> 8.38 us  [body(): got = lax.all_to_all(blocks, ('dp', 'row', 'col'), 0, 0)]
    gather x2 -> x0, local copies, waits for them, and re-layouts: 6.85 us -> none  [body(): partial = jnp.take(partial.astype(jnp.bfloat16), edit_slots, axis=0)]
    reshape x0 -> x3, local copies, waits for them, and re-layouts: none -> 6.49 us  [the longest x2 5.81 us: body(): partial.reshape(n_dp, slots // n_dp, n_rc, cols // n_rc)]
    reduce_sum x0 -> x1, other arithmetic: none -> 3.99 us  [body(): total = jnp.sum(got.astype(jnp.float32), axis=0)]
    unnamed x14 -> x12, local copies, waits for them, and re-layouts: 8.76 us -> 5.08 us
where the time goes in v6:
time: 152 us
  blocking collectives  61.5 us (40%)
  local copies, waits for them, and re-layouts  28.2 us (19%)
  waiting for transfers between devices  22.6 us (15%)
  matrix products  20.5 us (13%)
  other arithmetic  14.5 us (10%)
  starting transfers between devices  4.45 us (3%)
    all_to_all x1, blocking collectives, reduce_scatter(): got = lax.all_to_all(pieces, axis, 0, 0)  34.4 us
    all_to_all x1, blocking collectives, body(): got = lax.all_to_all(blocks, ('dp', 'row', 'col'), 0, 0)  27.1 us
    all_to_all x1, waiting for transfers between devices, all_gather(): got = lax.all_to_all(pieces, axis, 0, 0)  22.6 us
    dot_general x1, matrix products, body(): jnp.dot(inverse_gram, edit_keys, preferred_element_type=jnp.float32)  12.8 us
    all_to_all x2, local copies, waits for them, and re-layouts, body(): got = lax.all_to_all(blocks, ('dp', 'row', 'col'), 0, 0)  8.55 us
    all_to_all x1, other arithmetic, body(): got = lax.all_to_all(blocks, ('dp', 'row', 'col'), 0, 0)  8.38 us
    reshape x2, local copies, waits for them, and re-layouts, body(): partial.reshape(n_dp, slots // n_dp, n_rc, cols // n_rc)  5.81 us
    unnamed x12, local copies, waits for them, and re-layouts  5.08 us
  transfers between devices with their start and end apart: 1, of which 1 were waited for; matrix products, arithmetic and copies ran while one was open for 0% of the time, Pallas kernels for 0%

profile of v6, /device:TPU:0, one launch (start us, length us, event | category | flops | bytes accessed | tf_op | source)
XLA Modules:
  0.0 151.8 jit_solution(8618748710028822446)
XLA Ops:
  0.0 0.0 copy-start
  0.0 12.8 %convolution_convert_fusion.1 = bf16[1848,512]{1,0:T(8,128)(2,1)} fusion(bf16[1848,3696]{1,0:T(8,128)(2,1)} %param.13, bf16[3696,512]{1,0:T(8,128)(2,1)} %param.14), kind=kOutput, calls=%fused_computation.1 | convolution fusion | flops 6995079168 | bytes 19337472 | tf_op jit(solution)/shard_map/dot_general | solution.py:38
  12.8 3.4 %reshape.22 = bf16[8,231,512]{2,1,0:T(8,128)(2,1)} reshape(bf16[1848,512]{1,0:T(8,128)(2,1)} %convolution_convert_fusion.1) | data formatting | bytes 3784704 | tf_op jit(solution)/shard_map/reshape | solution.py:8
  16.1 34.4 %all_to_all.20 = bf16[8,231,512]{2,1,0:T(8,128)(2,1)} all-to-all(bf16[8,231,512]{2,1,0:T(8,128)(2,1)} %reshape.22), channel_id=1, replica_groups=mesh['dp'=8,'row'=4,'col'=4] {'dp'}, dimensions={0} | all-to-all | bytes 3784704 | tf_op jit(solution)/shard_map/all_to_all | solution.py:9
  50.6 1.8 %reduce_sum.30 = bf16[231,512]{1,0:T(8,128)(2,1)S(1)} reduce(bf16[8,231,512]{2,1,0:T(8,128)(2,1)} %all_to_all.20, bf16[]{:T(256)} %constant.2.clone.1), dimensions={0}, to_apply=%region_0.1 | reduce | flops 827904 | bytes 2128898 | tf_op jit(solution)/shard_map/reduce_sum | solution.py:10
  52.4 1.4 broadcast_in_dim.18
  53.8 0.0 copy-start.1
  53.8 0.0 copy-start.2
  53.8 0.0 copy-start.3
  53.8 4.4 %all-to-all-start.1 = ((bf16[8,231,512]{2,1,0:T(8,128)(2,1)}), bf16[8,231,512]{2,1,0:T(8,128)(2,1)}, u32[]{:S(2)}, u32[]{:S(2)}) async-start(bf16[8,231,512]{2,1,0:T(8,128)(2,1)} %broadcast_in_dim.18), calls=%async_computation.1 | async-start | bytes 3801088 | tf_op jit(solution)/shard_map/all_to_all | solution.py:15
  58.3 0.0 copy-done.1
  58.3 0.0 copy-done.2
  58.3 0.0 copy-start.4
  58.3 0.2 select_reduce_fusion
  58.5 0.0 copy-done.3
  58.6 22.6 %all-to-all-done.1 = bf16[8,231,512]{2,1,0:T(8,128)(2,1)} async-done(((bf16[8,231,512]{2,1,0:T(8,128)(2,1)}), bf16[8,231,512]{2,1,0:T(8,128)(2,1)}, u32[]{:S(2)}, u32[]{:S(2)}) %all-to-all-start.1) | async-done | bytes 1892384 | tf_op jit(solution)/shard_map/all_to_all | solution.py:15
  81.2 3.3 %reshape.23 = bf16[1848,512]{1,0:T(8,128)(2,1)} reshape(bf16[8,231,512]{2,1,0:T(8,128)(2,1)} %all-to-all-done.1) | data formatting | bytes 3784704 | tf_op jit(solution)/shard_map/reshape | solution.py:16
  84.5 0.0 copy-done
  84.5 0.0 copy-done.4
  84.5 4.8 %fusion.1 = f32[512,512]{1,0:T(8,128)} fusion(bf16[512,1848]{0,1:T(8,128)(2,1)S(1)} %copy-done, bf16[1848,512]{1,0:T(8,128)(2,1)} %reshape.23, s32[512]{0:T(512)S(1)} %copy-done.4), kind=kOutput, calls=%fused_computation.10 | convolution fusion | flops 1938976768 | bytes 4835328 | tf_op jit(solution)/shard_map/dot_general | solution.py:43
  89.3 2.9 %convolution_convert_fusion.2 = bf16[512,1024]{1,0:T(8,128)(2,1)S(1)} fusion(f32[512,512]{1,0:T(8,128)} %fusion.1, bf16[512,1024]{1,0:T(8,128)(2,1)} %param.9, f32[512]{0:T(512)S(1)} %select_multiply_fusion), kind=kOutput, calls=%fused_computation.5 | convolution fusion | flops 1612709888 | bytes 3147776 | tf_op jit(solution)/shard_map/dot_general | solution.py:44
  92.2 2.3 %reshape.24 = bf16[8,64,16,64]{3,2,1,0:T(8,128)(2,1)} reshape(bf16[512,1024]{1,0:T(8,128)(2,1)S(1)} %convolution_convert_fusion.2) | data formatting | bytes 2097152 | tf_op jit(solution)/shard_map/reshape | solution.py:53
  94.5 3.5 %copy.15 = bf16[8,64,16,64]{3,1,2,0:T(8,128)(2,1)} copy(bf16[8,64,16,64]{3,2,1,0:T(8,128)(2,1)} %reshape.24) | data formatting | bytes 2097152 | tf_op jit(solution)/shard_map/reshape | solution.py:53
  98.0 8.0 %all_to_all.16 = bf16[128,1,4096]{2,1,0:T(2,128)(2,1)} reshape(bf16[8,16,64,64]{3,2,1,0:T(8,128)(2,1)} %bitcast.10) | data formatting | bytes 2097152 | tf_op jit(solution)/shard_map/all_to_all | solution.py:55
  106.1 0.5 broadcast.6
  106.6 8.4 %reduce.2 = bf16[128,4096]{1,0:T(8,128)(2,1)S(1)} reduce(bf16[128,1,4096]{2,1,0:T(2,128)(2,1)} %all_to_all.16, bf16[]{:T(256)} %broadcast.6), dimensions={1}, to_apply=%all_to_all.16.reduce_sub_computation | reduce | bytes 2097154 | tf_op jit(solution)/shard_map/all_to_all | solution.py:55
  115.0 1.6 %reshape.26 = bf16[128,2,2048]{2,1,0:T(2,128)(2,1)} reshape(bf16[128,4096]{1,0:T(8,128)(2,1)S(1)} %reduce.2) | data formatting | bytes 2097152
  116.6 27.1 %all_to_all.21 = bf16[128,2,2048]{2,1,0:T(2,128)(2,1)S(1)} all-to-all(bf16[128,2,2048]{2,1,0:T(2,128)(2,1)} %reshape.26), channel_id=1, replica_groups=mesh['dp'=8,'row'=4,'col'=4] {'dp','row','col'}, dimensions={0} | all-to-all | bytes 2097152 | tf_op jit(solution)/shard_map/all_to_all | solution.py:55
  143.6 3.5 %reshape.27 = bf16[128,1,4096]{2,1,0:T(2,128)(2,1)} reshape(bf16[128,2,2048]{2,1,0:T(2,128)(2,1)S(1)} %all_to_all.21) | data formatting | bytes 2097152
  147.1 4.0 %convert_reduce_fusion = f32[4096]{0:T(1024)S(1)} fusion(bf16[128,1,4096]{2,1,0:T(2,128)(2,1)} %reshape.27), kind=kLoop, calls=%fused_computation.3 | loop fusion | flops 1044480 | bytes 1064960 | tf_op jit(solution)/shard_map/reduce_sum | solution.py:56
  151.1 0.7 reshape.25
  (1 shorter events, 0.0 us)
Async XLA Ops:
  0.0 84.5 %copy-start = (bf16[512,1848]{0,1:T(8,128)(2,1)S(1)}, bf16[512,1848]{0,1:T(8,128)(2,1)}, u32[]{:S(2)}) copy-start(bf16[512,1848]{0,1:T(8,128)(2,1)} %param.8) | copy-start | bytes 5677060
  53.8 4.5 %copy-start.1 = (f32[512]{0:T(512)S(1)}, f32[512]{0:T(512)}, u32[]{:S(2)}) copy-start(f32[512]{0:T(512)} %param.12) | copy-start | bytes 6148
  53.8 4.5 %copy-start.2 = (s32[512]{0:T(512)S(1)}, s32[512]{0:T(512)}, u32[]{:S(2)}) copy-start(s32[512]{0:T(512)} %param.11) | copy-start | bytes 6148
  53.8 4.7 %copy-start.3 = (s32[512]{0:T(512)S(1)}, s32[512]{0:T(512)}, u32[]{:S(2)}) copy-start(s32[512]{0:T(512)} %param.10) | copy-start | bytes 6148
  53.8 27.4 %all-to-all-start.1 = ((bf16[8,231,512]{2,1,0:T(8,128)(2,1)}), bf16[8,231,512]{2,1,0:T(8,128)(2,1)}, u32[]{:S(2)}, u32[]{:S(2)}) async-start(bf16[8,231,512]{2,1,0:T(8,128)(2,1)} %broadcast_in_dim.18), calls=%async_computation.1 | async-start | bytes 3801088 | tf_op jit(solution)/shard_map/all_to_all | solution.py:15
  58.3 26.2 %copy-start.4 = (s32[512]{0:T(512)S(1)}, s32[512]{0:T(512)}, u32[]{:S(2)}) copy-start(s32[512]{0:T(512)} %param.15) | copy-start | bytes 6148

commit v7 on v3

--- a/solution.py
+++ b/solution.py
@@ -2,6 +2,26 @@
 import jax.numpy as jnp
 from jax import lax
 from jax.sharding import PartitionSpec as P
+
+
+Z_GROUPS = [[0, 1, 2, 3], [4, 5, 6, 7]]
+X_GROUPS = [[0, 4], [1, 5], [2, 6], [3, 7]]
+
+
+def reduce_scatter_dp(x):
+    pieces = x.reshape((4, x.shape[0] // 4) + x.shape[1:])
+    got = lax.all_to_all(pieces, "dp", 0, 0, axis_index_groups=Z_GROUPS)
+    part = jnp.sum(got.astype(jnp.float32), axis=0).astype(jnp.bfloat16)
+    pieces = part.reshape((2, part.shape[0] // 2) + part.shape[1:])
+    got = lax.all_to_all(pieces, "dp", 0, 0, axis_index_groups=X_GROUPS)
+    return jnp.sum(got.astype(jnp.float32), axis=0)
+
+
+def all_gather_dp(x):
+    got = lax.all_to_all(jnp.broadcast_to(x[None], (2,) + x.shape), "dp", 0, 0, axis_index_groups=X_GROUPS)
+    part = got.reshape((2 * x.shape[0],) + x.shape[1:])
+    got = lax.all_to_all(jnp.broadcast_to(part[None], (4,) + part.shape), "dp", 0, 0, axis_index_groups=Z_GROUPS)
+    return got.reshape((4 * part.shape[0],) + part.shape[1:])
 
 
 def reduce_scatter(x, axis, parts):
@@ -36,8 +56,8 @@
     scaled = (out_cotangent.astype(jnp.float32) * weight[:, None]).astype(jnp.bfloat16)
 
     gram_keys = jnp.dot(inverse_gram, edit_keys, preferred_element_type=jnp.float32)
-    gram_keys = reduce_scatter(gram_keys.astype(jnp.bfloat16), "dp", n_dp)
-    gram_keys = all_gather(gram_keys.astype(jnp.bfloat16), "dp", n_dp)
+    gram_keys = reduce_scatter_dp(gram_keys.astype(jnp.bfloat16))
+    gram_keys = all_gather_dp(gram_keys.astype(jnp.bfloat16))
     acts_keys = jnp.dot(hidden_acts, gram_keys, preferred_element_type=jnp.float32)
     partial = lax.dot_general(
         scaled,

time: 129 us -> 142 us (1.10)
  blocking collectives: 47.7 us -> 62.8 us
  waiting for transfers between devices: 38.8 us -> 36.6 us
    all_to_all x0 -> x3, blocking collectives: none -> 52 us  [the longest x1 29.9 us: reduce_scatter_dp(): got = lax.all_to_all(pieces, 'dp', 0, 0, axis_index_groups=Z_GROUPS)]
    all_to_all x2 -> x1, blocking collectives: 47.7 us -> 10.8 us  [reduce_scatter(): got = lax.all_to_all(pieces, axis, 0, 0)]
    all_to_all x1, waiting for transfers between devices: 22.6 us -> 20.5 us  [all_gather_dp(): lax.all_to_all(jnp.broadcast_to(part[None], (4,) + part.shape), 'dp', 0,...]
    reduce_sum x0 -> x2, other arithmetic: none -> 2.13 us  [the longest x1 2.04 us: reduce_scatter_dp(): part = jnp.sum(got.astype(jnp.float32), axis=0).astype(jnp.bfloat16)]
    reduce_sum x3 -> x2, other arithmetic: 2.63 us -> 0.79 us  [reduce_scatter(): return jnp.sum(got.astype(jnp.float32), axis=0)]
    reshape x2 -> x3, local copies, waits for them, and re-layouts: 6.69 us -> 6.65 us  [the longest x1 3.29 us: reduce_scatter_dp(): pieces = x.reshape((4, x.shape[0] // 4) + x.shape[1:])]
where the time goes in v7:
time: 142 us
  blocking collectives  62.8 us (44%)
  waiting for transfers between devices  36.6 us (26%)
  matrix products  18.4 us (13%)
  local copies, waits for them, and re-layouts  10.2 us (7%)
  starting transfers between devices  9.14 us (6%)
  other arithmetic  4.28 us (3%)
    all_to_all x1, blocking collectives, reduce_scatter_dp(): got = lax.all_to_all(pieces, 'dp', 0, 0, axis_index_groups=Z_GROUPS)  29.9 us
    all_to_all x1, waiting for transfers between devices, all_gather_dp(): lax.all_to_all(jnp.broadcast_to(part[None], (4,) + part.shape), 'dp', 0,...  20.5 us
    all_to_all x1, waiting for transfers between devices, reduce_scatter(): got = lax.all_to_all(pieces, axis, 0, 0)  16.1 us
    dot_general x1, matrix products, body(): jnp.dot(inverse_gram, edit_keys, preferred_element_type=jnp.float32)  12.8 us
    all_to_all x1, blocking collectives, reduce_scatter_dp(): got = lax.all_to_all(pieces, 'dp', 0, 0, axis_index_groups=X_GROUPS)  11.9 us
    all_to_all x1, blocking collectives, reduce_scatter(): got = lax.all_to_all(pieces, axis, 0, 0)  10.8 us
    all_to_all x1, blocking collectives, all_gather_dp(): lax.all_to_all(jnp.broadcast_to(x[None], (2,) + x.shape), 'dp', 0, 0, axi...  10.2 us
    all_to_all x1, starting transfers between devices, reduce_scatter(): got = lax.all_to_all(pieces, axis, 0, 0)  4.6 us
  transfers between devices with their start and end apart: 2, of which 2 were waited for; matrix products, arithmetic and copies ran while one was open for 0% of the time, Pallas kernels for 0%

profile of v7, /device:TPU:0, one launch (start us, length us, event | category | flops | bytes accessed | tf_op | source)
XLA Modules:
  0.0 141.6 jit_solution(14258757905129256142)
XLA Ops:
  0.0 0.0 copy-start
  0.0 12.8 %convolution_convert_fusion = bf16[1848,512]{1,0:T(8,128)(2,1)} fusion(bf16[1848,3696]{1,0:T(8,128)(2,1)} %param.13, bf16[3696,512]{1,0:T(8,128)(2,1)} %param.14), kind=kOutput, calls=%fused_computation.1 | convolution fusion | flops 6995079168 | bytes 19337472 | tf_op jit(solution)/shard_map/dot_general | solution.py:58
  12.8 3.3 %reshape.29 = bf16[4,462,512]{2,1,0:T(8,128)(2,1)} reshape(bf16[1848,512]{1,0:T(8,128)(2,1)} %convolution_convert_fusion) | data formatting | bytes 3784704 | tf_op jit(solution)/shard_map/reshape | solution.py:12
  16.1 29.9 %all_to_all.30 = bf16[4,462,512]{2,1,0:T(8,128)(2,1)} all-to-all(bf16[4,462,512]{2,1,0:T(8,128)(2,1)} %reshape.29), channel_id=1, replica_groups={{0,16,32,48},{64,80,96,112},{1,17,33,49},{65,81,97,113},{2,18,34,50},{6..., dimensions={0} | all-to-all | bytes 3784704 | tf_op jit(solution)/shard_map/all_to_all | solution.py:13
  45.9 2.0 %reduce_sum.52 = bf16[462,512]{1,0:T(8,128)(2,1)S(1)} reduce(bf16[4,462,512]{2,1,0:T(8,128)(2,1)} %all_to_all.30, bf16[]{:T(256)} %constant.26.clone.1), dimensions={0}, to_apply=%region_1.2 | reduce | flops 709632 | bytes 2365442 | tf_op jit(solution)/shard_map/reduce_sum | solution.py:14
  48.0 0.1 reshape.30
  48.1 11.9 %all_to_all.31 = bf16[2,231,512]{2,1,0:T(8,128)(2,1)S(1)} all-to-all(bf16[2,231,512]{2,1,0:T(8,128)(2,1)S(1)} %reshape.30), channel_id=1, replica_groups={{0,64},{16,80},{32,96},{48,112},{1,65},{17,81},{33,97},{49,113},{2,66},..., dimensions={0} | all-to-all | bytes 946176 | tf_op jit(solution)/shard_map/all_to_all | solution.py:16
  60.0 0.1 reduce_sum.53
  60.1 10.2 %all_to_all.32 = bf16[2,231,512]{2,1,0:T(8,128)(2,1)S(1)} all-to-all(bf16[2,231,512]{2,1,0:T(8,128)(2,1)S(1)} %broadcast_in_dim.52), channel_id=1, replica_groups={{0,64},{16,80},{32,96},{48,112},{1,65},{17,81},{33,97},{49,113},{2,66},..., dimensions={0} | all-to-all | bytes 946176 | tf_op jit(solution)/shard_map/all_to_all | solution.py:21
  70.3 0.1 broadcast_in_dim.53
  70.4 1.4 broadcast_in_dim.54
  71.8 0.0 copy-start.3
  71.8 0.0 copy-start.4
  71.8 0.0 copy-start.5
  71.8 4.5 %all-to-all-start.3 = ((bf16[4,462,512]{2,1,0:T(8,128)(2,1)}), bf16[4,462,512]{2,1,0:T(8,128)(2,1)}, u32[]{:S(2)}, u32[]{:S(2)}) async-start(bf16[4,462,512]{2,1,0:T(8,128)(2,1)} %broadcast_in_dim.54), calls=%async_computation.3 | async-start | bytes 3801088 | tf_op jit(solution)/shard_map/all_to_all | solution.py:23
  76.4 0.0 copy-done.3
  76.4 0.0 copy-done.4
  76.4 0.2 select_reduce_fusion
  76.6 0.0 copy-done.5
  76.6 20.5 %all-to-all-done.3 = bf16[4,462,512]{2,1,0:T(8,128)(2,1)} async-done(((bf16[4,462,512]{2,1,0:T(8,128)(2,1)}), bf16[4,462,512]{2,1,0:T(8,128)(2,1)}, u32[]{:S(2)}, u32[]{:S(2)}) %all-to-all-start.3) | async-done | bytes 1892384 | tf_op jit(solution)/shard_map/all_to_all | solution.py:23
  97.1 3.3 %reshape.31 = bf16[1848,512]{1,0:T(8,128)(2,1)} reshape(bf16[4,462,512]{2,1,0:T(8,128)(2,1)} %all-to-all-done.3) | data formatting | bytes 3784704 | tf_op jit(solution)/shard_map/reshape | solution.py:24
  100.4 0.0 copy-done
  100.4 0.0 copy-start.1
  100.4 2.9 %fusion.1 = f32[512,512]{1,0:T(8,128)S(1)} fusion(bf16[1848,512]{1,0:T(8,128)(2,1)} %reshape.31, bf16[512,1848]{0,1:T(8,128)(2,1)S(1)} %copy-done), kind=kOutput, calls=%fused_computation.13 | convolution fusion | flops 968884224 | bytes 4833280 | tf_op jit(solution)/shard_map/dot_general | solution.py:61
  103.3 0.0 copy-done.1
  103.3 0.0 copy-start.2
  103.3 2.7 %convolution_convert_fusion.1 = bf16[1024,512]{1,0:T(8,128)(2,1)} fusion(f32[512,512]{1,0:T(8,128)S(1)} %fusion.1, bf16[512,1024]{1,0:T(8,128)(2,1)S(1)} %copy-done.1, f32[512]{0:T(512)S(1)} %select_multiply_fusion), kind=kOutput, calls=%fused_computation.4 | convolution fusion | flops 1612709888 | bytes 3147776 | tf_op jit(solution)/shard_map/dot_general | solution.py:62
  106.0 4.6 %all-to-all-start.4 = ((bf16[16,64,512]{2,1,0:T(8,128)(2,1)}), bf16[16,64,512]{2,1,0:T(8,128)(2,1)S(1)}, u32[]{:S(2)}, u32[]{:S(2)}) async-start(bf16[16,64,512]{2,1,0:T(8,128)(2,1)} %bitcast.9), calls=%async_computation.4 | async-start | bytes 2097152 | tf_op jit(solution)/shard_map/all_to_all | solution.py:29
  110.6 0.0 copy-done.2
  110.7 0.1 broadcast_in_dim.47
  110.8 16.1 %all-to-all-done.4 = bf16[16,64,512]{2,1,0:T(8,128)(2,1)S(1)} async-done(((bf16[16,64,512]{2,1,0:T(8,128)(2,1)}), bf16[16,64,512]{2,1,0:T(8,128)(2,1)S(1)}, u32[]{:S(2)}, u32[]{:S(2)}) %all-to-all-start.4) | async-done | bytes 1048608 | tf_op jit(solution)/shard_map/all_to_all | solution.py:29
  126.9 0.1 convert_reduce_fusion
  127.0 0.1 copy.10
  127.2 1.0 gather_fusion
  128.2 0.1 broadcast_select_fusion
  128.4 0.2 reshape.42
  128.5 10.8 %all_to_all.33 = f32[8,1,4096]{2,1,0:T(1,128)S(1)} all-to-all(f32[8,1,4096]{2,1,0:T(1,128)S(1)} %reshape.42), channel_id=1, replica_groups=mesh['dp'=8,'row'=4,'col'=4] {'dp'}, dimensions={0} | all-to-all | bytes 262144 | tf_op jit(solution)/shard_map/all_to_all | solution.py:29
  139.4 0.5 broadcast.14
  139.9 1.0 reduce.2
  140.9 0.1 reshape.43
  141.0 0.6 reduce_sum.55
  (5 shorter events, 0.1 us)
Async XLA Ops:
  0.0 100.4 %copy-start = (bf16[512,1848]{0,1:T(8,128)(2,1)S(1)}, bf16[512,1848]{0,1:T(8,128)(2,1)}, u32[]{:S(2)}) copy-start(bf16[512,1848]{0,1:T(8,128)(2,1)} %param.8) | copy-start | bytes 5677060
  71.8 4.5 %copy-start.3 = (f32[512]{0:T(512)S(1)}, f32[512]{0:T(512)}, u32[]{:S(2)}) copy-start(f32[512]{0:T(512)} %param.12) | copy-start | bytes 6148
  71.8 4.6 %copy-start.4 = (s32[512]{0:T(512)S(1)}, s32[512]{0:T(512)}, u32[]{:S(2)}) copy-start(s32[512]{0:T(512)} %param.11) | copy-start | bytes 6148
  71.8 4.8 %copy-start.5 = (s32[512]{0:T(512)S(1)}, s32[512]{0:T(512)}, u32[]{:S(2)}) copy-start(s32[512]{0:T(512)} %param.10) | copy-start | bytes 6148
  71.8 25.3 %all-to-all-start.3 = ((bf16[4,462,512]{2,1,0:T(8,128)(2,1)}), bf16[4,462,512]{2,1,0:T(8,128)(2,1)}, u32[]{:S(2)}, u32[]{:S(2)}) async-start(bf16[4,462,512]{2,1,0:T(8,128)(2,1)} %broadcast_in_dim.54), calls=%async_computation.3 | async-start | bytes 3801088 | tf_op jit(solution)/shard_map/all_to_all | solution.py:23
  100.4 2.9 %copy-start.1 = (bf16[512,1024]{1,0:T(8,128)(2,1)S(1)}, bf16[512,1024]{1,0:T(8,128)(2,1)}, u32[]{:S(2)}) copy-start(bf16[512,1024]{1,0:T(8,128)(2,1)} %param.9) | copy-start | bytes 3145732
  103.3 7.4 %copy-start.2 = (s32[512]{0:T(512)S(1)}, s32[512]{0:T(512)}, u32[]{:S(2)}) copy-start(s32[512]{0:T(512)} %param.15) | copy-start | bytes 6148
  106.0 20.9 %all-to-all-start.4 = ((bf16[16,64,512]{2,1,0:T(8,128)(2,1)}), bf16[16,64,512]{2,1,0:T(8,128)(2,1)S(1)}, u32[]{:S(2)}, u32[]{:S(2)}) async-start(bf16[16,64,512]{2,1,0:T(8,128)(2,1)} %bitcast.9), calls=%async_computation.4 | async-start | bytes 2097152 | tf_op jit(solution)/shard_map/all_to_all | solution.py:29

commit v8 on v6

--- a/solution.py
+++ b/solution.py
@@ -41,20 +41,20 @@
     order = (jnp.arange(edits, dtype=jnp.int32)[:, None] == edit_slots[None, :]).astype(jnp.bfloat16)
     gram_keys = jnp.dot(gram_keys, order, preferred_element_type=jnp.float32).astype(jnp.bfloat16)
     acts_keys = jnp.dot(hidden_acts, gram_keys, preferred_element_type=jnp.float32)
+    slots = acts_keys.shape[1]
+    cols = scaled.shape[1]
     partial = lax.dot_general(
-        acts_keys,
         scaled,
+        acts_keys.reshape(acts_keys.shape[0], n_dp, slots // n_dp),
         (((0,), (0,)), ((), ())),
         precision=lax.Precision.HIGH,
         preferred_element_type=jnp.float32,
     )
-    partial = partial.astype(jnp.bfloat16)
-    slots, cols = partial.shape
-    blocks = partial.reshape(n_dp, slots // n_dp, n_rc, cols // n_rc).transpose(0, 2, 1, 3)
-    blocks = blocks.reshape(n_dp * n_rc, (slots // n_dp) * (cols // n_rc))
+    blocks = partial.astype(jnp.bfloat16).transpose(1, 0, 2)
+    blocks = blocks.reshape(n_dp * n_rc, 2, (cols // n_rc) * (slots // n_dp) // 2)
     got = lax.all_to_all(blocks, ("dp", "row", "col"), 0, 0)
     total = jnp.sum(got.astype(jnp.float32), axis=0)
-    return total.reshape(slots // n_dp, cols // n_rc)
+    return total.reshape(cols // n_rc, slots // n_dp).T
 
 
 def solution(mesh):

time: 152 us -> 127 us (0.84)
  local copies, waits for them, and re-layouts: 28.2 us -> 14.6 us
  other arithmetic: 14.5 us -> 3.13 us
    all_to_all x2 -> x0, local copies, waits for them, and re-layouts: 8.55 us -> none  [body(): got = lax.all_to_all(blocks, ('dp', 'row', 'col'), 0, 0)]
    all_to_all x1 -> x0, other arithmetic: 8.38 us -> none  [body(): got = lax.all_to_all(blocks, ('dp', 'row', 'col'), 0, 0)]
    unnamed x12, local copies, waits for them, and re-layouts: 5.08 us -> 0.03 us
    reduce_sum x1, other arithmetic: 3.99 us -> 0.88 us  [body(): total = jnp.sum(got.astype(jnp.float32), axis=0)]
    dot_general x1 -> x0, matrix products: 2.88 us -> none  [body(): lax.dot_general(acts_keys, scaled, (((0,), (0,)), ((), ())), precision=la...]
    unnamed x0 -> x1, matrix products: none -> 2.61 us
    reshape x3 -> x2, local copies, waits for them, and re-layouts: 6.49 us -> 4 us  [the longest x1 3.92 us: body(): blocks = blocks.reshape(n_dp * n_rc, 2, cols // n_rc * (slots // n_dp) // 2)]
    convert_element_type x0 -> x1, local copies, waits for them, and re-layouts: none -> 1.83 us  [body(): blocks = partial.astype(jnp.bfloat16).transpose(1, 0, 2)]
where the time goes in v8:
time: 127 us; the launch traced here: 126 us
  blocking collectives  61.3 us (48%)
  waiting for transfers between devices  22.6 us (18%)
  matrix products  20.3 us (16%)
  local copies, waits for them, and re-layouts  14.6 us (11%)
  starting transfers between devices  4.45 us (4%)
  other arithmetic  3.13 us (2%)
    all_to_all x1, blocking collectives, reduce_scatter(): got = lax.all_to_all(pieces, axis, 0, 0)  34.4 us
    all_to_all x1, blocking collectives, body(): got = lax.all_to_all(blocks, ('dp', 'row', 'col'), 0, 0)  26.9 us
    all_to_all x1, waiting for transfers between devices, all_gather(): got = lax.all_to_all(pieces, axis, 0, 0)  22.6 us
    dot_general x1, matrix products, body(): jnp.dot(inverse_gram, edit_keys, preferred_element_type=jnp.float32)  12.8 us
    dot_general x1, matrix products, body(): jnp.dot(hidden_acts, gram_keys, preferred_element_type=jnp.float32)  4.89 us
    all_to_all x1, starting transfers between devices, all_gather(): got = lax.all_to_all(pieces, axis, 0, 0)  4.45 us
    reshape x1, local copies, waits for them, and re-layouts, body(): blocks = blocks.reshape(n_dp * n_rc, 2, cols // n_rc * (slots // n_dp) // 2)  3.92 us
    reshape x1, local copies, waits for them, and re-layouts, reduce_scatter(): pieces = x.reshape((parts, x.shape[0] // parts) + x.shape[1:])  3.36 us
  transfers between devices with their start and end apart: 1, of which 1 were waited for; matrix products, arithmetic and copies ran while one was open for 0% of the time, Pallas kernels for 0%

profile of v8, /device:TPU:0, one launch (start us, length us, event | category | flops | bytes accessed | tf_op | source)
XLA Modules:
  0.0 126.5 jit_solution(16441555590273994041)
XLA Ops:
  0.0 0.0 copy-start
  0.0 12.8 %convolution_convert_fusion.1 = bf16[1848,512]{1,0:T(8,128)(2,1)} fusion(bf16[1848,3696]{1,0:T(8,128)(2,1)} %param.13, bf16[3696,512]{1,0:T(8,128)(2,1)} %param.14), kind=kOutput, calls=%fused_computation.1 | convolution fusion | flops 6995079168 | bytes 19337472 | tf_op jit(solution)/shard_map/dot_general | solution.py:38
  12.8 3.4 %reshape.20 = bf16[8,231,512]{2,1,0:T(8,128)(2,1)} reshape(bf16[1848,512]{1,0:T(8,128)(2,1)} %convolution_convert_fusion.1) | data formatting | bytes 3784704 | tf_op jit(solution)/shard_map/reshape | solution.py:8
  16.1 34.4 %all_to_all.15 = bf16[8,231,512]{2,1,0:T(8,128)(2,1)} all-to-all(bf16[8,231,512]{2,1,0:T(8,128)(2,1)} %reshape.20), channel_id=1, replica_groups=mesh['dp'=8,'row'=4,'col'=4] {'dp'}, dimensions={0} | all-to-all | bytes 3784704 | tf_op jit(solution)/shard_map/all_to_all | solution.py:9
  50.6 1.8 %reduce_sum.31 = bf16[231,512]{1,0:T(8,128)(2,1)S(1)} reduce(bf16[8,231,512]{2,1,0:T(8,128)(2,1)} %all_to_all.15, bf16[]{:T(256)} %constant.10.clone.1), dimensions={0}, to_apply=%region_1.2 | reduce | flops 827904 | bytes 2128898 | tf_op jit(solution)/shard_map/reduce_sum | solution.py:10
  52.4 1.4 %broadcast_in_dim.31 = bf16[8,231,512]{2,1,0:T(8,128)(2,1)} broadcast(bf16[231,512]{1,0:T(8,128)(2,1)S(1)} %reduce_sum.31), dimensions={1,2} | broadcast | bytes 2128896 | tf_op jit(solution)/shard_map/broadcast_in_dim | solution.py:14
  53.8 0.0 copy-start.2
  53.8 0.0 copy-start.3
  53.8 0.0 copy-start.4
  53.8 4.4 %all-to-all-start.1 = ((bf16[8,231,512]{2,1,0:T(8,128)(2,1)}), bf16[8,231,512]{2,1,0:T(8,128)(2,1)}, u32[]{:S(2)}, u32[]{:S(2)}) async-start(bf16[8,231,512]{2,1,0:T(8,128)(2,1)} %broadcast_in_dim.31), calls=%async_computation.1 | async-start | bytes 3801088 | tf_op jit(solution)/shard_map/all_to_all | solution.py:15
  58.3 0.0 copy-done.2
  58.3 0.0 copy-done.3
  58.3 0.0 copy-start.5
  58.3 0.2 select_reduce_fusion
  58.5 0.0 copy-done.4
  58.6 22.6 %all-to-all-done.1 = bf16[8,231,512]{2,1,0:T(8,128)(2,1)} async-done(((bf16[8,231,512]{2,1,0:T(8,128)(2,1)}), bf16[8,231,512]{2,1,0:T(8,128)(2,1)}, u32[]{:S(2)}, u32[]{:S(2)}) %all-to-all-start.1) | async-done | bytes 1892384 | tf_op jit(solution)/shard_map/all_to_all | solution.py:15
  81.2 3.3 %reshape.21 = bf16[1848,512]{1,0:T(8,128)(2,1)} reshape(bf16[8,231,512]{2,1,0:T(8,128)(2,1)} %all-to-all-done.1) | data formatting | bytes 3784704 | tf_op jit(solution)/shard_map/reshape | solution.py:16
  84.5 0.0 copy-done
  84.5 0.0 copy-done.5
  84.5 0.0 copy-start.1
  84.5 4.9 %convolution_bitcast_fusion = f32[512,512]{0,1:T(8,128)} fusion(bf16[512,1848]{0,1:T(8,128)(2,1)S(1)} %copy-done, bf16[1848,512]{1,0:T(8,128)(2,1)} %reshape.21, s32[512]{0:T(512)S(1)} %copy-done.5), kind=kOutput, calls=%fused_computation.4 | convolution fusion | flops 1938976768 | bytes 4835328 | tf_op jit(solution)/shard_map/dot_general | solution.py:43
  89.4 0.0 copy-done.1
  89.4 2.6 %fusion = f32[1024,512]{0,1:S(1)} fusion(f32[512,512]{0,1:T(8,128)} %convolution_bitcast_fusion, bf16[512,1024]{1,0:T(8,128)(2,1)S(1)} %copy-done.1, f32[512]{0:T(512)S(1)} %select_multiply_fusion), kind=kOutput, calls=%fused_computation.5 | convolution fusion | flops 1612185600 | bytes 4196352
  92.0 0.2 convert_bitcast_fusion
  92.2 1.8 %copy.11 = bf16[8,1024,64]{2,1,0:T(8,128)(2,1)} copy(bf16[8,1024,64]{1,2,0:T(8,128)(2,1)S(1)} %convert_bitcast_fusion) | data formatting | bytes 2097152 | tf_op jit(solution)/shard_map/convert_element_type | solution.py:53
  94.0 3.9 %reshape.23 = bf16[128,2,2048]{2,1,0:T(2,128)(2,1)S(1)} reshape(bf16[8,1024,64]{2,1,0:T(8,128)(2,1)} %copy.11) | data formatting | bytes 2097152 | tf_op jit(solution)/shard_map/reshape | solution.py:54
  98.0 26.9 %all_to_all.16 = bf16[128,2,2048]{2,1,0:T(2,128)(2,1)S(1)} all-to-all(bf16[128,2,2048]{2,1,0:T(2,128)(2,1)S(1)} %reshape.23), channel_id=1, replica_groups=mesh['dp'=8,'row'=4,'col'=4] {'dp','row','col'}, dimensions={0} | all-to-all | bytes 2097152 | tf_op jit(solution)/shard_map/all_to_all | solution.py:55
  124.8 0.9 convert_reduce_fusion
  125.7 0.1 reshape.24
  125.8 0.7 copy.12
  (1 shorter events, 0.0 us)
Async XLA Ops:
  0.0 84.5 %copy-start = (bf16[512,1848]{0,1:T(8,128)(2,1)S(1)}, bf16[512,1848]{0,1:T(8,128)(2,1)}, u32[]{:S(2)}) copy-start(bf16[512,1848]{0,1:T(8,128)(2,1)} %param.8) | copy-start | bytes 5677060
  53.8 4.5 %copy-start.2 = (f32[512]{0:T(512)S(1)}, f32[512]{0:T(512)}, u32[]{:S(2)}) copy-start(f32[512]{0:T(512)} %param.12) | copy-start | bytes 6148
  53.8 4.5 %copy-start.3 = (s32[512]{0:T(512)S(1)}, s32[512]{0:T(512)}, u32[]{:S(2)}) copy-start(s32[512]{0:T(512)} %param.11) | copy-start | bytes 6148
  53.8 4.7 %copy-start.4 = (s32[512]{0:T(512)S(1)}, s32[512]{0:T(512)}, u32[]{:S(2)}) copy-start(s32[512]{0:T(512)} %param.10) | copy-start | bytes 6148
  53.8 27.4 %all-to-all-start.1 = ((bf16[8,231,512]{2,1,0:T(8,128)(2,1)}), bf16[8,231,512]{2,1,0:T(8,128)(2,1)}, u32[]{:S(2)}, u32[]{:S(2)}) async-start(bf16[8,231,512]{2,1,0:T(8,128)(2,1)} %broadcast_in_dim.31), calls=%async_computation.1 | async-start | bytes 3801088 | tf_op jit(solution)/shard_map/all_to_all | solution.py:15
  58.3 26.2 %copy-start.5 = (s32[512]{0:T(512)S(1)}, s32[512]{0:T(512)}, u32[]{:S(2)}) copy-start(s32[512]{0:T(512)} %param.15) | copy-start | bytes 6148
  84.5 4.9 %copy-start.1 = (bf16[512,1024]{1,0:T(8,128)(2,1)S(1)}, bf16[512,1024]{1,0:T(8,128)(2,1)}, u32[]{:S(2)}) copy-start(bf16[512,1024]{1,0:T(8,128)(2,1)} %param.9) | copy-start | bytes 3145732

commit v9 on v8

--- a/solution.py
+++ b/solution.py
@@ -52,7 +52,16 @@
     )
     blocks = partial.astype(jnp.bfloat16).transpose(1, 0, 2)
     blocks = blocks.reshape(n_dp * n_rc, 2, (cols // n_rc) * (slots // n_dp) // 2)
-    got = lax.all_to_all(blocks, ("dp", "row", "col"), 0, 0)
+    n_row, n_col = lax.axis_size("row"), lax.axis_size("col")
+    core = lax.axis_index("row") % 2
+    split = blocks.reshape((n_dp, n_row // 2, 2, n_col) + blocks.shape[1:])
+    mine = jnp.take(split, core, axis=2)
+    other = jnp.take(split, 1 - core, axis=2)
+    other = lax.ppermute(other, "row", [(r, r ^ 1) for r in range(n_row)])
+    summed = (mine.astype(jnp.float32) + other.astype(jnp.float32)).astype(jnp.bfloat16)
+    summed = summed.reshape((n_dp * n_rc // 2,) + blocks.shape[1:])
+    groups = [[m for m in range(n_dp * n_rc) if (m // n_col) % 2 == c] for c in range(2)]
+    got = lax.all_to_all(summed, ("dp", "row", "col"), 0, 0, axis_index_groups=groups)
     total = jnp.sum(got.astype(jnp.float32), axis=0)
     return total.reshape(cols // n_rc, slots // n_dp).T
 

time: 127 us -> 126 us (level)
  blocking collectives: 61.3 us -> 56.3 us
  other arithmetic: 3.13 us -> 5.29 us
  waiting for transfers between devices: 22.6 us -> 24.6 us
    all_to_all x1, blocking collectives: 26.9 us -> 21.8 us  [body(): lax.all_to_all(summed, ('dp', 'row', 'col'), 0, 0, axis_index_groups=groups)]
    another operation x0 -> x1, local copies, waits for them, and re-layouts: none -> 3.92 us  [body(): split = blocks.reshape((n_dp, n_row // 2, 2, n_col) + blocks.shape[1:])]
    reshape x1 -> x0, local copies, waits for them, and re-layouts: 3.92 us -> none  [body(): blocks = blocks.reshape(n_dp * n_rc, 2, cols // n_rc * (slots // n_dp) // 2)]
    convert_element_type x0 -> x1, other arithmetic: none -> 2.13 us  [body(): (mine.astype(jnp.float32) + other.astype(jnp.float32)).astype(jnp.bfloat16)]
    ppermute x0 -> x1, waiting for transfers between devices: none -> 2.01 us  [body(): other = lax.ppermute(other, 'row', [(r, r ^ 1) for r in range(n_row)])]
  transfers between devices with their start and end apart: 1 -> 2, of which waited for: 1 -> 2; matrix products, arithmetic and copies ran while one was open for 0% -> 0% of each run, Pallas kernels for 0% -> 0%
where the time goes in v9:
time: 126 us
  blocking collectives  56.3 us (45%)
  waiting for transfers between devices  24.6 us (20%)
  matrix products  20.3 us (16%)
  local copies, waits for them, and re-layouts  14.6 us (12%)
  other arithmetic  5.29 us (4%)
  starting transfers between devices  4.54 us (4%)
    all_to_all x1, blocking collectives, reduce_scatter(): got = lax.all_to_all(pieces, axis, 0, 0)  34.4 us
    all_to_all x1, waiting for transfers between devices, all_gather(): got = lax.all_to_all(pieces, axis, 0, 0)  22.6 us
    all_to_all x1, blocking collectives, body(): lax.all_to_all(summed, ('dp', 'row', 'col'), 0, 0, axis_index_groups=groups)  21.8 us
    dot_general x1, matrix products, body(): jnp.dot(inverse_gram, edit_keys, preferred_element_type=jnp.float32)  12.8 us
    dot_general x1, matrix products, body(): jnp.dot(hidden_acts, gram_keys, preferred_element_type=jnp.float32)  4.89 us
    all_to_all x1, starting transfers between devices, all_gather(): got = lax.all_to_all(pieces, axis, 0, 0)  4.45 us
    another operation x1, local copies, waits for them, and re-layouts, body(): split = blocks.reshape((n_dp, n_row // 2, 2, n_col) + blocks.shape[1:])  3.92 us
    reshape x1, local copies, waits for them, and re-layouts, reduce_scatter(): pieces = x.reshape((parts, x.shape[0] // parts) + x.shape[1:])  3.36 us
  transfers between devices with their start and end apart: 2, of which 2 were waited for; matrix products, arithmetic and copies ran while one was open for 0% of the time, Pallas kernels for 0%

profile of v9, /device:TPU:0, one launch (start us, length us, event | category | flops | bytes accessed | tf_op | source)
XLA Modules:
  0.0 125.7 jit_solution(3723208767403836816)
XLA Ops:
  0.0 0.0 copy-start
  0.0 12.8 %convolution_convert_fusion.1 = bf16[1848,512]{1,0:T(8,128)(2,1)} fusion(bf16[1848,3696]{1,0:T(8,128)(2,1)} %param.15, bf16[3696,512]{1,0:T(8,128)(2,1)} %param.16), kind=kOutput, calls=%fused_computation.1 | convolution fusion | flops 6995079168 | bytes 19337472 | tf_op jit(solution)/shard_map/dot_general | solution.py:38
  12.8 3.4 %reshape.21 = bf16[8,231,512]{2,1,0:T(8,128)(2,1)} reshape(bf16[1848,512]{1,0:T(8,128)(2,1)} %convolution_convert_fusion.1) | data formatting | bytes 3784704 | tf_op jit(solution)/shard_map/reshape | solution.py:8
  16.2 34.4 %all_to_all.15 = bf16[8,231,512]{2,1,0:T(8,128)(2,1)} all-to-all(bf16[8,231,512]{2,1,0:T(8,128)(2,1)} %reshape.21), channel_id=1, replica_groups=mesh['dp'=8,'row'=4,'col'=4] {'dp'}, dimensions={0} | all-to-all | bytes 3784704 | tf_op jit(solution)/shard_map/all_to_all | solution.py:9
  50.6 1.8 %reduce_sum.31 = bf16[231,512]{1,0:T(8,128)(2,1)S(1)} reduce(bf16[8,231,512]{2,1,0:T(8,128)(2,1)} %all_to_all.15, bf16[]{:T(256)} %constant.35.clone.1), dimensions={0}, to_apply=%region_1.2 | reduce | flops 827904 | bytes 2128898 | tf_op jit(solution)/shard_map/reduce_sum | solution.py:10
  52.4 1.4 %broadcast_in_dim.40 = bf16[8,231,512]{2,1,0:T(8,128)(2,1)} broadcast(bf16[231,512]{1,0:T(8,128)(2,1)S(1)} %reduce_sum.31), dimensions={1,2} | broadcast | bytes 2128896 | tf_op jit(solution)/shard_map/broadcast_in_dim | solution.py:14
  53.8 0.0 copy-start.2
  53.8 0.0 copy-start.3
  53.8 0.0 copy-start.4
  53.8 4.5 %all-to-all-start.1 = ((bf16[8,231,512]{2,1,0:T(8,128)(2,1)}), bf16[8,231,512]{2,1,0:T(8,128)(2,1)}, u32[]{:S(2)}, u32[]{:S(2)}) async-start(bf16[8,231,512]{2,1,0:T(8,128)(2,1)} %broadcast_in_dim.40), calls=%async_computation.1 | async-start | bytes 3801088 | tf_op jit(solution)/shard_map/all_to_all | solution.py:15
  58.3 0.0 copy-start.5
  58.3 0.0 copy-done.2
  58.3 0.0 copy-done.3
  58.3 0.2 select_reduce_fusion
  58.6 0.0 copy-done.4
  58.6 22.6 %all-to-all-done.1 = bf16[8,231,512]{2,1,0:T(8,128)(2,1)} async-done(((bf16[8,231,512]{2,1,0:T(8,128)(2,1)}), bf16[8,231,512]{2,1,0:T(8,128)(2,1)}, u32[]{:S(2)}, u32[]{:S(2)}) %all-to-all-start.1) | async-done | bytes 1892384 | tf_op jit(solution)/shard_map/all_to_all | solution.py:15
  81.2 3.3 %reshape.22 = bf16[1848,512]{1,0:T(8,128)(2,1)} reshape(bf16[8,231,512]{2,1,0:T(8,128)(2,1)} %all-to-all-done.1) | data formatting | bytes 3784704 | tf_op jit(solution)/shard_map/reshape | solution.py:16
  84.5 0.0 copy-done
  84.5 0.0 copy-done.5
  84.5 0.0 copy-start.1
  84.5 4.9 %convolution_bitcast_fusion = f32[512,512]{0,1:T(8,128)} fusion(bf16[512,1848]{0,1:T(8,128)(2,1)S(1)} %copy-done, bf16[1848,512]{1,0:T(8,128)(2,1)} %reshape.22, s32[512]{0:T(512)S(1)} %copy-done.5), kind=kOutput, calls=%fused_computation.3 | convolution fusion | flops 1938976768 | bytes 4835328 | tf_op jit(solution)/shard_map/dot_general | solution.py:43
  89.4 0.0 copy-done.1
  89.4 2.6 %fusion = f32[1024,512]{0,1:S(1)} fusion(f32[512,512]{0,1:T(8,128)} %convolution_bitcast_fusion, bf16[512,1024]{1,0:T(8,128)(2,1)S(1)} %copy-done.1, f32[512]{0:T(512)S(1)} %select_multiply_fusion), kind=kOutput, calls=%fused_computation.4 | convolution fusion | flops 1612185600 | bytes 4196352
  92.0 0.2 convert_bitcast_fusion
  92.2 1.8 %copy.13 = bf16[8,1024,64]{2,1,0:T(8,128)(2,1)} copy(bf16[8,1024,64]{1,2,0:T(8,128)(2,1)S(1)} %convert_bitcast_fusion) | data formatting | bytes 2097152 | tf_op jit(solution)/shard_map/convert_element_type | solution.py:53
  94.0 3.9 %reshape_reshape.3 = bf16[8,2,2,4,2,2048]{5,4,3,2,1,0:T(2,128)(2,1)S(1)} reshape(bf16[8,1024,64]{2,1,0:T(8,128)(2,1)} %copy.13) | data formatting | bytes 2097152 | tf_op jit(solution)/shard_map/reshape;reshape | solution.py:57
  98.0 0.5 fusion.3
  98.4 0.1 collective-permute-start
  98.5 2.0 %collective-permute-done = bf16[8,2,4,2,2048]{4,3,2,1,0:T(2,128)(2,1)} collective-permute-done((bf16[8,2,4,2,2048]{4,3,2,1,0:T(2,128)(2,1)S(1)}, bf16[8,2,4,2,2048]{4,3,2,1,0:T(2,128)(2,1)}, u32[]{:S(2)}, u32[]{:S(2)}) %collective-permute-start) | collective-permute-done | bytes 524320 | tf_op jit(solution)/shard_map/ppermute | solution.py:60
  100.5 2.1 %add_convert_fusion = bf16[8,2,4,2,2048]{4,3,2,1,0:T(2,128)(2,1)S(1)} fusion(bf16[8,2,4,2,2048]{4,3,2,1,0:T(2,128)(2,1)} %collective-permute-done, pred[]{:T(512)S(6)} %and.13, bf16[8,2,2,4,2,2048]{5,4,3,2,1,0:T(2,128)(2,1)S(1)} %reshape_reshape.3, s32[]{:T(128)S(6)} %select_n.30), kind=kLoop, calls=%fused_computation.6 | loop fusion | flops 1310720 | bytes 1572869 | tf_op jit(solution)/shard_map/convert_element_type | solution.py:61
  102.7 21.8 %all_to_all.16 = bf16[64,2,2048]{2,1,0:T(2,128)(2,1)S(1)} all-to-all(bf16[64,2,2048]{2,1,0:T(2,128)(2,1)S(1)} %bitcast.25), channel_id=1, replica_groups={{0,1,2,3,8,9,10,11,16,17,18,19,24,25,26,27,32,33,34,35,40,41,42,43,48,4..., dimensions={0} | all-to-all | bytes 1048576 | tf_op jit(solution)/shard_map/all_to_all | solution.py:64
  124.5 0.4 convert_reduce_fusion
  124.9 0.1 reshape.25
  125.0 0.7 copy.15
  (1 shorter events, 0.0 us)
Async XLA Ops:
  0.0 84.5 %copy-start = (bf16[512,1848]{0,1:T(8,128)(2,1)S(1)}, bf16[512,1848]{0,1:T(8,128)(2,1)}, u32[]{:S(2)}) copy-start(bf16[512,1848]{0,1:T(8,128)(2,1)} %param.10) | copy-start | bytes 5677060
  53.8 4.5 %copy-start.2 = (f32[512]{0:T(512)S(1)}, f32[512]{0:T(512)}, u32[]{:S(2)}) copy-start(f32[512]{0:T(512)} %param.14) | copy-start | bytes 6148
  53.8 4.5 %copy-start.3 = (s32[512]{0:T(512)S(1)}, s32[512]{0:T(512)}, u32[]{:S(2)}) copy-start(s32[512]{0:T(512)} %param.13) | copy-start | bytes 6148
  53.8 4.8 %copy-start.4 = (s32[512]{0:T(512)S(1)}, s32[512]{0:T(512)}, u32[]{:S(2)}) copy-start(s32[512]{0:T(512)} %param.12) | copy-start | bytes 6148
  53.8 27.4 %all-to-all-start.1 = ((bf16[8,231,512]{2,1,0:T(8,128)(2,1)}), bf16[8,231,512]{2,1,0:T(8,128)(2,1)}, u32[]{:S(2)}, u32[]{:S(2)}) async-start(bf16[8,231,512]{2,1,0:T(8,128)(2,1)} %broadcast_in_dim.40), calls=%async_computation.1 | async-start | bytes 3801088 | tf_op jit(solution)/shard_map/all_to_all | solution.py:15
  58.3 26.3 %copy-start.5 = (s32[512]{0:T(512)S(1)}, s32[512]{0:T(512)}, u32[]{:S(2)}) copy-start(s32[512]{0:T(512)} %param.17) | copy-start | bytes 6148
  84.5 4.9 %copy-start.1 = (bf16[512,1024]{1,0:T(8,128)(2,1)S(1)}, bf16[512,1024]{1,0:T(8,128)(2,1)}, u32[]{:S(2)}) copy-start(bf16[512,1024]{1,0:T(8,128)(2,1)} %param.11) | copy-start | bytes 3145732
  98.4 2.1 %collective-permute-start = (bf16[8,2,4,2,2048]{4,3,2,1,0:T(2,128)(2,1)S(1)}, bf16[8,2,4,2,2048]{4,3,2,1,0:T(2,128)(2,1)}, u32[]{:S(2)}, u32[]{:S(2)}) collective-permute-start(bf16[8,2,4,2,2048]{4,3,2,1,0:T(2,128)(2,1)S(1)} %fusion.3), channel_id=1, source_target_pairs={{0,4},{4,0},{8,12},{12,8},{1,5},{5,1},{9,13},{13,9},{2,6},{6,2},{1... | collective-permute-start | bytes 1572872 | tf_op jit(solution)/shard_map/ppermute | solution.py:60

commit v10 on v8

--- a/solution.py
+++ b/solution.py
@@ -37,10 +37,12 @@
 
     gram_keys = jnp.dot(inverse_gram, edit_keys, preferred_element_type=jnp.float32)
     gram_keys = reduce_scatter(gram_keys.astype(jnp.bfloat16), "dp", n_dp)
-    gram_keys = all_gather(gram_keys.astype(jnp.bfloat16), "dp", n_dp)
+    gram_keys = gram_keys.astype(jnp.bfloat16)
+    gathered = lax.all_to_all(jnp.broadcast_to(gram_keys[None], (n_dp,) + gram_keys.shape), "dp", 0, 0)
     order = (jnp.arange(edits, dtype=jnp.int32)[:, None] == edit_slots[None, :]).astype(jnp.bfloat16)
-    gram_keys = jnp.dot(gram_keys, order, preferred_element_type=jnp.float32).astype(jnp.bfloat16)
-    acts_keys = jnp.dot(hidden_acts, gram_keys, preferred_element_type=jnp.float32)
+    gathered = jnp.dot(gathered, order, preferred_element_type=jnp.float32).astype(jnp.bfloat16)
+    acts = hidden_acts.reshape(hidden_acts.shape[0], n_dp, hidden_acts.shape[1] // n_dp)
+    acts_keys = lax.dot_general(acts, gathered, (((1, 2), (0, 1)), ((), ())), preferred_element_type=jnp.float32)
     slots = acts_keys.shape[1]
     cols = scaled.shape[1]
     partial = lax.dot_general(

time: 127 us -> 115 us (0.906)
  local copies, waits for them, and re-layouts: 14.6 us -> 9.98 us
  waiting for transfers between devices: 22.6 us -> 19.1 us
  other arithmetic: 3.13 us -> 1.61 us
    all_to_all x1, waiting for transfers between devices: 22.6 us -> 19.1 us  [body(): lax.all_to_all(jnp.broadcast_to(gram_keys[None], (n_dp,) + gram_keys.shap...]
    reshape x1, local copies, waits for them, and re-layouts: 3.92 us -> 1.5 us  [body(): blocks = blocks.reshape(n_dp * n_rc, 2, cols // n_rc * (slots // n_dp) // 2)]
    reduce_sum x1, other arithmetic: 1.85 us -> 0.33 us  [reduce_scatter(): return jnp.sum(got.astype(jnp.float32), axis=0)]
    reshape x1, local copies, waits for them, and re-layouts: 3.36 us -> 1.84 us  [reduce_scatter(): pieces = x.reshape((parts, x.shape[0] // parts) + x.shape[1:])]
  transfers between devices with their start and end apart: 1 -> 1, of which waited for: 1 -> 1; matrix products, arithmetic and copies ran while one was open for 0% -> 3% of each run, Pallas kernels for 0% -> 0%
where the time goes in v10:
time: 115 us
  blocking collectives  61.2 us (53%)
  matrix products  19.1 us (17%)
  waiting for transfers between devices  19.1 us (17%)
  local copies, waits for them, and re-layouts  9.98 us (9%)
  starting transfers between devices  3.59 us (3%)
  other arithmetic  1.61 us (1%)
    all_to_all x1, blocking collectives, reduce_scatter(): got = lax.all_to_all(pieces, axis, 0, 0)  34.3 us
    all_to_all x1, blocking collectives, body(): got = lax.all_to_all(blocks, ('dp', 'row', 'col'), 0, 0)  26.8 us
    all_to_all x1, waiting for transfers between devices, body(): lax.all_to_all(jnp.broadcast_to(gram_keys[None], (n_dp,) + gram_keys.shap...  19.1 us
    dot_general x1, matrix products, body(): jnp.dot(inverse_gram, edit_keys, preferred_element_type=jnp.float32)  11.7 us
    dot_general x1, matrix products, body(): lax.dot_general(acts, gathered, (((1, 2), (0, 1)), ((), ())), preferred_e...  4.82 us
    all_to_all x1, starting transfers between devices, body(): lax.all_to_all(jnp.broadcast_to(gram_keys[None], (n_dp,) + gram_keys.shap...  3.59 us
    reshape x1, local copies, waits for them, and re-layouts, body(): hidden_acts.reshape(hidden_acts.shape[0], n_dp, hidden_acts.shape[1] // n...  3.38 us
    unnamed x1, matrix products  2.57 us
  transfers between devices with their start and end apart: 1, of which 1 were waited for; matrix products, arithmetic and copies ran while one was open for 3% of the time, Pallas kernels for 0%

profile of v10, /device:TPU:0, one launch (start us, length us, event | category | flops | bytes accessed | tf_op | source)
XLA Modules:
  0.0 114.7 jit_solution(12842106132960568733)
XLA Ops:
  0.0 11.7 %convolution_convert_fusion = bf16[1848,512]{1,0:T(8,128)(2,1)S(1)} fusion(bf16[1848,3696]{1,0:T(8,128)(2,1)} %param.13, bf16[3696,512]{1,0:T(8,128)(2,1)} %param.14), kind=kOutput, calls=%fused_computation | convolution fusion | flops 6995079168 | bytes 19337472 | tf_op jit(solution)/shard_map/dot_general | solution.py:38
  11.7 1.8 %reshape.20 = bf16[8,231,512]{2,1,0:T(8,128)(2,1)} reshape(bf16[1848,512]{1,0:T(8,128)(2,1)S(1)} %convolution_convert_fusion) | data formatting | bytes 3784704 | tf_op jit(solution)/shard_map/reshape | solution.py:8
  13.6 34.3 %all_to_all.15 = bf16[8,231,512]{2,1,0:T(8,128)(2,1)S(1)} all-to-all(bf16[8,231,512]{2,1,0:T(8,128)(2,1)} %reshape.20), channel_id=1, replica_groups=mesh['dp'=8,'row'=4,'col'=4] {'dp'}, dimensions={0} | all-to-all | bytes 3784704 | tf_op jit(solution)/shard_map/all_to_all | solution.py:9
  47.9 0.3 reduce_sum.31
  48.2 1.4 %broadcast_in_dim.31 = bf16[8,231,512]{2,1,0:T(8,128)(2,1)} broadcast(bf16[231,512]{1,0:T(8,128)(2,1)S(1)} %reduce_sum.31), dimensions={1,2} | broadcast | bytes 2128896 | tf_op jit(solution)/shard_map/broadcast_in_dim | solution.py:41
  49.6 3.6 %all-to-all-start.1 = ((bf16[8,231,512]{2,1,0:T(8,128)(2,1)}), bf16[8,231,512]{2,1,0:T(8,128)(2,1)S(1)}, u32[]{:S(2)}, u32[]{:S(2)}) async-start(bf16[8,231,512]{2,1,0:T(8,128)(2,1)} %broadcast_in_dim.31), calls=%async_computation.1 | async-start | bytes 3801088 | tf_op jit(solution)/shard_map/all_to_all | solution.py:41
  53.2 0.0 copy-start.1
  53.2 0.0 copy-start.2
  53.2 0.0 copy-start.3
  53.2 0.0 copy-start.4
  53.3 3.4 %reshape.21 = bf16[512,8,231]{0,2,1:T(8,128)(2,1)} reshape(bf16[512,1848]{0,1:T(8,128)(2,1)} %param.8) | data formatting | bytes 3784704 | tf_op jit(solution)/shard_map/reshape | solution.py:44
  56.6 0.0 copy-done.1
  56.6 0.0 copy-done.2
  56.6 0.2 select_reduce_fusion
  56.9 0.0 copy-done.3
  56.9 0.0 copy-start
  56.9 19.1 %all-to-all-done.1 = bf16[8,231,512]{2,1,0:T(8,128)(2,1)S(1)} async-done(((bf16[8,231,512]{2,1,0:T(8,128)(2,1)}), bf16[8,231,512]{2,1,0:T(8,128)(2,1)S(1)}, u32[]{:S(2)}, u32[]{:S(2)}) %all-to-all-start.1) | async-done | bytes 1892384 | tf_op jit(solution)/shard_map/all_to_all | solution.py:41
  76.1 0.0 copy-done.4
  76.1 4.8 %fusion.4 = f32[512,512]{0,1:T(8,128)} fusion(bf16[512,8,231]{0,2,1:T(8,128)(2,1)} %reshape.21, bf16[8,231,512]{2,1,0:T(8,128)(2,1)S(1)} %all-to-all-done.1, s32[512]{0:T(512)S(1)} %copy-done.4), kind=kOutput, calls=%fused_computation.6 | convolution fusion | flops 1938976768 | bytes 4835328 | tf_op jit(solution)/shard_map/dot_general | solution.py:45
  80.9 0.0 copy-done
  80.9 2.6 %fusion.7 = f32[1024,512]{0,1:S(1)} fusion(f32[512,512]{0,1:T(8,128)} %fusion.4, bf16[512,1024]{1,0:T(8,128)(2,1)S(1)} %copy-done, f32[512]{0:T(512)S(1)} %select_multiply_fusion), kind=kOutput, calls=%fused_computation.7 | convolution fusion | flops 1612185600 | bytes 4196352
  83.5 0.2 convert_bitcast_fusion
  83.6 1.1 copy.11
  84.7 1.5 %reshape.23 = bf16[128,2,2048]{2,1,0:T(2,128)(2,1)S(1)} reshape(bf16[8,1024,64]{2,1,0:T(8,128)(2,1)S(1)} %copy.11) | data formatting | bytes 2097152 | tf_op jit(solution)/shard_map/reshape | solution.py:56
  86.2 26.8 %all_to_all.16 = bf16[128,2,2048]{2,1,0:T(2,128)(2,1)S(1)} all-to-all(bf16[128,2,2048]{2,1,0:T(2,128)(2,1)S(1)} %reshape.23), channel_id=1, replica_groups=mesh['dp'=8,'row'=4,'col'=4] {'dp','row','col'}, dimensions={0} | all-to-all | bytes 2097152 | tf_op jit(solution)/shard_map/all_to_all | solution.py:57
  113.1 0.9 convert_reduce_fusion
  113.9 0.1 reshape.24
  114.0 0.7 copy.12
  (1 shorter events, 0.0 us)
Async XLA Ops:
  49.6 26.5 %all-to-all-start.1 = ((bf16[8,231,512]{2,1,0:T(8,128)(2,1)}), bf16[8,231,512]{2,1,0:T(8,128)(2,1)S(1)}, u32[]{:S(2)}, u32[]{:S(2)}) async-start(bf16[8,231,512]{2,1,0:T(8,128)(2,1)} %broadcast_in_dim.31), calls=%async_computation.1 | async-start | bytes 3801088 | tf_op jit(solution)/shard_map/all_to_all | solution.py:41
  53.2 3.4 %copy-start.1 = (f32[512]{0:T(512)S(1)}, f32[512]{0:T(512)}, u32[]{:S(2)}) copy-start(f32[512]{0:T(512)} %param.12) | copy-start | bytes 6148
  53.2 3.4 %copy-start.2 = (s32[512]{0:T(512)S(1)}, s32[512]{0:T(512)}, u32[]{:S(2)}) copy-start(s32[512]{0:T(512)} %param.11) | copy-start | bytes 6148
  53.2 3.7 %copy-start.3 = (s32[512]{0:T(512)S(1)}, s32[512]{0:T(512)}, u32[]{:S(2)}) copy-start(s32[512]{0:T(512)} %param.10) | copy-start | bytes 6148
  53.2 22.8 %copy-start.4 = (s32[512]{0:T(512)S(1)}, s32[512]{0:T(512)}, u32[]{:S(2)}) copy-start(s32[512]{0:T(512)} %param.15) | copy-start | bytes 6148
  56.9 24.0 %copy-start = (bf16[512,1024]{1,0:T(8,128)(2,1)S(1)}, bf16[512,1024]{1,0:T(8,128)(2,1)}, u32[]{:S(2)}) copy-start(bf16[512,1024]{1,0:T(8,128)(2,1)} %param.9) | copy-start | bytes 3145732

commit v11 on v10

--- a/solution.py
+++ b/solution.py
@@ -37,10 +37,9 @@
 
     gram_keys = jnp.dot(inverse_gram, edit_keys, preferred_element_type=jnp.float32)
     gram_keys = reduce_scatter(gram_keys.astype(jnp.bfloat16), "dp", n_dp)
-    gram_keys = gram_keys.astype(jnp.bfloat16)
+    order = (jnp.arange(edits, dtype=jnp.int32)[:, None] == edit_slots[None, :]).astype(jnp.bfloat16)
+    gram_keys = jnp.dot(gram_keys.astype(jnp.bfloat16), order, preferred_element_type=jnp.float32).astype(jnp.bfloat16)
     gathered = lax.all_to_all(jnp.broadcast_to(gram_keys[None], (n_dp,) + gram_keys.shape), "dp", 0, 0)
-    order = (jnp.arange(edits, dtype=jnp.int32)[:, None] == edit_slots[None, :]).astype(jnp.bfloat16)
-    gathered = jnp.dot(gathered, order, preferred_element_type=jnp.float32).astype(jnp.bfloat16)
     acts = hidden_acts.reshape(hidden_acts.shape[0], n_dp, hidden_acts.shape[1] // n_dp)
     acts_keys = lax.dot_general(acts, gathered, (((1, 2), (0, 1)), ((), ())), preferred_element_type=jnp.float32)
     slots = acts_keys.shape[1]

time: 115 us -> 112 us (0.974)
  matrix products: 19.1 us -> 16.3 us
    dot_general x1, matrix products: 4.82 us -> 2.79 us  [body(): lax.dot_general(acts, gathered, (((1, 2), (0, 1)), ((), ())), preferred_e...]
    unnamed x1, matrix products: 2.57 us -> 1.37 us
where the time goes in v11:
time: 112 us
  blocking collectives  61.3 us (55%)
  waiting for transfers between devices  19.2 us (17%)
  matrix products  16.3 us (15%)
  local copies, waits for them, and re-layouts  9.97 us (9%)
  starting transfers between devices  3.59 us (3%)
  other arithmetic  1.61 us (1%)
    all_to_all x1, blocking collectives, reduce_scatter(): got = lax.all_to_all(pieces, axis, 0, 0)  34.5 us
    all_to_all x1, blocking collectives, body(): got = lax.all_to_all(blocks, ('dp', 'row', 'col'), 0, 0)  26.8 us
    all_to_all x1, waiting for transfers between devices, body(): lax.all_to_all(jnp.broadcast_to(gram_keys[None], (n_dp,) + gram_keys.shap...  19.2 us
    dot_general x1, matrix products, body(): jnp.dot(inverse_gram, edit_keys, preferred_element_type=jnp.float32)  11.7 us
    all_to_all x1, starting transfers between devices, body(): lax.all_to_all(jnp.broadcast_to(gram_keys[None], (n_dp,) + gram_keys.shap...  3.59 us
    reshape x1, local copies, waits for them, and re-layouts, body(): hidden_acts.reshape(hidden_acts.shape[0], n_dp, hidden_acts.shape[1] // n...  3.34 us
    dot_general x1, matrix products, body(): lax.dot_general(acts, gathered, (((1, 2), (0, 1)), ((), ())), preferred_e...  2.79 us
  transfers between devices with their start and end apart: 1, of which 1 were waited for; matrix products, arithmetic and copies ran while one was open for 3% of the time, Pallas kernels for 0%

profile of v11, /device:TPU:0, one launch (start us, length us, event | category | flops | bytes accessed | tf_op | source)
XLA Modules:
  0.0 112.1 jit_solution(14494288042110720564)
XLA Ops:
  0.0 11.7 %convolution_convert_fusion = bf16[1848,512]{1,0:T(8,128)(2,1)S(1)} fusion(bf16[1848,3696]{1,0:T(8,128)(2,1)} %param.13, bf16[3696,512]{1,0:T(8,128)(2,1)} %param.14), kind=kOutput, calls=%fused_computation | convolution fusion | flops 6995079168 | bytes 19337472 | tf_op jit(solution)/shard_map/dot_general | solution.py:38
  11.7 1.8 %reshape.20 = bf16[8,231,512]{2,1,0:T(8,128)(2,1)} reshape(bf16[1848,512]{1,0:T(8,128)(2,1)S(1)} %convolution_convert_fusion) | data formatting | bytes 3784704 | tf_op jit(solution)/shard_map/reshape | solution.py:8
  13.6 0.0 copy-start.4
  13.6 34.5 %all_to_all.15 = bf16[8,231,512]{2,1,0:T(8,128)(2,1)S(1)} all-to-all(bf16[8,231,512]{2,1,0:T(8,128)(2,1)} %reshape.20), channel_id=1, replica_groups=mesh['dp'=8,'row'=4,'col'=4] {'dp'}, dimensions={0} | all-to-all | bytes 3784704 | tf_op jit(solution)/shard_map/all_to_all | solution.py:9
  48.0 0.3 reduce_sum.31
  48.4 0.0 copy-done.4
  48.4 0.4 convolution_convert_fusion.1
  48.8 1.4 %broadcast_in_dim.31 = bf16[8,231,512]{2,1,0:T(8,128)(2,1)} broadcast(bf16[231,512]{1,0:T(8,128)(2,1)S(1)} %convolution_convert_fusion.1), dimensions={1,2} | broadcast | bytes 2128896 | tf_op jit(solution)/shard_map/broadcast_in_dim | solution.py:42
  50.2 3.6 %all-to-all-start.1 = ((bf16[8,231,512]{2,1,0:T(8,128)(2,1)}), bf16[8,231,512]{2,1,0:T(8,128)(2,1)S(1)}, u32[]{:S(2)}, u32[]{:S(2)}) async-start(bf16[8,231,512]{2,1,0:T(8,128)(2,1)} %broadcast_in_dim.31), calls=%async_computation.1 | async-start | bytes 3801088 | tf_op jit(solution)/shard_map/all_to_all | solution.py:42
  53.8 0.0 copy-start.1
  53.8 0.0 copy-start.2
  53.8 0.0 copy-start.3
  53.8 3.3 %reshape.21 = bf16[512,8,231]{0,2,1:T(8,128)(2,1)} reshape(bf16[512,1848]{0,1:T(8,128)(2,1)} %param.8) | data formatting | bytes 3784704 | tf_op jit(solution)/shard_map/reshape | solution.py:43
  57.1 0.0 copy-done.1
  57.1 0.0 copy-done.2
  57.1 0.2 select_reduce_fusion
  57.4 0.0 copy-done.3
  57.4 0.0 copy-start
  57.4 19.2 %all-to-all-done.1 = bf16[8,231,512]{2,1,0:T(8,128)(2,1)S(1)} async-done(((bf16[8,231,512]{2,1,0:T(8,128)(2,1)}), bf16[8,231,512]{2,1,0:T(8,128)(2,1)S(1)}, u32[]{:S(2)}, u32[]{:S(2)}) %all-to-all-start.1) | async-done | bytes 1892384 | tf_op jit(solution)/shard_map/all_to_all | solution.py:42
  76.6 2.8 %convolution_bitcast_fusion = f32[512,512]{0,1:T(8,128)S(1)} fusion(bf16[8,231,512]{2,1,0:T(8,128)(2,1)S(1)} %all-to-all-done.1, bf16[512,8,231]{0,2,1:T(8,128)(2,1)} %reshape.21), kind=kOutput, calls=%fused_computation.3 | convolution fusion | flops 968884224 | bytes 4833280 | tf_op jit(solution)/shard_map/dot_general | solution.py:44
  79.4 0.0 copy-done
  79.4 1.4 %fusion = f32[1024,512]{0,1:S(1)} fusion(f32[512,512]{0,1:T(8,128)S(1)} %convolution_bitcast_fusion, bf16[512,1024]{1,0:T(8,128)(2,1)S(1)} %copy-done, f32[512]{0:T(512)S(1)} %select_multiply_fusion), kind=kOutput, calls=%fused_computation.5 | convolution fusion | flops 1612185600 | bytes 4196352
  80.8 0.2 convert_bitcast_fusion
  81.0 1.1 copy.11
  82.1 1.5 %reshape.23 = bf16[128,2,2048]{2,1,0:T(2,128)(2,1)S(1)} reshape(bf16[8,1024,64]{2,1,0:T(8,128)(2,1)S(1)} %copy.11) | data formatting | bytes 2097152 | tf_op jit(solution)/shard_map/reshape | solution.py:55
  83.6 26.8 %all_to_all.16 = bf16[128,2,2048]{2,1,0:T(2,128)(2,1)S(1)} all-to-all(bf16[128,2,2048]{2,1,0:T(2,128)(2,1)S(1)} %reshape.23), channel_id=1, replica_groups=mesh['dp'=8,'row'=4,'col'=4] {'dp','row','col'}, dimensions={0} | all-to-all | bytes 2097152 | tf_op jit(solution)/shard_map/all_to_all | solution.py:56
  110.4 0.9 convert_reduce_fusion
  111.3 0.1 reshape.24
  111.4 0.7 copy.12
  (1 shorter events, 0.0 us)
Async XLA Ops:
  13.6 34.8 %copy-start.4 = (s32[512]{0:T(512)S(1)}, s32[512]{0:T(512)}, u32[]{:S(2)}) copy-start(s32[512]{0:T(512)} %param.15) | copy-start | bytes 6148
  50.2 26.5 %all-to-all-start.1 = ((bf16[8,231,512]{2,1,0:T(8,128)(2,1)}), bf16[8,231,512]{2,1,0:T(8,128)(2,1)S(1)}, u32[]{:S(2)}, u32[]{:S(2)}) async-start(bf16[8,231,512]{2,1,0:T(8,128)(2,1)} %broadcast_in_dim.31), calls=%async_computation.1 | async-start | bytes 3801088 | tf_op jit(solution)/shard_map/all_to_all | solution.py:42
  53.8 3.4 %copy-start.1 = (f32[512]{0:T(512)S(1)}, f32[512]{0:T(512)}, u32[]{:S(2)}) copy-start(f32[512]{0:T(512)} %param.12) | copy-start | bytes 6148
  53.8 3.4 %copy-start.2 = (s32[512]{0:T(512)S(1)}, s32[512]{0:T(512)}, u32[]{:S(2)}) copy-start(s32[512]{0:T(512)} %param.11) | copy-start | bytes 6148
  53.8 3.6 %copy-start.3 = (s32[512]{0:T(512)S(1)}, s32[512]{0:T(512)}, u32[]{:S(2)}) copy-start(s32[512]{0:T(512)} %param.10) | copy-start | bytes 6148
  57.4 22.0 %copy-start = (bf16[512,1024]{1,0:T(8,128)(2,1)S(1)}, bf16[512,1024]{1,0:T(8,128)(2,1)}, u32[]{:S(2)}) copy-start(bf16[512,1024]{1,0:T(8,128)(2,1)} %param.9) | copy-start | bytes 3145732

commit v12 on v11

--- a/solution.py
+++ b/solution.py
@@ -35,12 +35,20 @@
     weight = jnp.where(is_paraphrase == 1, looked, jnp.float32(1.0)) / jnp.sqrt(jnp.float32(tokens))
     scaled = (out_cotangent.astype(jnp.float32) * weight[:, None]).astype(jnp.bfloat16)
 
-    gram_keys = jnp.dot(inverse_gram, edit_keys, preferred_element_type=jnp.float32)
-    gram_keys = reduce_scatter(gram_keys.astype(jnp.bfloat16), "dp", n_dp)
+    ff = inverse_gram.shape[0]
+    first = (ff // n_dp) // 2 // 16 * 16 * n_dp
+    chunks = ((0, first), (first, ff))
+    reduced = []
+    for lo, hi in chunks:
+        part = jnp.dot(inverse_gram[lo:hi], edit_keys, preferred_element_type=jnp.float32)
+        reduced.append(reduce_scatter(part.astype(jnp.bfloat16), "dp", n_dp))
+    gram_keys = jnp.concatenate(reduced, axis=0)
     order = (jnp.arange(edits, dtype=jnp.int32)[:, None] == edit_slots[None, :]).astype(jnp.bfloat16)
     gram_keys = jnp.dot(gram_keys.astype(jnp.bfloat16), order, preferred_element_type=jnp.float32).astype(jnp.bfloat16)
     gathered = lax.all_to_all(jnp.broadcast_to(gram_keys[None], (n_dp,) + gram_keys.shape), "dp", 0, 0)
-    acts = hidden_acts.reshape(hidden_acts.shape[0], n_dp, hidden_acts.shape[1] // n_dp)
+    acts = jnp.concatenate(
+        [hidden_acts[:, lo:hi].reshape(hidden_acts.shape[0], n_dp, (hi - lo) // n_dp) for lo, hi in chunks], axis=2
+    )
     acts_keys = lax.dot_general(acts, gathered, (((1, 2), (0, 1)), ((), ())), preferred_element_type=jnp.float32)
     slots = acts_keys.shape[1]
     cols = scaled.shape[1]

time: 112 us -> 117 us (1.045)
  blocking collectives: 61.3 us -> 26.8 us
  waiting for transfers between devices: 19.2 us -> 43.1 us
  starting transfers between devices: 3.59 us -> 16.1 us
  matrix products: 16.3 us -> 21.3 us
  local copies, waits for them, and re-layouts: 9.97 us -> 7.48 us
    all_to_all x1 -> x0, blocking collectives: 34.5 us -> none  [reduce_scatter(): got = lax.all_to_all(pieces, axis, 0, 0)]
    all_to_all x0 -> x2, waiting for transfers between devices: none -> 20.5 us  [reduce_scatter(): got = lax.all_to_all(pieces, axis, 0, 0)]
    all_to_all x0 -> x2, starting transfers between devices: none -> 11.8 us  [reduce_scatter(): got = lax.all_to_all(pieces, axis, 0, 0)]
    dot_general x1 -> x2, matrix products: 11.7 us -> 16.7 us  [body(): jnp.dot(inverse_gram[lo:hi], edit_keys, preferred_element_type=jnp.float32)]
    all_to_all x1, waiting for transfers between devices: 19.2 us -> 22.6 us  [body(): lax.all_to_all(jnp.broadcast_to(gram_keys[None], (n_dp,) + gram_keys.shap...]
    reshape x1, local copies, waits for them, and re-layouts: 3.34 us -> 0.29 us  [body(): hidden_acts[:, lo:hi].reshape(hidden_acts.shape[0], n_dp, (hi - lo) // n_dp)]
  transfers between devices with their start and end apart: 1 -> 3, of which waited for: 1 -> 3; matrix products, arithmetic and copies ran while one was open for 3% -> 9% of each run, Pallas kernels for 0% -> 0%
where the time goes in v12:
time: 117 us
  waiting for transfers between devices  43.1 us (37%)
  blocking collectives  26.8 us (23%)
  matrix products  21.3 us (18%)
  starting transfers between devices  16.1 us (14%)
  local copies, waits for them, and re-layouts  7.48 us (6%)
  other arithmetic  1.56 us (1%)
    all_to_all x1, blocking collectives, body(): got = lax.all_to_all(blocks, ('dp', 'row', 'col'), 0, 0)  26.8 us
    all_to_all x1, waiting for transfers between devices, body(): lax.all_to_all(jnp.broadcast_to(gram_keys[None], (n_dp,) + gram_keys.shap...  22.6 us
    all_to_all x2, waiting for transfers between devices, reduce_scatter(): got = lax.all_to_all(pieces, axis, 0, 0)  20.5 us
    dot_general x2, matrix products, body(): jnp.dot(inverse_gram[lo:hi], edit_keys, preferred_element_type=jnp.float32)  16.7 us
    all_to_all x2, starting transfers between devices, reduce_scatter(): got = lax.all_to_all(pieces, axis, 0, 0)  11.8 us
    all_to_all x1, starting transfers between devices, body(): lax.all_to_all(jnp.broadcast_to(gram_keys[None], (n_dp,) + gram_keys.shap...  4.31 us
    dot_general x1, matrix products, body(): lax.dot_general(acts, gathered, (((1, 2), (0, 1)), ((), ())), preferred_e...  2.9 us
  transfers between devices with their start and end apart: 3, of which 3 were waited for; matrix products, arithmetic and copies ran while one was open for 9% of the time, Pallas kernels for 0%

profile of v12, /device:TPU:0, one launch (start us, length us, event | category | flops | bytes accessed | tf_op | source)
XLA Modules:
  0.0 116.6 jit_solution(10263828539921441185)
XLA Ops:
  0.0 8.6 %fusion.11 = bf16[896,512]{1,0:T(8,128)(2,1)} fusion(bf16[3696,512]{1,0:T(8,128)(2,1)} %param.14, bf16[1848,3696]{1,0:T(8,128)(2,1)} %param.13), kind=kOutput, calls=%fused_computation.11 | convolution fusion | flops 3391553536 | bytes 11354112 | tf_op jit(solution)/shard_map/dot_general | solution.py:43
  8.6 7.9 %all-to-all-start = ((bf16[8,112,512]{2,1,0:T(8,128)(2,1)}), bf16[8,112,512]{2,1,0:T(8,128)(2,1)S(1)}, u32[]{:S(2)}, u32[]{:S(2)}) async-start(bf16[8,112,512]{2,1,0:T(8,128)(2,1)} %bitcast.1), calls=%async_computation | async-start | bytes 1835008 | tf_op jit(solution)/shard_map/all_to_all | solution.py:9
  16.5 8.0 %fusion.8 = bf16[952,512]{1,0:T(8,128)(2,1)S(1)} fusion(bf16[3696,512]{1,0:T(8,128)(2,1)} %param.14, bf16[1848,3696]{1,0:T(8,128)(2,1)} %param.13), kind=kOutput, calls=%fused_computation.10 | convolution fusion | flops 3603525632 | bytes 11827200 | tf_op jit(solution)/shard_map/dot_general | solution.py:43
  24.6 1.3 %reshape.29 = bf16[8,119,512]{2,1,0:T(8,128)(2,1)} reshape(bf16[952,512]{1,0:T(8,128)(2,1)S(1)} %fusion.8) | data formatting | bytes 1949696 | tf_op jit(solution)/shard_map/reshape | solution.py:8
  25.8 0.0 copy-start.4
  25.8 5.3 %all-to-all-done = bf16[8,112,512]{2,1,0:T(8,128)(2,1)S(1)} async-done(((bf16[8,112,512]{2,1,0:T(8,128)(2,1)}), bf16[8,112,512]{2,1,0:T(8,128)(2,1)S(1)}, u32[]{:S(2)}, u32[]{:S(2)}) %all-to-all-start) | async-done | bytes 917536 | tf_op jit(solution)/shard_map/all_to_all | solution.py:9
  31.1 3.9 %all-to-all-start.1 = ((bf16[8,119,512]{2,1,0:T(8,128)(2,1)}), bf16[8,119,512]{2,1,0:T(8,128)(2,1)S(1)}, u32[]{:S(2)}, u32[]{:S(2)}) async-start(bf16[8,119,512]{2,1,0:T(8,128)(2,1)} %reshape.29), calls=%async_computation.1 | async-start | bytes 1966080 | tf_op jit(solution)/shard_map/all_to_all | solution.py:9
  35.1 0.1 reduce
  35.2 15.2 %all-to-all-done.1 = bf16[8,119,512]{2,1,0:T(8,128)(2,1)S(1)} async-done(((bf16[8,119,512]{2,1,0:T(8,128)(2,1)}), bf16[8,119,512]{2,1,0:T(8,128)(2,1)S(1)}, u32[]{:S(2)}, u32[]{:S(2)}) %all-to-all-start.1) | async-done | bytes 974880 | tf_op jit(solution)/shard_map/all_to_all | solution.py:9
  50.4 0.1 reduce.1
  50.5 0.0 copy-done.4
  50.5 0.4 convolution_convert_fusion
  50.9 1.4 %broadcast_in_dim.31 = bf16[8,231,512]{2,1,0:T(8,128)(2,1)} broadcast(bf16[231,512]{1,0:T(8,128)(2,1)S(1)} %convolution_convert_fusion), dimensions={1,2} | broadcast | bytes 2128896 | tf_op jit(solution)/shard_map/broadcast_in_dim | solution.py:48
  52.3 4.3 %all-to-all-start.2 = ((bf16[8,231,512]{2,1,0:T(8,128)(2,1)}), bf16[8,231,512]{2,1,0:T(8,128)(2,1)}, u32[]{:S(2)}, u32[]{:S(2)}) async-start(bf16[8,231,512]{2,1,0:T(8,128)(2,1)} %broadcast_in_dim.31), calls=%async_computation.2 | async-start | bytes 3801088 | tf_op jit(solution)/shard_map/all_to_all | solution.py:48
  56.6 0.0 slice-start
  56.7 0.0 copy-start.1
  56.7 0.0 copy-start.2
  56.7 0.0 copy-start.3
  56.7 0.0 slice-start.1
  56.7 1.1 slice-done
  57.8 0.3 reshape.27
  58.1 0.0 copy-done.1
  58.1 0.0 copy-done.2
  58.2 0.2 select_reduce_fusion
  58.4 0.0 copy-done.3
  58.4 22.6 %all-to-all-done.2 = bf16[8,231,512]{2,1,0:T(8,128)(2,1)} async-done(((bf16[8,231,512]{2,1,0:T(8,128)(2,1)}), bf16[8,231,512]{2,1,0:T(8,128)(2,1)}, u32[]{:S(2)}, u32[]{:S(2)}) %all-to-all-start.2) | async-done | bytes 1892384 | tf_op jit(solution)/shard_map/all_to_all | solution.py:48
  81.0 0.0 slice-done.1
  81.0 0.0 copy-start
  81.0 2.9 %fusion.14 = f32[512,512]{0,1:T(8,128)S(1)} fusion(bf16[8,231,512]{2,1,0:T(8,128)(2,1)} %all-to-all-done.2, bf16[512,8,119]{0,2,1:T(8,128)(2,1)S(1)} %reshape.27, bf16[512,8,112]{0,2,1:T(8,128)(2,1)S(1)} %bitcast.19), kind=kOutput, calls=%fused_computation.12 | convolution fusion | flops 972668928 | bytes 4833280 | tf_op jit(solution)/shard_map/dot_general | solution.py:52
  83.9 0.0 copy-done
  83.9 1.4 %fusion.17 = f32[1024,512]{0,1:S(1)} fusion(f32[512,512]{0,1:T(8,128)S(1)} %fusion.14, bf16[512,1024]{1,0:T(8,128)(2,1)S(1)} %copy-done, f32[512]{0:T(512)S(1)} %select_multiply_fusion), kind=kOutput, calls=%fused_computation.14 | convolution fusion | flops 1612185600 | bytes 4196352
  85.3 0.2 convert_bitcast_fusion
  85.5 1.1 copy.11
  86.6 1.5 %reshape.31 = bf16[128,2,2048]{2,1,0:T(2,128)(2,1)S(1)} reshape(bf16[8,1024,64]{2,1,0:T(8,128)(2,1)S(1)} %copy.11) | data formatting | bytes 2097152 | tf_op jit(solution)/shard_map/reshape | solution.py:63
  88.1 26.8 %all_to_all.20 = bf16[128,2,2048]{2,1,0:T(2,128)(2,1)S(1)} all-to-all(bf16[128,2,2048]{2,1,0:T(2,128)(2,1)S(1)} %reshape.31), channel_id=1, replica_groups=mesh['dp'=8,'row'=4,'col'=4] {'dp','row','col'}, dimensions={0} | all-to-all | bytes 2097152 | tf_op jit(solution)/shard_map/all_to_all | solution.py:64
  114.9 0.9 convert_reduce_fusion
  115.8 0.1 reshape.32
  115.9 0.7 copy.12
  (1 shorter events, 0.0 us)
Async XLA Ops:
  8.6 22.5 %all-to-all-start = ((bf16[8,112,512]{2,1,0:T(8,128)(2,1)}), bf16[8,112,512]{2,1,0:T(8,128)(2,1)S(1)}, u32[]{:S(2)}, u32[]{:S(2)}) async-start(bf16[8,112,512]{2,1,0:T(8,128)(2,1)} %bitcast.1), calls=%async_computation | async-start | bytes 1835008 | tf_op jit(solution)/shard_map/all_to_all | solution.py:9
  25.8 24.7 %copy-start.4 = (s32[512]{0:T(512)S(1)}, s32[512]{0:T(512)}, u32[]{:S(2)}) copy-start(s32[512]{0:T(512)} %param.15) | copy-start | bytes 6148
  31.1 19.2 %all-to-all-start.1 = ((bf16[8,119,512]{2,1,0:T(8,128)(2,1)}), bf16[8,119,512]{2,1,0:T(8,128)(2,1)S(1)}, u32[]{:S(2)}, u32[]{:S(2)}) async-start(bf16[8,119,512]{2,1,0:T(8,128)(2,1)} %reshape.29), calls=%async_computation.1 | async-start | bytes 1966080 | tf_op jit(solution)/shard_map/all_to_all | solution.py:9
  52.3 28.7 %all-to-all-start.2 = ((bf16[8,231,512]{2,1,0:T(8,128)(2,1)}), bf16[8,231,512]{2,1,0:T(8,128)(2,1)}, u32[]{:S(2)}, u32[]{:S(2)}) async-start(bf16[8,231,512]{2,1,0:T(8,128)(2,1)} %broadcast_in_dim.31), calls=%async_computation.2 | async-start | bytes 3801088 | tf_op jit(solution)/shard_map/all_to_all | solution.py:48
  56.6 1.2 %slice-start = ((bf16[512,1848]{0,1:T(8,128)(2,1)}), bf16[512,952]{0,1:T(8,128)(2,1)S(1)}, s32[]{:S(2)}) async-start(bf16[512,1848]{0,1:T(8,128)(2,1)} %param.8), calls=%async_computation.4 | async-start | bytes 1949696 | tf_op jit(solution)/shard_map/slice | solution.py:50
  56.7 1.5 %copy-start.1 = (f32[512]{0:T(512)S(1)}, f32[512]{0:T(512)}, u32[]{:S(2)}) copy-start(f32[512]{0:T(512)} %param.12) | copy-start | bytes 6148
  56.7 1.5 %copy-start.2 = (s32[512]{0:T(512)S(1)}, s32[512]{0:T(512)}, u32[]{:S(2)}) copy-start(s32[512]{0:T(512)} %param.11) | copy-start | bytes 6148
  56.7 1.7 %copy-start.3 = (s32[512]{0:T(512)S(1)}, s32[512]{0:T(512)}, u32[]{:S(2)}) copy-start(s32[512]{0:T(512)} %param.10) | copy-start | bytes 6148
  56.7 24.3 %slice-start.1 = ((bf16[512,1848]{0,1:T(8,128)(2,1)}), bf16[512,896]{0,1:T(8,128)(2,1)S(1)}, s32[]{:S(2)}) async-start(bf16[512,1848]{0,1:T(8,128)(2,1)} %param.8), calls=%async_computation.5 | async-start | bytes 1835008 | tf_op jit(solution)/shard_map/slice | solution.py:50
  81.0 2.9 %copy-start = (bf16[512,1024]{1,0:T(8,128)(2,1)S(1)}, bf16[512,1024]{1,0:T(8,128)(2,1)}, u32[]{:S(2)}) copy-start(bf16[512,1024]{1,0:T(8,128)(2,1)} %param.9) | copy-start | bytes 3145732

commit v13 on v11

--- a/solution.py
+++ b/solution.py
@@ -46,9 +46,8 @@
     cols = scaled.shape[1]
     partial = lax.dot_general(
         scaled,
-        acts_keys.reshape(acts_keys.shape[0], n_dp, slots // n_dp),
+        acts_keys.astype(jnp.bfloat16).reshape(acts_keys.shape[0], n_dp, slots // n_dp),
         (((0,), (0,)), ((), ())),
-        precision=lax.Precision.HIGH,
         preferred_element_type=jnp.float32,
     )
     blocks = partial.astype(jnp.bfloat16).transpose(1, 0, 2)

time: 112 us -> 113 us (level)
  waiting for transfers between devices: 19.2 us -> 20.8 us
  local copies, waits for them, and re-layouts: 9.97 us -> 8.45 us
    dot_general x1 -> x0, matrix products: 2.79 us -> none  [body(): lax.dot_general(acts, gathered, (((1, 2), (0, 1)), ((), ())), preferred_e...]
    unnamed x1, matrix products: 1.37 us -> 3.93 us
    all_to_all x1, waiting for transfers between devices: 19.2 us -> 20.8 us  [body(): lax.all_to_all(jnp.broadcast_to(gram_keys[None], (n_dp,) + gram_keys.shap...]
    reshape x1, local copies, waits for them, and re-layouts: 3.34 us -> 1.85 us  [body(): hidden_acts.reshape(hidden_acts.shape[0], n_dp, hidden_acts.shape[1] // n...]
  transfers between devices with their start and end apart: 1 -> 1, of which waited for: 1 -> 1; matrix products, arithmetic and copies ran while one was open for 3% -> 2% of each run, Pallas kernels for 0% -> 0%
where the time goes in v13:
time: 113 us
  blocking collectives  61.3 us (54%)
  waiting for transfers between devices  20.8 us (18%)
  matrix products  16 us (14%)
  local copies, waits for them, and re-layouts  8.45 us (7%)
  starting transfers between devices  4.45 us (4%)
  other arithmetic  1.62 us (1%)
    all_to_all x1, blocking collectives, reduce_scatter(): got = lax.all_to_all(pieces, axis, 0, 0)  34.5 us
    all_to_all x1, blocking collectives, body(): got = lax.all_to_all(blocks, ('dp', 'row', 'col'), 0, 0)  26.8 us
    all_to_all x1, waiting for transfers between devices, body(): lax.all_to_all(jnp.broadcast_to(gram_keys[None], (n_dp,) + gram_keys.shap...  20.8 us
    dot_general x1, matrix products, body(): jnp.dot(inverse_gram, edit_keys, preferred_element_type=jnp.float32)  11.7 us
    all_to_all x1, starting transfers between devices, body(): lax.all_to_all(jnp.broadcast_to(gram_keys[None], (n_dp,) + gram_keys.shap...  4.45 us
    unnamed x1, matrix products  3.93 us
  transfers between devices with their start and end apart: 1, of which 1 were waited for; matrix products, arithmetic and copies ran while one was open for 2% of the time, Pallas kernels for 0%

profile of v13, /device:TPU:0, one launch (start us, length us, event | category | flops | bytes accessed | tf_op | source)
XLA Modules:
  0.0 112.7 jit_solution(12617917829117391625)
XLA Ops:
  0.0 11.7 %convolution_convert_fusion = bf16[1848,512]{1,0:T(8,128)(2,1)S(1)} fusion(bf16[1848,3696]{1,0:T(8,128)(2,1)} %param.13, bf16[3696,512]{1,0:T(8,128)(2,1)} %param.14), kind=kOutput, calls=%fused_computation | convolution fusion | flops 6995079168 | bytes 19337472 | tf_op jit(solution)/shard_map/dot_general | solution.py:38
  11.7 1.8 %reshape.20 = bf16[8,231,512]{2,1,0:T(8,128)(2,1)} reshape(bf16[1848,512]{1,0:T(8,128)(2,1)S(1)} %convolution_convert_fusion) | data formatting | bytes 3784704 | tf_op jit(solution)/shard_map/reshape | solution.py:8
  13.6 0.0 copy-start.5
  13.6 34.5 %all_to_all.15 = bf16[8,231,512]{2,1,0:T(8,128)(2,1)S(1)} all-to-all(bf16[8,231,512]{2,1,0:T(8,128)(2,1)} %reshape.20), channel_id=1, replica_groups=mesh['dp'=8,'row'=4,'col'=4] {'dp'}, dimensions={0} | all-to-all | bytes 3784704 | tf_op jit(solution)/shard_map/all_to_all | solution.py:9
  48.0 0.3 reduce_sum.31
  48.4 0.0 copy-done.5
  48.4 0.4 convolution_convert_fusion.1
  48.8 1.4 %broadcast_in_dim.31 = bf16[8,231,512]{2,1,0:T(8,128)(2,1)} broadcast(bf16[231,512]{1,0:T(8,128)(2,1)S(1)} %convolution_convert_fusion.1), dimensions={1,2} | broadcast | bytes 2128896 | tf_op jit(solution)/shard_map/broadcast_in_dim | solution.py:42
  50.1 0.0 copy-start
  50.1 4.4 %all-to-all-start.1 = ((bf16[8,231,512]{2,1,0:T(8,128)(2,1)}), bf16[8,231,512]{2,1,0:T(8,128)(2,1)}, u32[]{:S(2)}, u32[]{:S(2)}) async-start(bf16[8,231,512]{2,1,0:T(8,128)(2,1)} %broadcast_in_dim.31), calls=%async_computation.1 | async-start | bytes 3801088 | tf_op jit(solution)/shard_map/all_to_all | solution.py:42
  54.6 0.0 copy-done
  54.6 0.0 copy-start.1
  54.6 0.0 copy-start.2
  54.6 0.0 copy-start.3
  54.6 0.0 copy-start.4
  54.6 1.9 %reshape.21 = bf16[512,8,231]{0,2,1:T(8,128)(2,1)} reshape(bf16[512,1848]{0,1:T(8,128)(2,1)S(1)} %copy-done) | data formatting | bytes 3784704 | tf_op jit(solution)/shard_map/reshape | solution.py:43
  56.5 0.0 copy-done.1
  56.5 0.0 copy-done.2
  56.5 0.2 select_reduce_fusion
  56.7 0.0 copy-done.3
  56.8 20.8 %all-to-all-done.1 = bf16[8,231,512]{2,1,0:T(8,128)(2,1)} async-done(((bf16[8,231,512]{2,1,0:T(8,128)(2,1)}), bf16[8,231,512]{2,1,0:T(8,128)(2,1)}, u32[]{:S(2)}, u32[]{:S(2)}) %all-to-all-start.1) | async-done | bytes 1892384 | tf_op jit(solution)/shard_map/all_to_all | solution.py:42
  77.5 0.0 copy-done.4
  77.5 3.9 %fusion.2 = f32[1024,512]{0,1:S(1)} fusion(bf16[8,231,512]{2,1,0:T(8,128)(2,1)} %all-to-all-done.1, bf16[512,8,231]{0,2,1:T(8,128)(2,1)} %reshape.21, bf16[512,1024]{1,0:T(8,128)(2,1)S(1)} %copy-done.4, f32[512]{0:T(512)S(1)} %select_multiply_fusion), kind=kOutput, calls=%fused_computation.7 | convolution fusion | flops 1507590144 | bytes 6932480
  81.5 0.2 convert_bitcast_fusion
  81.6 1.1 copy.11
  82.7 1.5 %reshape.23 = bf16[128,2,2048]{2,1,0:T(2,128)(2,1)S(1)} reshape(bf16[8,1024,64]{2,1,0:T(8,128)(2,1)S(1)} %copy.11) | data formatting | bytes 2097152 | tf_op jit(solution)/shard_map/reshape | solution.py:54
  84.2 26.8 %all_to_all.16 = bf16[128,2,2048]{2,1,0:T(2,128)(2,1)S(1)} all-to-all(bf16[128,2,2048]{2,1,0:T(2,128)(2,1)S(1)} %reshape.23), channel_id=1, replica_groups=mesh['dp'=8,'row'=4,'col'=4] {'dp','row','col'}, dimensions={0} | all-to-all | bytes 2097152 | tf_op jit(solution)/shard_map/all_to_all | solution.py:55
  111.0 0.9 convert_reduce_fusion
  111.9 0.1 reshape.24
  112.0 0.7 copy.12
  (1 shorter events, 0.0 us)
Async XLA Ops:
  13.6 34.8 %copy-start.5 = (s32[512]{0:T(512)S(1)}, s32[512]{0:T(512)}, u32[]{:S(2)}) copy-start(s32[512]{0:T(512)} %param.15) | copy-start | bytes 6148
  50.1 4.5 %copy-start = (bf16[512,1848]{0,1:T(8,128)(2,1)S(1)}, bf16[512,1848]{0,1:T(8,128)(2,1)}, u32[]{:S(2)}) copy-start(bf16[512,1848]{0,1:T(8,128)(2,1)} %param.8) | copy-start | bytes 5677060
  50.1 27.4 %all-to-all-start.1 = ((bf16[8,231,512]{2,1,0:T(8,128)(2,1)}), bf16[8,231,512]{2,1,0:T(8,128)(2,1)}, u32[]{:S(2)}, u32[]{:S(2)}) async-start(bf16[8,231,512]{2,1,0:T(8,128)(2,1)} %broadcast_in_dim.31), calls=%async_computation.1 | async-start | bytes 3801088 | tf_op jit(solution)/shard_map/all_to_all | solution.py:42
  54.6 1.9 %copy-start.1 = (f32[512]{0:T(512)S(1)}, f32[512]{0:T(512)}, u32[]{:S(2)}) copy-start(f32[512]{0:T(512)} %param.12) | copy-start | bytes 6148
  54.6 1.9 %copy-start.2 = (s32[512]{0:T(512)S(1)}, s32[512]{0:T(512)}, u32[]{:S(2)}) copy-start(s32[512]{0:T(512)} %param.11) | copy-start | bytes 6148
  54.6 2.1 %copy-start.3 = (s32[512]{0:T(512)S(1)}, s32[512]{0:T(512)}, u32[]{:S(2)}) copy-start(s32[512]{0:T(512)} %param.10) | copy-start | bytes 6148
  54.6 22.9 %copy-start.4 = (bf16[512,1024]{1,0:T(8,128)(2,1)S(1)}, bf16[512,1024]{1,0:T(8,128)(2,1)}, u32[]{:S(2)}) copy-start(bf16[512,1024]{1,0:T(8,128)(2,1)} %param.9) | copy-start | bytes 3145732

commit v14 on v11

--- a/solution.py
+++ b/solution.py
@@ -1,7 +1,32 @@
 import jax
 import jax.numpy as jnp
 from jax import lax
+from jax.experimental import pallas as pl
 from jax.sharding import PartitionSpec as P
+
+
+def gram_keys_kernel(g_ref, k_ref, o_ref):
+    o_ref[...] = jnp.dot(g_ref[...], k_ref[...], preferred_element_type=jnp.float32).astype(o_ref.dtype)
+
+
+def gram_times_keys(gram, keys, block_rows):
+    rows, inner = gram.shape
+    width = keys.shape[1]
+    return pl.pallas_call(
+        gram_keys_kernel,
+        grid=(rows // block_rows,),
+        in_specs=[
+            pl.BlockSpec((block_rows, inner), lambda i: (i, 0)),
+            pl.BlockSpec((inner, width), lambda i: (0, 0)),
+        ],
+        out_specs=pl.BlockSpec((block_rows, width), lambda i: (i, 0)),
+        out_shape=jax.ShapeDtypeStruct((rows, width), jnp.bfloat16),
+        cost_estimate=pl.CostEstimate(
+            flops=2 * rows * inner * width,
+            bytes_accessed=2 * (rows * inner + inner * width + rows * width),
+            transcendentals=0,
+        ),
+    )(gram, keys)
 
 
 def reduce_scatter(x, axis, parts):
@@ -35,7 +60,7 @@
     weight = jnp.where(is_paraphrase == 1, looked, jnp.float32(1.0)) / jnp.sqrt(jnp.float32(tokens))
     scaled = (out_cotangent.astype(jnp.float32) * weight[:, None]).astype(jnp.bfloat16)
 
-    gram_keys = jnp.dot(inverse_gram, edit_keys, preferred_element_type=jnp.float32)
+    gram_keys = gram_times_keys(inverse_gram, edit_keys, inverse_gram.shape[0] // 7)
     gram_keys = reduce_scatter(gram_keys.astype(jnp.bfloat16), "dp", n_dp)
     order = (jnp.arange(edits, dtype=jnp.int32)[:, None] == edit_slots[None, :]).astype(jnp.bfloat16)
     gram_keys = jnp.dot(gram_keys.astype(jnp.bfloat16), order, preferred_element_type=jnp.float32).astype(jnp.bfloat16)

time: 112 us -> 116 us (1.036)
  Pallas kernels: 0 us -> 13.3 us
  matrix products: 16.3 us -> 4.54 us
  local copies, waits for them, and re-layouts: 9.97 us -> 11.8 us
    pallas_call x0 -> x1, Pallas kernels: none -> 13.3 us  [gram_times_keys(): pl.pallas_call(gram_keys_kernel, grid=(rows // block_rows,), in_specs=[pl...]
    dot_general x1 -> x0, matrix products: 11.7 us -> none  [body(): jnp.dot(inverse_gram, edit_keys, preferred_element_type=jnp.float32)]
    reshape x1, local copies, waits for them, and re-layouts: 1.84 us -> 3.36 us  [reduce_scatter(): pieces = x.reshape((parts, x.shape[0] // parts) + x.shape[1:])]
where the time goes in v14:
time: 116 us; the launch traced here: 115 us
  blocking collectives  61.2 us (53%)
  waiting for transfers between devices  19.2 us (17%)
  Pallas kernels  13.3 us (11%)
  local copies, waits for them, and re-layouts  11.8 us (10%)
  matrix products  4.54 us (4%)
  starting transfers between devices  3.59 us (3%)
  other arithmetic  1.61 us (1%)
    all_to_all x1, blocking collectives, reduce_scatter(): got = lax.all_to_all(pieces, axis, 0, 0)  34.3 us
    all_to_all x1, blocking collectives, body(): got = lax.all_to_all(blocks, ('dp', 'row', 'col'), 0, 0)  26.8 us
    all_to_all x1, waiting for transfers between devices, body(): lax.all_to_all(jnp.broadcast_to(gram_keys[None], (n_dp,) + gram_keys.shap...  19.2 us
    pallas_call x1, Pallas kernels, gram_times_keys(): pl.pallas_call(gram_keys_kernel, grid=(rows // block_rows,), in_specs=[pl...  13.3 us
    all_to_all x1, starting transfers between devices, body(): lax.all_to_all(jnp.broadcast_to(gram_keys[None], (n_dp,) + gram_keys.shap...  3.59 us
    reshape x1, local copies, waits for them, and re-layouts, reduce_scatter(): pieces = x.reshape((parts, x.shape[0] // parts) + x.shape[1:])  3.36 us
    reshape x1, local copies, waits for them, and re-layouts, body(): hidden_acts.reshape(hidden_acts.shape[0], n_dp, hidden_acts.shape[1] // n...  3.34 us
    dot_general x1, matrix products, body(): lax.dot_general(acts, gathered, (((1, 2), (0, 1)), ((), ())), preferred_e...  2.79 us
  transfers between devices with their start and end apart: 1, of which 1 were waited for; matrix products, arithmetic and copies ran while one was open for 3% of the time, Pallas kernels for 0%

profile of v14, /device:TPU:0, one launch (start us, length us, event | category | flops | bytes accessed | tf_op | source)
XLA Modules:
  0.0 115.4 jit_solution(5601176408070050208)
XLA Ops:
  0.0 13.3 %shard_map.82 = bf16[1848,512]{1,0:T(8,128)(2,1)} custom-call(bf16[1848,3696]{1,0:T(8,128)(2,1)} %g_ref.1, bf16[3696,512]{1,0:T(8,128)(2,1)} %k_ref.1), custom_call_target="tpu_custom_call" | custom-call | flops 6994132992 | bytes 19337472 | tf_op jit(solution)/shard_map/pallas_call | solution.py:15
  13.3 3.4 %reshape.20 = bf16[8,231,512]{2,1,0:T(8,128)(2,1)} reshape(bf16[1848,512]{1,0:T(8,128)(2,1)} %shard_map.82) | data formatting | bytes 3784704 | tf_op jit(solution)/shard_map/reshape | solution.py:33
  16.7 34.3 %all_to_all.15 = bf16[8,231,512]{2,1,0:T(8,128)(2,1)S(1)} all-to-all(bf16[8,231,512]{2,1,0:T(8,128)(2,1)} %reshape.20), channel_id=1, replica_groups=mesh['dp'=8,'row'=4,'col'=4] {'dp'}, dimensions={0} | all-to-all | bytes 3784704 | tf_op jit(solution)/shard_map/all_to_all | solution.py:34
  51.0 0.0 copy-start.4
  51.0 0.3 reduce_sum.31
  51.4 0.4 copy-done.4
  51.7 0.4 convolution_convert_fusion
  52.1 1.4 %broadcast_in_dim.31 = bf16[8,231,512]{2,1,0:T(8,128)(2,1)} broadcast(bf16[231,512]{1,0:T(8,128)(2,1)S(1)} %convolution_convert_fusion), dimensions={1,2} | broadcast | bytes 2128896 | tf_op jit(solution)/shard_map/broadcast_in_dim | solution.py:67
  53.5 3.6 %all-to-all-start.1 = ((bf16[8,231,512]{2,1,0:T(8,128)(2,1)}), bf16[8,231,512]{2,1,0:T(8,128)(2,1)S(1)}, u32[]{:S(2)}, u32[]{:S(2)}) async-start(bf16[8,231,512]{2,1,0:T(8,128)(2,1)} %broadcast_in_dim.31), calls=%async_computation.1 | async-start | bytes 3801088 | tf_op jit(solution)/shard_map/all_to_all | solution.py:67
  57.1 0.0 copy-start.1
  57.1 0.0 copy-start.2
  57.1 0.0 copy-start.3
  57.1 3.3 %reshape.21 = bf16[512,8,231]{0,2,1:T(8,128)(2,1)} reshape(bf16[512,1848]{0,1:T(8,128)(2,1)} %param.8) | data formatting | bytes 3784704 | tf_op jit(solution)/shard_map/reshape | solution.py:68
  60.5 0.0 copy-done.1
  60.5 0.0 copy-done.2
  60.5 0.2 select_reduce_fusion
  60.7 0.0 copy-done.3
  60.7 0.0 copy-start
  60.8 19.2 %all-to-all-done.1 = bf16[8,231,512]{2,1,0:T(8,128)(2,1)S(1)} async-done(((bf16[8,231,512]{2,1,0:T(8,128)(2,1)}), bf16[8,231,512]{2,1,0:T(8,128)(2,1)S(1)}, u32[]{:S(2)}, u32[]{:S(2)}) %all-to-all-start.1) | async-done | bytes 1892384 | tf_op jit(solution)/shard_map/all_to_all | solution.py:67
  80.0 2.8 %convolution_bitcast_fusion = f32[512,512]{0,1:T(8,128)S(1)} fusion(bf16[8,231,512]{2,1,0:T(8,128)(2,1)S(1)} %all-to-all-done.1, bf16[512,8,231]{0,2,1:T(8,128)(2,1)} %reshape.21), kind=kOutput, calls=%fused_computation.2 | convolution fusion | flops 968884224 | bytes 4833280 | tf_op jit(solution)/shard_map/dot_general | solution.py:69
  82.8 0.0 copy-done
  82.8 1.4 %fusion = f32[1024,512]{0,1:S(1)} fusion(f32[512,512]{0,1:T(8,128)S(1)} %convolution_bitcast_fusion, bf16[512,1024]{1,0:T(8,128)(2,1)S(1)} %copy-done, f32[512]{0:T(512)S(1)} %select_multiply_fusion), kind=kOutput, calls=%fused_computation.4 | convolution fusion | flops 1612185600 | bytes 4196352
  84.1 0.2 convert_bitcast_fusion
  84.3 1.1 copy.11
  85.4 1.5 %reshape.23 = bf16[128,2,2048]{2,1,0:T(2,128)(2,1)S(1)} reshape(bf16[8,1024,64]{2,1,0:T(8,128)(2,1)S(1)} %copy.11) | data formatting | bytes 2097152 | tf_op jit(solution)/shard_map/reshape | solution.py:80
  86.9 26.8 %all_to_all.16 = bf16[128,2,2048]{2,1,0:T(2,128)(2,1)S(1)} all-to-all(bf16[128,2,2048]{2,1,0:T(2,128)(2,1)S(1)} %reshape.23), channel_id=1, replica_groups=mesh['dp'=8,'row'=4,'col'=4] {'dp','row','col'}, dimensions={0} | all-to-all | bytes 2097152 | tf_op jit(solution)/shard_map/all_to_all | solution.py:81
  113.7 0.9 convert_reduce_fusion
  114.6 0.1 reshape.24
  114.7 0.7 copy.12
  (1 shorter events, 0.0 us)
Async XLA Ops:
  51.0 0.7 copy-start.4
  53.5 26.5 %all-to-all-start.1 = ((bf16[8,231,512]{2,1,0:T(8,128)(2,1)}), bf16[8,231,512]{2,1,0:T(8,128)(2,1)S(1)}, u32[]{:S(2)}, u32[]{:S(2)}) async-start(bf16[8,231,512]{2,1,0:T(8,128)(2,1)} %broadcast_in_dim.31), calls=%async_computation.1 | async-start | bytes 3801088 | tf_op jit(solution)/shard_map/all_to_all | solution.py:67
  57.1 3.4 %copy-start.1 = (f32[512]{0:T(512)S(1)}, f32[512]{0:T(512)}, u32[]{:S(2)}) copy-start(f32[512]{0:T(512)} %param.12) | copy-start | bytes 6148
  57.1 3.4 %copy-start.2 = (s32[512]{0:T(512)S(1)}, s32[512]{0:T(512)}, u32[]{:S(2)}) copy-start(s32[512]{0:T(512)} %param.11) | copy-start | bytes 6148
  57.1 3.6 %copy-start.3 = (s32[512]{0:T(512)S(1)}, s32[512]{0:T(512)}, u32[]{:S(2)}) copy-start(s32[512]{0:T(512)} %param.10) | copy-start | bytes 6148
  60.7 22.0 %copy-start = (bf16[512,1024]{1,0:T(8,128)(2,1)S(1)}, bf16[512,1024]{1,0:T(8,128)(2,1)}, u32[]{:S(2)}) copy-start(bf16[512,1024]{1,0:T(8,128)(2,1)} %param.9) | copy-start | bytes 3145732

commit v15 on v11

--- a/solution.py
+++ b/solution.py
@@ -37,10 +37,11 @@
 
     gram_keys = jnp.dot(inverse_gram, edit_keys, preferred_element_type=jnp.float32)
     gram_keys = reduce_scatter(gram_keys.astype(jnp.bfloat16), "dp", n_dp)
+    acts = hidden_acts.reshape(hidden_acts.shape[0], n_dp, hidden_acts.shape[1] // n_dp)
+    acts, gram_keys = lax.optimization_barrier((acts, gram_keys))
     order = (jnp.arange(edits, dtype=jnp.int32)[:, None] == edit_slots[None, :]).astype(jnp.bfloat16)
     gram_keys = jnp.dot(gram_keys.astype(jnp.bfloat16), order, preferred_element_type=jnp.float32).astype(jnp.bfloat16)
     gathered = lax.all_to_all(jnp.broadcast_to(gram_keys[None], (n_dp,) + gram_keys.shape), "dp", 0, 0)
-    acts = hidden_acts.reshape(hidden_acts.shape[0], n_dp, hidden_acts.shape[1] // n_dp)
     acts_keys = lax.dot_general(acts, gathered, (((1, 2), (0, 1)), ((), ())), preferred_element_type=jnp.float32)
     slots = acts_keys.shape[1]
     cols = scaled.shape[1]

time: 112 us -> 113 us (level)
  blocking collectives: 61.3 us -> 26.8 us
  waiting for transfers between devices: 19.2 us -> 45.2 us
  starting transfers between devices: 3.59 us -> 12.8 us
    all_to_all x1 -> x0, blocking collectives: 34.5 us -> none  [reduce_scatter(): got = lax.all_to_all(pieces, axis, 0, 0)]
    all_to_all x0 -> x1, waiting for transfers between devices: none -> 20.9 us  [reduce_scatter(): got = lax.all_to_all(pieces, axis, 0, 0)]
    all_to_all x0 -> x1, starting transfers between devices: none -> 7.89 us  [reduce_scatter(): got = lax.all_to_all(pieces, axis, 0, 0)]
    all_to_all x1, waiting for transfers between devices: 19.2 us -> 24.3 us  [body(): lax.all_to_all(jnp.broadcast_to(gram_keys[None], (n_dp,) + gram_keys.shap...]
    all_to_all x1, starting transfers between devices: 3.59 us -> 4.9 us  [body(): lax.all_to_all(jnp.broadcast_to(gram_keys[None], (n_dp,) + gram_keys.shap...]
  transfers between devices with their start and end apart: 1 -> 2, of which waited for: 1 -> 2; matrix products, arithmetic and copies ran while one was open for 3% -> 3% of each run, Pallas kernels for 0% -> 0%
where the time goes in v15:
time: 113 us
  waiting for transfers between devices  45.2 us (40%)
  blocking collectives  26.8 us (24%)
  matrix products  16.3 us (14%)
  starting transfers between devices  12.8 us (11%)
  local copies, waits for them, and re-layouts  9.96 us (9%)
  other arithmetic  1.54 us (1%)
    all_to_all x1, blocking collectives, body(): got = lax.all_to_all(blocks, ('dp', 'row', 'col'), 0, 0)  26.8 us
    all_to_all x1, waiting for transfers between devices, body(): lax.all_to_all(jnp.broadcast_to(gram_keys[None], (n_dp,) + gram_keys.shap...  24.3 us
    all_to_all x1, waiting for transfers between devices, reduce_scatter(): got = lax.all_to_all(pieces, axis, 0, 0)  20.9 us
    dot_general x1, matrix products, body(): jnp.dot(inverse_gram, edit_keys, preferred_element_type=jnp.float32)  11.7 us
    all_to_all x1, starting transfers between devices, reduce_scatter(): got = lax.all_to_all(pieces, axis, 0, 0)  7.89 us
    all_to_all x1, starting transfers between devices, body(): lax.all_to_all(jnp.broadcast_to(gram_keys[None], (n_dp,) + gram_keys.shap...  4.9 us
    reshape x1, local copies, waits for them, and re-layouts, body(): hidden_acts.reshape(hidden_acts.shape[0], n_dp, hidden_acts.shape[1] // n...  3.36 us
    dot_general x1, matrix products, body(): lax.dot_general(acts, gathered, (((1, 2), (0, 1)), ((), ())), preferred_e...  2.81 us
  transfers between devices with their start and end apart: 2, of which 2 were waited for; matrix products, arithmetic and copies ran while one was open for 3% of the time, Pallas kernels for 0%

profile of v15, /device:TPU:0, one launch (start us, length us, event | category | flops | bytes accessed | tf_op | source)
XLA Modules:
  0.0 112.8 jit_solution(1983191173967227951)
XLA Ops:
  0.0 11.7 %convolution_convert_fusion = bf16[1848,512]{1,0:T(8,128)(2,1)S(1)} fusion(bf16[1848,3696]{1,0:T(8,128)(2,1)} %param.13, bf16[3696,512]{1,0:T(8,128)(2,1)} %param.14), kind=kOutput, calls=%fused_computation.1 | convolution fusion | flops 6995079168 | bytes 19337472 | tf_op jit(solution)/shard_map/dot_general | solution.py:38
  11.7 1.8 %reshape.21 = bf16[8,231,512]{2,1,0:T(8,128)(2,1)} reshape(bf16[1848,512]{1,0:T(8,128)(2,1)S(1)} %convolution_convert_fusion) | data formatting | bytes 3784704 | tf_op jit(solution)/shard_map/reshape | solution.py:8
  13.5 7.9 %all-to-all-start = ((bf16[8,231,512]{2,1,0:T(8,128)(2,1)}), bf16[8,231,512]{2,1,0:T(8,128)(2,1)S(1)}, u32[]{:S(2)}, u32[]{:S(2)}) async-start(bf16[8,231,512]{2,1,0:T(8,128)(2,1)} %reshape.21), calls=%async_computation | async-start | bytes 3801088 | tf_op jit(solution)/shard_map/all_to_all | solution.py:9
  21.4 0.0 copy-start.5
  21.4 3.4 %reshape.20 = bf16[512,8,231]{0,2,1:T(8,128)(2,1)} reshape(bf16[512,1848]{0,1:T(8,128)(2,1)} %param.8) | data formatting | bytes 3784704 | tf_op jit(solution)/shard_map/reshape | solution.py:40
  24.8 20.9 %all-to-all-done = bf16[8,231,512]{2,1,0:T(8,128)(2,1)S(1)} async-done(((bf16[8,231,512]{2,1,0:T(8,128)(2,1)}), bf16[8,231,512]{2,1,0:T(8,128)(2,1)S(1)}, u32[]{:S(2)}, u32[]{:S(2)}) %all-to-all-start) | async-done | bytes 1892384 | tf_op jit(solution)/shard_map/all_to_all | solution.py:9
  45.7 0.3 convert_reduce_fusion
  46.0 0.0 copy-done.5
  46.0 0.4 convolution_convert_fusion.1
  46.4 1.4 %broadcast_in_dim.31 = bf16[8,231,512]{2,1,0:T(8,128)(2,1)} broadcast(bf16[231,512]{1,0:T(8,128)(2,1)S(1)} %convolution_convert_fusion.1), dimensions={1,2} | broadcast | bytes 2128896 | tf_op jit(solution)/shard_map/broadcast_in_dim | solution.py:44
  47.8 0.0 copy-start.2
  47.8 0.0 copy-start.3
  47.8 0.0 copy-start.4
  47.8 0.0 copy-start
  47.8 4.9 %all-to-all-start.1 = ((bf16[8,231,512]{2,1,0:T(8,128)(2,1)}), bf16[8,231,512]{2,1,0:T(8,128)(2,1)}, u32[]{:S(2)}, u32[]{:S(2)}) async-start(bf16[8,231,512]{2,1,0:T(8,128)(2,1)} %broadcast_in_dim.31), calls=%async_computation.1 | async-start | bytes 3801088 | tf_op jit(solution)/shard_map/all_to_all | solution.py:44
  52.7 0.0 copy-done.2
  52.7 0.0 copy-done.3
  52.7 0.2 select_reduce_fusion
  53.0 0.0 copy-done.4
  53.0 0.0 copy-start.1
  53.0 24.3 %all-to-all-done.1 = bf16[8,231,512]{2,1,0:T(8,128)(2,1)} async-done(((bf16[8,231,512]{2,1,0:T(8,128)(2,1)}), bf16[8,231,512]{2,1,0:T(8,128)(2,1)}, u32[]{:S(2)}, u32[]{:S(2)}) %all-to-all-start.1) | async-done | bytes 1892384 | tf_op jit(solution)/shard_map/all_to_all | solution.py:44
  77.3 0.0 copy-done
  77.3 2.8 %convolution_bitcast_fusion = f32[512,512]{0,1:T(8,128)S(1)} fusion(bf16[512,8,231]{0,2,1:T(8,128)(2,1)S(1)} %copy-done, bf16[8,231,512]{2,1,0:T(8,128)(2,1)} %all-to-all-done.1), kind=kOutput, calls=%fused_computation.4 | convolution fusion | flops 968884224 | bytes 4833280 | tf_op jit(solution)/shard_map/dot_general | solution.py:45
  80.1 0.0 copy-done.1
  80.1 1.4 %fusion = f32[1024,512]{0,1:S(1)} fusion(f32[512,512]{0,1:T(8,128)S(1)} %convolution_bitcast_fusion, bf16[512,1024]{1,0:T(8,128)(2,1)S(1)} %copy-done.1, f32[512]{0:T(512)S(1)} %select_multiply_fusion), kind=kOutput, calls=%fused_computation.6 | convolution fusion | flops 1612185600 | bytes 4196352
  81.5 0.2 convert_bitcast_fusion
  81.7 1.1 copy.11
  82.8 1.5 %reshape.23 = bf16[128,2,2048]{2,1,0:T(2,128)(2,1)S(1)} reshape(bf16[8,1024,64]{2,1,0:T(8,128)(2,1)S(1)} %copy.11) | data formatting | bytes 2097152 | tf_op jit(solution)/shard_map/reshape | solution.py:56
  84.3 26.8 %all_to_all.15 = bf16[128,2,2048]{2,1,0:T(2,128)(2,1)S(1)} all-to-all(bf16[128,2,2048]{2,1,0:T(2,128)(2,1)S(1)} %reshape.23), channel_id=1, replica_groups=mesh['dp'=8,'row'=4,'col'=4] {'dp','row','col'}, dimensions={0} | all-to-all | bytes 2097152 | tf_op jit(solution)/shard_map/all_to_all | solution.py:57
  111.1 0.9 convert_reduce_fusion.1
  112.0 0.1 reshape.24
  112.1 0.7 copy.12
  (1 shorter events, 0.0 us)
Async XLA Ops:
  13.5 32.2 %all-to-all-start = ((bf16[8,231,512]{2,1,0:T(8,128)(2,1)}), bf16[8,231,512]{2,1,0:T(8,128)(2,1)S(1)}, u32[]{:S(2)}, u32[]{:S(2)}) async-start(bf16[8,231,512]{2,1,0:T(8,128)(2,1)} %reshape.21), calls=%async_computation | async-start | bytes 3801088 | tf_op jit(solution)/shard_map/all_to_all | solution.py:9
  21.4 24.6 %copy-start.5 = (s32[512]{0:T(512)S(1)}, s32[512]{0:T(512)}, u32[]{:S(2)}) copy-start(s32[512]{0:T(512)} %param.15) | copy-start | bytes 6148
  47.8 4.9 %copy-start.2 = (f32[512]{0:T(512)S(1)}, f32[512]{0:T(512)}, u32[]{:S(2)}) copy-start(f32[512]{0:T(512)} %param.12) | copy-start | bytes 6148
  47.8 4.9 %copy-start.3 = (s32[512]{0:T(512)S(1)}, s32[512]{0:T(512)}, u32[]{:S(2)}) copy-start(s32[512]{0:T(512)} %param.11) | copy-start | bytes 6148
  47.8 5.2 %copy-start.4 = (s32[512]{0:T(512)S(1)}, s32[512]{0:T(512)}, u32[]{:S(2)}) copy-start(s32[512]{0:T(512)} %param.10) | copy-start | bytes 6148
  47.8 29.5 %copy-start = (bf16[512,8,231]{0,2,1:T(8,128)(2,1)S(1)}, bf16[512,8,231]{0,2,1:T(8,128)(2,1)}, u32[]{:S(2)}) copy-start(bf16[512,8,231]{0,2,1:T(8,128)(2,1)} %reshape.20) | copy-start | bytes 5677060
  47.8 29.5 %all-to-all-start.1 = ((bf16[8,231,512]{2,1,0:T(8,128)(2,1)}), bf16[8,231,512]{2,1,0:T(8,128)(2,1)}, u32[]{:S(2)}, u32[]{:S(2)}) async-start(bf16[8,231,512]{2,1,0:T(8,128)(2,1)} %broadcast_in_dim.31), calls=%async_computation.1 | async-start | bytes 3801088 | tf_op jit(solution)/shard_map/all_to_all | solution.py:44
  53.0 27.1 %copy-start.1 = (bf16[512,1024]{1,0:T(8,128)(2,1)S(1)}, bf16[512,1024]{1,0:T(8,128)(2,1)}, u32[]{:S(2)}) copy-start(bf16[512,1024]{1,0:T(8,128)(2,1)} %param.9) | copy-start | bytes 3145732

commit v16 on v13

--- a/solution.py
+++ b/solution.py
@@ -41,15 +41,13 @@
     gram_keys = jnp.dot(gram_keys.astype(jnp.bfloat16), order, preferred_element_type=jnp.float32).astype(jnp.bfloat16)
     gathered = lax.all_to_all(jnp.broadcast_to(gram_keys[None], (n_dp,) + gram_keys.shape), "dp", 0, 0)
     acts = hidden_acts.reshape(hidden_acts.shape[0], n_dp, hidden_acts.shape[1] // n_dp)
-    acts_keys = lax.dot_general(acts, gathered, (((1, 2), (0, 1)), ((), ())), preferred_element_type=jnp.float32)
-    slots = acts_keys.shape[1]
+    grad_part = lax.dot_general(scaled, acts, (((0,), (0,)), ((), ())), preferred_element_type=jnp.float32)
+    partial = lax.dot_general(
+        grad_part.astype(jnp.bfloat16), gathered, (((1, 2), (0, 1)), ((), ())), preferred_element_type=jnp.float32
+    )
+    slots = partial.shape[1]
     cols = scaled.shape[1]
-    partial = lax.dot_general(
-        scaled,
-        acts_keys.astype(jnp.bfloat16).reshape(acts_keys.shape[0], n_dp, slots // n_dp),
-        (((0,), (0,)), ((), ())),
-        preferred_element_type=jnp.float32,
-    )
+    partial = partial.reshape(cols, n_dp, slots // n_dp)
     blocks = partial.astype(jnp.bfloat16).transpose(1, 0, 2)
     blocks = blocks.reshape(n_dp * n_rc, 2, (cols // n_rc) * (slots // n_dp) // 2)
     got = lax.all_to_all(blocks, ("dp", "row", "col"), 0, 0)

time: 113 us -> 114 us (level)
  matrix products: 16 us -> 18.3 us
  waiting for transfers between devices: 20.8 us -> 19.2 us
  local copies, waits for them, and re-layouts: 8.45 us -> 9.97 us
    dot_general x0 -> x1, matrix products: none -> 6.24 us  [body(): lax.dot_general(grad_part.astype(jnp.bfloat16), gathered, (((1, 2), (0, 1...]
    unnamed x1 -> x0, matrix products: 3.93 us -> none
    all_to_all x1, waiting for transfers between devices: 20.8 us -> 19.2 us  [body(): lax.all_to_all(jnp.broadcast_to(gram_keys[None], (n_dp,) + gram_keys.shap...]
    reshape x1, local copies, waits for them, and re-layouts: 1.85 us -> 3.34 us  [body(): hidden_acts.reshape(hidden_acts.shape[0], n_dp, hidden_acts.shape[1] // n...]
  transfers between devices with their start and end apart: 1 -> 1, of which waited for: 1 -> 1; matrix products, arithmetic and copies ran while one was open for 2% -> 3% of each run, Pallas kernels for 0% -> 0%
where the time goes in v16:
time: 114 us
  blocking collectives  61.3 us (54%)
  waiting for transfers between devices  19.2 us (17%)
  matrix products  18.3 us (16%)
  local copies, waits for them, and re-layouts  9.97 us (9%)
  starting transfers between devices  3.59 us (3%)
  other arithmetic  1.46 us (1%)
    all_to_all x1, blocking collectives, reduce_scatter(): got = lax.all_to_all(pieces, axis, 0, 0)  34.5 us
    all_to_all x1, blocking collectives, body(): got = lax.all_to_all(blocks, ('dp', 'row', 'col'), 0, 0)  26.8 us
    all_to_all x1, waiting for transfers between devices, body(): lax.all_to_all(jnp.broadcast_to(gram_keys[None], (n_dp,) + gram_keys.shap...  19.2 us
    dot_general x1, matrix products, body(): jnp.dot(inverse_gram, edit_keys, preferred_element_type=jnp.float32)  11.7 us
    dot_general x1, matrix products, body(): lax.dot_general(grad_part.astype(jnp.bfloat16), gathered, (((1, 2), (0, 1...  6.24 us
    all_to_all x1, starting transfers between devices, body(): lax.all_to_all(jnp.broadcast_to(gram_keys[None], (n_dp,) + gram_keys.shap...  3.59 us
    reshape x1, local copies, waits for them, and re-layouts, body(): hidden_acts.reshape(hidden_acts.shape[0], n_dp, hidden_acts.shape[1] // n...  3.34 us
  transfers between devices with their start and end apart: 1, of which 1 were waited for; matrix products, arithmetic and copies ran while one was open for 3% of the time, Pallas kernels for 0%

profile of v16, /device:TPU:0, one launch (start us, length us, event | category | flops | bytes accessed | tf_op | source)
XLA Modules:
  0.0 114.0 jit_solution(529910630527917710)
XLA Ops:
  0.0 11.7 %convolution_convert_fusion = bf16[1848,512]{1,0:T(8,128)(2,1)S(1)} fusion(bf16[1848,3696]{1,0:T(8,128)(2,1)} %param.13, bf16[3696,512]{1,0:T(8,128)(2,1)} %param.14), kind=kOutput, calls=%fused_computation.2 | convolution fusion | flops 6995079168 | bytes 19337472 | tf_op jit(solution)/shard_map/dot_general | solution.py:38
  11.7 1.8 %reshape.20 = bf16[8,231,512]{2,1,0:T(8,128)(2,1)} reshape(bf16[1848,512]{1,0:T(8,128)(2,1)S(1)} %convolution_convert_fusion) | data formatting | bytes 3784704 | tf_op jit(solution)/shard_map/reshape | solution.py:8
  13.6 0.0 copy-start.3
  13.6 34.5 %all_to_all.15 = bf16[8,231,512]{2,1,0:T(8,128)(2,1)S(1)} all-to-all(bf16[8,231,512]{2,1,0:T(8,128)(2,1)} %reshape.20), channel_id=1, replica_groups=mesh['dp'=8,'row'=4,'col'=4] {'dp'}, dimensions={0} | all-to-all | bytes 3784704 | tf_op jit(solution)/shard_map/all_to_all | solution.py:9
  48.0 0.3 reduce_sum.31
  48.4 0.0 copy-done.3
  48.4 0.4 convolution_convert_fusion.1
  48.8 1.4 %broadcast_in_dim.31 = bf16[8,231,512]{2,1,0:T(8,128)(2,1)} broadcast(bf16[231,512]{1,0:T(8,128)(2,1)S(1)} %convolution_convert_fusion.1), dimensions={1,2} | broadcast | bytes 2128896 | tf_op jit(solution)/shard_map/broadcast_in_dim | solution.py:42
  50.2 3.6 %all-to-all-start.1 = ((bf16[8,231,512]{2,1,0:T(8,128)(2,1)}), bf16[8,231,512]{2,1,0:T(8,128)(2,1)S(1)}, u32[]{:S(2)}, u32[]{:S(2)}) async-start(bf16[8,231,512]{2,1,0:T(8,128)(2,1)} %broadcast_in_dim.31), calls=%async_computation.1 | async-start | bytes 3801088 | tf_op jit(solution)/shard_map/all_to_all | solution.py:42
  53.8 0.0 copy-start
  53.8 0.0 copy-start.1
  53.8 0.0 copy-start.2
  53.8 3.3 %reshape.19 = bf16[512,8,231]{0,2,1:T(8,128)(2,1)} reshape(bf16[512,1848]{0,1:T(8,128)(2,1)} %param.8) | data formatting | bytes 3784704 | tf_op jit(solution)/shard_map/reshape | solution.py:43
  57.1 0.0 copy-done
  57.1 0.0 copy-done.1
  57.1 0.2 select_reduce_fusion
  57.4 0.0 copy-done.2
  57.4 19.2 %all-to-all-done.1 = bf16[8,231,512]{2,1,0:T(8,128)(2,1)S(1)} async-done(((bf16[8,231,512]{2,1,0:T(8,128)(2,1)}), bf16[8,231,512]{2,1,0:T(8,128)(2,1)S(1)}, u32[]{:S(2)}, u32[]{:S(2)}) %all-to-all-start.1) | async-done | bytes 1892384 | tf_op jit(solution)/shard_map/all_to_all | solution.py:42
  76.6 6.2 %bitcast_convert_fusion = bf16[1024,512]{0,1:T(8,128)(2,1)S(1)} fusion(bf16[8,231,512]{2,1,0:T(8,128)(2,1)S(1)} %all-to-all-done.1, bf16[512,8,231]{0,2,1:T(8,128)(2,1)} %reshape.19, bf16[512,1024]{1,0:T(8,128)(2,1)} %param.9, f32[512]{0:T(512)S(1)} %select_multiply_fusion), kind=kOutput, calls=%fused_computation.3 | convolution fusion | flops 3879526400 | bytes 5883904 | tf_op jit(solution)/shard_map/dot_general | solution.py:45
  82.9 1.1 copy.11
  84.0 1.5 %reshape.21 = bf16[128,2,2048]{2,1,0:T(2,128)(2,1)S(1)} reshape(bf16[8,1024,64]{2,1,0:T(8,128)(2,1)S(1)} %bitcast.16) | data formatting | bytes 2097152 | tf_op jit(solution)/shard_map/reshape | solution.py:52
  85.5 26.8 %all_to_all.16 = bf16[128,2,2048]{2,1,0:T(2,128)(2,1)S(1)} all-to-all(bf16[128,2,2048]{2,1,0:T(2,128)(2,1)S(1)} %reshape.21), channel_id=1, replica_groups=mesh['dp'=8,'row'=4,'col'=4] {'dp','row','col'}, dimensions={0} | all-to-all | bytes 2097152 | tf_op jit(solution)/shard_map/all_to_all | solution.py:53
  112.3 0.9 convert_reduce_fusion
  113.2 0.1 reshape.22
  113.3 0.7 copy.12
  (1 shorter events, 0.0 us)
Async XLA Ops:
  13.6 34.8 %copy-start.3 = (s32[512]{0:T(512)S(1)}, s32[512]{0:T(512)}, u32[]{:S(2)}) copy-start(s32[512]{0:T(512)} %param.15) | copy-start | bytes 6148
  50.2 26.5 %all-to-all-start.1 = ((bf16[8,231,512]{2,1,0:T(8,128)(2,1)}), bf16[8,231,512]{2,1,0:T(8,128)(2,1)S(1)}, u32[]{:S(2)}, u32[]{:S(2)}) async-start(bf16[8,231,512]{2,1,0:T(8,128)(2,1)} %broadcast_in_dim.31), calls=%async_computation.1 | async-start | bytes 3801088 | tf_op jit(solution)/shard_map/all_to_all | solution.py:42
  53.8 3.4 %copy-start = (f32[512]{0:T(512)S(1)}, f32[512]{0:T(512)}, u32[]{:S(2)}) copy-start(f32[512]{0:T(512)} %param.12) | copy-start | bytes 6148
  53.8 3.4 %copy-start.1 = (s32[512]{0:T(512)S(1)}, s32[512]{0:T(512)}, u32[]{:S(2)}) copy-start(s32[512]{0:T(512)} %param.11) | copy-start | bytes 6148
  53.8 3.6 %copy-start.2 = (s32[512]{0:T(512)S(1)}, s32[512]{0:T(512)}, u32[]{:S(2)}) copy-start(s32[512]{0:T(512)} %param.10) | copy-start | bytes 6148

commit v17 on v9

--- a/solution.py
+++ b/solution.py
@@ -37,10 +37,11 @@
 
     gram_keys = jnp.dot(inverse_gram, edit_keys, preferred_element_type=jnp.float32)
     gram_keys = reduce_scatter(gram_keys.astype(jnp.bfloat16), "dp", n_dp)
-    gram_keys = all_gather(gram_keys.astype(jnp.bfloat16), "dp", n_dp)
     order = (jnp.arange(edits, dtype=jnp.int32)[:, None] == edit_slots[None, :]).astype(jnp.bfloat16)
-    gram_keys = jnp.dot(gram_keys, order, preferred_element_type=jnp.float32).astype(jnp.bfloat16)
-    acts_keys = jnp.dot(hidden_acts, gram_keys, preferred_element_type=jnp.float32)
+    gram_keys = jnp.dot(gram_keys.astype(jnp.bfloat16), order, preferred_element_type=jnp.float32).astype(jnp.bfloat16)
+    gathered = lax.all_to_all(jnp.broadcast_to(gram_keys[None], (n_dp,) + gram_keys.shape), "dp", 0, 0)
+    acts = hidden_acts.reshape(hidden_acts.shape[0], n_dp, hidden_acts.shape[1] // n_dp)
+    acts_keys = lax.dot_general(acts, gathered, (((1, 2), (0, 1)), ((), ())), preferred_element_type=jnp.float32)
     slots = acts_keys.shape[1]
     cols = scaled.shape[1]
     partial = lax.dot_general(

time: 126 us -> 110 us (0.87)
  local copies, waits for them, and re-layouts: 14.6 us -> 9.96 us
  matrix products: 20.3 us -> 16.3 us
  waiting for transfers between devices: 24.6 us -> 21.1 us
  other arithmetic: 5.29 us -> 2.36 us
    all_to_all x1, waiting for transfers between devices: 22.6 us -> 19.2 us  [body(): lax.all_to_all(jnp.broadcast_to(gram_keys[None], (n_dp,) + gram_keys.shap...]
    another operation x1, local copies, waits for them, and re-layouts: 3.92 us -> 1.5 us  [body(): split = blocks.reshape((n_dp, n_row // 2, 2, n_col) + blocks.shape[1:])]
    dot_general x1 -> x2, matrix products: 4.89 us -> 3.17 us  [the longest x1 2.79 us: body(): lax.dot_general(acts, gathered, (((1, 2), (0, 1)), ((), ())), preferred_e...]
    reduce_sum x1, other arithmetic: 1.85 us -> 0.33 us  [reduce_scatter(): return jnp.sum(got.astype(jnp.float32), axis=0)]
    reshape x1, local copies, waits for them, and re-layouts: 3.36 us -> 1.84 us  [reduce_scatter(): pieces = x.reshape((parts, x.shape[0] // parts) + x.shape[1:])]
    convert_element_type x1, other arithmetic: 2.13 us -> 0.72 us  [body(): (mine.astype(jnp.float32) + other.astype(jnp.float32)).astype(jnp.bfloat16)]
  transfers between devices with their start and end apart: 2 -> 2, of which waited for: 2 -> 2; matrix products, arithmetic and copies ran while one was open for 0% -> 3% of each run, Pallas kernels for 0% -> 0%
where the time goes in v17:
time: 110 us
  blocking collectives  56.2 us (51%)
  waiting for transfers between devices  21.1 us (19%)
  matrix products  16.3 us (15%)
  local copies, waits for them, and re-layouts  9.96 us (9%)
  starting transfers between devices  3.68 us (3%)
  other arithmetic  2.36 us (2%)
    all_to_all x1, blocking collectives, reduce_scatter(): got = lax.all_to_all(pieces, axis, 0, 0)  34.5 us
    all_to_all x1, blocking collectives, body(): lax.all_to_all(summed, ('dp', 'row', 'col'), 0, 0, axis_index_groups=groups)  21.8 us
    all_to_all x1, waiting for transfers between devices, body(): lax.all_to_all(jnp.broadcast_to(gram_keys[None], (n_dp,) + gram_keys.shap...  19.2 us
    dot_general x1, matrix products, body(): jnp.dot(inverse_gram, edit_keys, preferred_element_type=jnp.float32)  11.7 us
    all_to_all x1, starting transfers between devices, body(): lax.all_to_all(jnp.broadcast_to(gram_keys[None], (n_dp,) + gram_keys.shap...  3.59 us
    reshape x1, local copies, waits for them, and re-layouts, body(): hidden_acts.reshape(hidden_acts.shape[0], n_dp, hidden_acts.shape[1] // n...  3.33 us
    dot_general x1, matrix products, body(): lax.dot_general(acts, gathered, (((1, 2), (0, 1)), ((), ())), preferred_e...  2.79 us
  transfers between devices with their start and end apart: 2, of which 2 were waited for; matrix products, arithmetic and copies ran while one was open for 3% of the time, Pallas kernels for 0%

profile of v17, /device:TPU:0, one launch (start us, length us, event | category | flops | bytes accessed | tf_op | source)
XLA Modules:
  0.0 109.8 jit_solution(2638362730683713269)
XLA Ops:
  0.0 11.7 %convolution_convert_fusion = bf16[1848,512]{1,0:T(8,128)(2,1)S(1)} fusion(bf16[1848,3696]{1,0:T(8,128)(2,1)} %param.15, bf16[3696,512]{1,0:T(8,128)(2,1)} %param.16), kind=kOutput, calls=%fused_computation | convolution fusion | flops 6995079168 | bytes 19337472 | tf_op jit(solution)/shard_map/dot_general | solution.py:38
  11.7 1.8 %reshape.21 = bf16[8,231,512]{2,1,0:T(8,128)(2,1)} reshape(bf16[1848,512]{1,0:T(8,128)(2,1)S(1)} %convolution_convert_fusion) | data formatting | bytes 3784704 | tf_op jit(solution)/shard_map/reshape | solution.py:8
  13.6 0.0 copy-start.4
  13.6 34.5 %all_to_all.15 = bf16[8,231,512]{2,1,0:T(8,128)(2,1)S(1)} all-to-all(bf16[8,231,512]{2,1,0:T(8,128)(2,1)} %reshape.21), channel_id=1, replica_groups=mesh['dp'=8,'row'=4,'col'=4] {'dp'}, dimensions={0} | all-to-all | bytes 3784704 | tf_op jit(solution)/shard_map/all_to_all | solution.py:9
  48.0 0.3 reduce_sum.31
  48.4 0.0 copy-done.4
  48.4 0.4 convolution_convert_fusion.1
  48.8 1.4 %broadcast_in_dim.40 = bf16[8,231,512]{2,1,0:T(8,128)(2,1)} broadcast(bf16[231,512]{1,0:T(8,128)(2,1)S(1)} %convolution_convert_fusion.1), dimensions={1,2} | broadcast | bytes 2128896 | tf_op jit(solution)/shard_map/broadcast_in_dim | solution.py:42
  50.2 3.6 %all-to-all-start.1 = ((bf16[8,231,512]{2,1,0:T(8,128)(2,1)}), bf16[8,231,512]{2,1,0:T(8,128)(2,1)S(1)}, u32[]{:S(2)}, u32[]{:S(2)}) async-start(bf16[8,231,512]{2,1,0:T(8,128)(2,1)} %broadcast_in_dim.40), calls=%async_computation.1 | async-start | bytes 3801088 | tf_op jit(solution)/shard_map/all_to_all | solution.py:42
  53.8 0.0 copy-start.1
  53.8 0.0 copy-start.2
  53.8 0.0 copy-start.3
  53.8 3.3 %reshape.22 = bf16[512,8,231]{0,2,1:T(8,128)(2,1)} reshape(bf16[512,1848]{0,1:T(8,128)(2,1)} %param.10) | data formatting | bytes 3784704 | tf_op jit(solution)/shard_map/reshape | solution.py:43
  57.2 0.0 copy-done.1
  57.2 0.0 copy-done.2
  57.2 0.2 select_reduce_fusion
  57.4 0.0 copy-done.3
  57.4 0.0 copy-start
  57.4 19.2 %all-to-all-done.1 = bf16[8,231,512]{2,1,0:T(8,128)(2,1)S(1)} async-done(((bf16[8,231,512]{2,1,0:T(8,128)(2,1)}), bf16[8,231,512]{2,1,0:T(8,128)(2,1)S(1)}, u32[]{:S(2)}, u32[]{:S(2)}) %all-to-all-start.1) | async-done | bytes 1892384 | tf_op jit(solution)/shard_map/all_to_all | solution.py:42
  76.6 2.8 %convolution_bitcast_fusion = f32[512,512]{0,1:T(8,128)S(1)} fusion(bf16[8,231,512]{2,1,0:T(8,128)(2,1)S(1)} %all-to-all-done.1, bf16[512,8,231]{0,2,1:T(8,128)(2,1)} %reshape.22), kind=kOutput, calls=%fused_computation.2 | convolution fusion | flops 968884224 | bytes 4833280 | tf_op jit(solution)/shard_map/dot_general | solution.py:44
  79.4 0.0 copy-done
  79.4 1.4 %fusion = f32[1024,512]{0,1:S(1)} fusion(f32[512,512]{0,1:T(8,128)S(1)} %convolution_bitcast_fusion, bf16[512,1024]{1,0:T(8,128)(2,1)S(1)} %copy-done, f32[512]{0:T(512)S(1)} %select_multiply_fusion), kind=kOutput, calls=%fused_computation.4 | convolution fusion | flops 1612185600 | bytes 4196352
  80.8 0.2 convert_bitcast_fusion
  81.0 1.1 copy.13
  82.1 1.5 %reshape_reshape.3 = bf16[8,2,2,4,2,2048]{5,4,3,2,1,0:T(2,128)(2,1)S(1)} reshape(bf16[8,1024,64]{2,1,0:T(8,128)(2,1)S(1)} %copy.13) | data formatting | bytes 2097152 | tf_op jit(solution)/shard_map/reshape;reshape | solution.py:58
  83.6 0.5 fusion.3
  84.0 0.1 collective-permute-start
  84.1 1.9 %collective-permute-done = bf16[8,2,4,2,2048]{4,3,2,1,0:T(2,128)(2,1)S(1)} collective-permute-done((bf16[8,2,4,2,2048]{4,3,2,1,0:T(2,128)(2,1)S(1)}, bf16[8,2,4,2,2048]{4,3,2,1,0:T(2,128)(2,1)S(1)}, u32[]{:S(2)}, u32[]{:S(2)}) %collective-permute-start) | collective-permute-done | bytes 524320 | tf_op jit(solution)/shard_map/ppermute | solution.py:61
  86.0 0.7 add_convert_fusion
  86.7 21.8 %all_to_all.16 = bf16[64,2,2048]{2,1,0:T(2,128)(2,1)S(1)} all-to-all(bf16[64,2,2048]{2,1,0:T(2,128)(2,1)S(1)} %bitcast.30), channel_id=1, replica_groups={{0,1,2,3,8,9,10,11,16,17,18,19,24,25,26,27,32,33,34,35,40,41,42,43,48,4..., dimensions={0} | all-to-all | bytes 1048576 | tf_op jit(solution)/shard_map/all_to_all | solution.py:65
  108.5 0.4 convert_reduce_fusion
  109.0 0.1 reshape.25
  109.1 0.7 copy.15
  (1 shorter events, 0.0 us)
Async XLA Ops:
  13.6 34.8 %copy-start.4 = (s32[512]{0:T(512)S(1)}, s32[512]{0:T(512)}, u32[]{:S(2)}) copy-start(s32[512]{0:T(512)} %param.17) | copy-start | bytes 6148
  50.2 26.5 %all-to-all-start.1 = ((bf16[8,231,512]{2,1,0:T(8,128)(2,1)}), bf16[8,231,512]{2,1,0:T(8,128)(2,1)S(1)}, u32[]{:S(2)}, u32[]{:S(2)}) async-start(bf16[8,231,512]{2,1,0:T(8,128)(2,1)} %broadcast_in_dim.40), calls=%async_computation.1 | async-start | bytes 3801088 | tf_op jit(solution)/shard_map/all_to_all | solution.py:42
  53.8 3.4 %copy-start.1 = (f32[512]{0:T(512)S(1)}, f32[512]{0:T(512)}, u32[]{:S(2)}) copy-start(f32[512]{0:T(512)} %param.14) | copy-start | bytes 6148
  53.8 3.4 %copy-start.2 = (s32[512]{0:T(512)S(1)}, s32[512]{0:T(512)}, u32[]{:S(2)}) copy-start(s32[512]{0:T(512)} %param.13) | copy-start | bytes 6148
  53.8 3.6 %copy-start.3 = (s32[512]{0:T(512)S(1)}, s32[512]{0:T(512)}, u32[]{:S(2)}) copy-start(s32[512]{0:T(512)} %param.12) | copy-start | bytes 6148
  57.4 22.0 %copy-start = (bf16[512,1024]{1,0:T(8,128)(2,1)S(1)}, bf16[512,1024]{1,0:T(8,128)(2,1)}, u32[]{:S(2)}) copy-start(bf16[512,1024]{1,0:T(8,128)(2,1)} %param.11) | copy-start | bytes 3145732
  84.0 2.0 %collective-permute-start = (bf16[8,2,4,2,2048]{4,3,2,1,0:T(2,128)(2,1)S(1)}, bf16[8,2,4,2,2048]{4,3,2,1,0:T(2,128)(2,1)S(1)}, u32[]{:S(2)}, u32[]{:S(2)}) collective-permute-start(bf16[8,2,4,2,2048]{4,3,2,1,0:T(2,128)(2,1)S(1)} %fusion.3), channel_id=1, source_target_pairs={{0,4},{4,0},{8,12},{12,8},{1,5},{5,1},{9,13},{13,9},{2,6},{6,2},{1... | collective-permute-start | bytes 1572872 | tf_op jit(solution)/shard_map/ppermute | solution.py:61

commit v18 on v17

--- a/solution.py
+++ b/solution.py
@@ -60,8 +60,13 @@
     other = jnp.take(split, 1 - core, axis=2)
     other = lax.ppermute(other, "row", [(r, r ^ 1) for r in range(n_row)])
     summed = (mine.astype(jnp.float32) + other.astype(jnp.float32)).astype(jnp.bfloat16)
-    summed = summed.reshape((n_dp * n_rc // 2,) + blocks.shape[1:])
-    groups = [[m for m in range(n_dp * n_rc) if (m // n_col) % 2 == c] for c in range(2)]
+    x_lo = lax.axis_index("row") // 2
+    mine = jnp.take(summed, x_lo, axis=1)
+    other = jnp.take(summed, 1 - x_lo, axis=1)
+    other = lax.ppermute(other, "row", [(r, r ^ 2) for r in range(n_row)])
+    summed = (mine.astype(jnp.float32) + other.astype(jnp.float32)).astype(jnp.bfloat16)
+    summed = summed.reshape((n_dp * n_col,) + blocks.shape[1:])
+    groups = [[m for m in range(n_dp * n_rc) if (m // n_col) % n_row == r] for r in range(n_row)]
     got = lax.all_to_all(summed, ("dp", "row", "col"), 0, 0, axis_index_groups=groups)
     total = jnp.sum(got.astype(jnp.float32), axis=0)
     return total.reshape(cols // n_rc, slots // n_dp).T

time: 110 us -> 115 us (1.045)
  waiting for transfers between devices: 21.1 us -> 28.6 us
  blocking collectives: 56.2 us -> 52.6 us
    ppermute x0 -> x1, waiting for transfers between devices: none -> 7.53 us  [body(): other = lax.ppermute(other, 'row', [(r, r ^ 2) for r in range(n_row)])]
    all_to_all x1, blocking collectives: 21.8 us -> 18.1 us  [body(): lax.all_to_all(summed, ('dp', 'row', 'col'), 0, 0, axis_index_groups=groups)]
  transfers between devices with their start and end apart: 2 -> 3, of which waited for: 2 -> 3; matrix products, arithmetic and copies ran while one was open for 3% -> 3% of each run, Pallas kernels for 0% -> 0%
where the time goes in v18:
time: 115 us
  blocking collectives  52.6 us (46%)
  waiting for transfers between devices  28.6 us (25%)
  matrix products  16.3 us (14%)
  local copies, waits for them, and re-layouts  9.95 us (9%)
  starting transfers between devices  4.58 us (4%)
  other arithmetic  2.8 us (2%)
    all_to_all x1, blocking collectives, reduce_scatter(): got = lax.all_to_all(pieces, axis, 0, 0)  34.5 us
    all_to_all x1, waiting for transfers between devices, body(): lax.all_to_all(jnp.broadcast_to(gram_keys[None], (n_dp,) + gram_keys.shap...  19.2 us
    all_to_all x1, blocking collectives, body(): lax.all_to_all(summed, ('dp', 'row', 'col'), 0, 0, axis_index_groups=groups)  18.1 us
    dot_general x1, matrix products, body(): jnp.dot(inverse_gram, edit_keys, preferred_element_type=jnp.float32)  11.7 us
    ppermute x1, waiting for transfers between devices, body(): other = lax.ppermute(other, 'row', [(r, r ^ 2) for r in range(n_row)])  7.53 us
    all_to_all x1, starting transfers between devices, body(): lax.all_to_all(jnp.broadcast_to(gram_keys[None], (n_dp,) + gram_keys.shap...  3.59 us
    reshape x1, local copies, waits for them, and re-layouts, body(): hidden_acts.reshape(hidden_acts.shape[0], n_dp, hidden_acts.shape[1] // n...  3.32 us
    dot_general x1, matrix products, body(): lax.dot_general(acts, gathered, (((1, 2), (0, 1)), ((), ())), preferred_e...  2.79 us
  transfers between devices with their start and end apart: 3, of which 3 were waited for; matrix products, arithmetic and copies ran while one was open for 3% of the time, Pallas kernels for 0%

profile of v18, /device:TPU:0, one launch (start us, length us, event | category | flops | bytes accessed | tf_op | source)
XLA Modules:
  0.0 115.0 jit_solution(3267813878436303921)
XLA Ops:
  0.0 11.7 %convolution_convert_fusion = bf16[1848,512]{1,0:T(8,128)(2,1)S(1)} fusion(bf16[1848,3696]{1,0:T(8,128)(2,1)} %param.17, bf16[3696,512]{1,0:T(8,128)(2,1)} %param.18), kind=kOutput, calls=%fused_computation | convolution fusion | flops 6995079168 | bytes 19337472 | tf_op jit(solution)/shard_map/dot_general | solution.py:38
  11.7 1.8 %reshape.22 = bf16[8,231,512]{2,1,0:T(8,128)(2,1)} reshape(bf16[1848,512]{1,0:T(8,128)(2,1)S(1)} %convolution_convert_fusion) | data formatting | bytes 3784704 | tf_op jit(solution)/shard_map/reshape | solution.py:8
  13.6 0.0 copy-start.4
  13.6 34.5 %all_to_all.15 = bf16[8,231,512]{2,1,0:T(8,128)(2,1)S(1)} all-to-all(bf16[8,231,512]{2,1,0:T(8,128)(2,1)} %reshape.22), channel_id=1, replica_groups=mesh['dp'=8,'row'=4,'col'=4] {'dp'}, dimensions={0} | all-to-all | bytes 3784704 | tf_op jit(solution)/shard_map/all_to_all | solution.py:9
  48.0 0.3 reduce_sum.31
  48.4 0.0 copy-done.4
  48.4 0.4 convolution_convert_fusion.1
  48.8 1.4 %broadcast_in_dim.49 = bf16[8,231,512]{2,1,0:T(8,128)(2,1)} broadcast(bf16[231,512]{1,0:T(8,128)(2,1)S(1)} %convolution_convert_fusion.1), dimensions={1,2} | broadcast | bytes 2128896 | tf_op jit(solution)/shard_map/broadcast_in_dim | solution.py:42
  50.2 3.6 %all-to-all-start.1 = ((bf16[8,231,512]{2,1,0:T(8,128)(2,1)}), bf16[8,231,512]{2,1,0:T(8,128)(2,1)S(1)}, u32[]{:S(2)}, u32[]{:S(2)}) async-start(bf16[8,231,512]{2,1,0:T(8,128)(2,1)} %broadcast_in_dim.49), calls=%async_computation.1 | async-start | bytes 3801088 | tf_op jit(solution)/shard_map/all_to_all | solution.py:42
  53.8 0.0 copy-start.1
  53.8 0.0 copy-start.2
  53.8 0.0 copy-start.3
  53.8 3.3 %reshape.23 = bf16[512,8,231]{0,2,1:T(8,128)(2,1)} reshape(bf16[512,1848]{0,1:T(8,128)(2,1)} %param.12) | data formatting | bytes 3784704 | tf_op jit(solution)/shard_map/reshape | solution.py:43
  57.1 0.0 copy-done.1
  57.1 0.0 copy-done.2
  57.1 0.2 select_reduce_fusion
  57.4 0.0 copy-done.3
  57.4 0.0 copy-start
  57.4 19.2 %all-to-all-done.1 = bf16[8,231,512]{2,1,0:T(8,128)(2,1)S(1)} async-done(((bf16[8,231,512]{2,1,0:T(8,128)(2,1)}), bf16[8,231,512]{2,1,0:T(8,128)(2,1)S(1)}, u32[]{:S(2)}, u32[]{:S(2)}) %all-to-all-start.1) | async-done | bytes 1892384 | tf_op jit(solution)/shard_map/all_to_all | solution.py:42
  76.6 2.8 %convolution_bitcast_fusion = f32[512,512]{0,1:T(8,128)S(1)} fusion(bf16[8,231,512]{2,1,0:T(8,128)(2,1)S(1)} %all-to-all-done.1, bf16[512,8,231]{0,2,1:T(8,128)(2,1)} %reshape.23), kind=kOutput, calls=%fused_computation.2 | convolution fusion | flops 968884224 | bytes 4833280 | tf_op jit(solution)/shard_map/dot_general | solution.py:44
  79.4 0.0 copy-done
  79.4 1.4 %fusion = f32[1024,512]{0,1:S(1)} fusion(f32[512,512]{0,1:T(8,128)S(1)} %convolution_bitcast_fusion, bf16[512,1024]{1,0:T(8,128)(2,1)S(1)} %copy-done, f32[512]{0:T(512)S(1)} %select_multiply_fusion), kind=kOutput, calls=%fused_computation.4 | convolution fusion | flops 1612185600 | bytes 4196352
  80.8 0.2 convert_bitcast_fusion
  81.0 1.1 copy.14
  82.0 1.5 %reshape_reshape.3 = bf16[8,2,2,4,2,2048]{5,4,3,2,1,0:T(2,128)(2,1)S(1)} reshape(bf16[8,1024,64]{2,1,0:T(8,128)(2,1)S(1)} %copy.14) | data formatting | bytes 2097152 | tf_op jit(solution)/shard_map/reshape;reshape | solution.py:58
  83.6 0.5 fusion.3
  84.0 0.1 collective-permute-start
  84.2 1.9 %collective-permute-done = bf16[8,2,4,2,2048]{4,3,2,1,0:T(2,128)(2,1)S(1)} collective-permute-done((bf16[8,2,4,2,2048]{4,3,2,1,0:T(2,128)(2,1)S(1)}, bf16[8,2,4,2,2048]{4,3,2,1,0:T(2,128)(2,1)S(1)}, u32[]{:S(2)}, u32[]{:S(2)}) %collective-permute-start) | collective-permute-done | bytes 524320 | tf_op jit(solution)/shard_map/ppermute | solution.py:61
  86.0 0.8 add_convert_fusion
  86.8 0.2 fusion.6
  87.1 0.9 collective-permute-start.1
  88.0 7.5 %collective-permute-done.1 = bf16[8,4,2,2048]{3,2,1,0:T(2,128)(2,1)S(1)} collective-permute-done((bf16[8,4,2,2048]{3,2,1,0:T(2,128)(2,1)S(1)}, bf16[8,4,2,2048]{3,2,1,0:T(2,128)(2,1)S(1)}, u32[]{:S(2)}, u32[]{:S(2)}) %collective-permute-start.1) | collective-permute-done | bytes 262176 | tf_op jit(solution)/shard_map/ppermute | solution.py:66
  95.5 0.3 add_convert_fusion.1
  95.8 18.1 %all_to_all.16 = bf16[32,2,2048]{2,1,0:T(2,128)(2,1)S(1)} all-to-all(bf16[32,2,2048]{2,1,0:T(2,128)(2,1)S(1)} %bitcast.38), channel_id=1, replica_groups={{0,1,2,3,16,17,18,19,32,33,34,35,48,49,50,51,64,65,66,67,80,81,82,83,96..., dimensions={0} | all-to-all | bytes 524288 | tf_op jit(solution)/shard_map/all_to_all | solution.py:70
  114.0 0.2 convert_reduce_fusion
  114.2 0.1 reshape.26
  114.3 0.7 copy.17
  (1 shorter events, 0.0 us)
Async XLA Ops:
  13.6 34.8 %copy-start.4 = (s32[512]{0:T(512)S(1)}, s32[512]{0:T(512)}, u32[]{:S(2)}) copy-start(s32[512]{0:T(512)} %param.19) | copy-start | bytes 6148
  50.2 26.5 %all-to-all-start.1 = ((bf16[8,231,512]{2,1,0:T(8,128)(2,1)}), bf16[8,231,512]{2,1,0:T(8,128)(2,1)S(1)}, u32[]{:S(2)}, u32[]{:S(2)}) async-start(bf16[8,231,512]{2,1,0:T(8,128)(2,1)} %broadcast_in_dim.49), calls=%async_computation.1 | async-start | bytes 3801088 | tf_op jit(solution)/shard_map/all_to_all | solution.py:42
  53.8 3.4 %copy-start.1 = (f32[512]{0:T(512)S(1)}, f32[512]{0:T(512)}, u32[]{:S(2)}) copy-start(f32[512]{0:T(512)} %param.16) | copy-start | bytes 6148
  53.8 3.4 %copy-start.2 = (s32[512]{0:T(512)S(1)}, s32[512]{0:T(512)}, u32[]{:S(2)}) copy-start(s32[512]{0:T(512)} %param.15) | copy-start | bytes 6148
  53.8 3.6 %copy-start.3 = (s32[512]{0:T(512)S(1)}, s32[512]{0:T(512)}, u32[]{:S(2)}) copy-start(s32[512]{0:T(512)} %param.14) | copy-start | bytes 6148
  57.4 22.0 %copy-start = (bf16[512,1024]{1,0:T(8,128)(2,1)S(1)}, bf16[512,1024]{1,0:T(8,128)(2,1)}, u32[]{:S(2)}) copy-start(bf16[512,1024]{1,0:T(8,128)(2,1)} %param.13) | copy-start | bytes 3145732
  84.0 2.0 %collective-permute-start = (bf16[8,2,4,2,2048]{4,3,2,1,0:T(2,128)(2,1)S(1)}, bf16[8,2,4,2,2048]{4,3,2,1,0:T(2,128)(2,1)S(1)}, u32[]{:S(2)}, u32[]{:S(2)}) collective-permute-start(bf16[8,2,4,2,2048]{4,3,2,1,0:T(2,128)(2,1)S(1)} %fusion.3), channel_id=1, source_target_pairs={{0,4},{4,0},{8,12},{12,8},{1,5},{5,1},{9,13},{13,9},{2,6},{6,2},{1... | collective-permute-start | bytes 1572872 | tf_op jit(solution)/shard_map/ppermute | solution.py:61
  87.1 8.4 %collective-permute-start.1 = (bf16[8,4,2,2048]{3,2,1,0:T(2,128)(2,1)S(1)}, bf16[8,4,2,2048]{3,2,1,0:T(2,128)(2,1)S(1)}, u32[]{:S(2)}, u32[]{:S(2)}) collective-permute-start(bf16[8,4,2,2048]{3,2,1,0:T(2,128)(2,1)S(1)} %fusion.6), channel_id=1, source_target_pairs={{0,8},{4,12},{8,0},{12,4},{1,9},{5,13},{9,1},{13,5},{2,10},{6,14},... | collective-permute-start | bytes 786440 | tf_op jit(solution)/shard_map/ppermute | solution.py:66

commit v19 on v17

--- a/solution.py
+++ b/solution.py
@@ -37,10 +37,11 @@
 
     gram_keys = jnp.dot(inverse_gram, edit_keys, preferred_element_type=jnp.float32)
     gram_keys = reduce_scatter(gram_keys.astype(jnp.bfloat16), "dp", n_dp)
+    acts = hidden_acts.reshape(hidden_acts.shape[0], n_dp, hidden_acts.shape[1] // n_dp)
+    acts, gram_keys = lax.optimization_barrier((acts, gram_keys))
     order = (jnp.arange(edits, dtype=jnp.int32)[:, None] == edit_slots[None, :]).astype(jnp.bfloat16)
     gram_keys = jnp.dot(gram_keys.astype(jnp.bfloat16), order, preferred_element_type=jnp.float32).astype(jnp.bfloat16)
     gathered = lax.all_to_all(jnp.broadcast_to(gram_keys[None], (n_dp,) + gram_keys.shape), "dp", 0, 0)
-    acts = hidden_acts.reshape(hidden_acts.shape[0], n_dp, hidden_acts.shape[1] // n_dp)
     acts_keys = lax.dot_general(acts, gathered, (((1, 2), (0, 1)), ((), ())), preferred_element_type=jnp.float32)
     slots = acts_keys.shape[1]
     cols = scaled.shape[1]

time: 110 us -> 111 us (level)
  blocking collectives: 56.2 us -> 21.8 us
  waiting for transfers between devices: 21.1 us -> 47.1 us
  starting transfers between devices: 3.68 us -> 12.9 us
    all_to_all x1 -> x0, blocking collectives: 34.5 us -> none  [reduce_scatter(): got = lax.all_to_all(pieces, axis, 0, 0)]
    all_to_all x0 -> x1, waiting for transfers between devices: none -> 20.9 us  [reduce_scatter(): got = lax.all_to_all(pieces, axis, 0, 0)]
    all_to_all x0 -> x1, starting transfers between devices: none -> 7.89 us  [reduce_scatter(): got = lax.all_to_all(pieces, axis, 0, 0)]
    all_to_all x1, waiting for transfers between devices: 19.2 us -> 24.3 us  [body(): lax.all_to_all(jnp.broadcast_to(gram_keys[None], (n_dp,) + gram_keys.shap...]
    all_to_all x1, starting transfers between devices: 3.59 us -> 4.9 us  [body(): lax.all_to_all(jnp.broadcast_to(gram_keys[None], (n_dp,) + gram_keys.shap...]
  transfers between devices with their start and end apart: 2 -> 3, of which waited for: 2 -> 3; matrix products, arithmetic and copies ran while one was open for 3% -> 3% of each run, Pallas kernels for 0% -> 0%
where the time goes in v19:
time: 111 us; the launch traced here: 110 us
  waiting for transfers between devices  47.1 us (42%)
  blocking collectives  21.8 us (20%)
  matrix products  16.3 us (15%)
  starting transfers between devices  12.9 us (12%)
  local copies, waits for them, and re-layouts  9.96 us (9%)
  other arithmetic  2.29 us (2%)
    all_to_all x1, waiting for transfers between devices, body(): lax.all_to_all(jnp.broadcast_to(gram_keys[None], (n_dp,) + gram_keys.shap...  24.3 us
    all_to_all x1, blocking collectives, body(): lax.all_to_all(summed, ('dp', 'row', 'col'), 0, 0, axis_index_groups=groups)  21.8 us
    all_to_all x1, waiting for transfers between devices, reduce_scatter(): got = lax.all_to_all(pieces, axis, 0, 0)  20.9 us
    dot_general x1, matrix products, body(): jnp.dot(inverse_gram, edit_keys, preferred_element_type=jnp.float32)  11.7 us
    all_to_all x1, starting transfers between devices, reduce_scatter(): got = lax.all_to_all(pieces, axis, 0, 0)  7.89 us
    all_to_all x1, starting transfers between devices, body(): lax.all_to_all(jnp.broadcast_to(gram_keys[None], (n_dp,) + gram_keys.shap...  4.9 us
    reshape x1, local copies, waits for them, and re-layouts, body(): hidden_acts.reshape(hidden_acts.shape[0], n_dp, hidden_acts.shape[1] // n...  3.35 us
    dot_general x1, matrix products, body(): lax.dot_general(acts, gathered, (((1, 2), (0, 1)), ((), ())), preferred_e...  2.81 us
  transfers between devices with their start and end apart: 3, of which 3 were waited for; matrix products, arithmetic and copies ran while one was open for 3% of the time, Pallas kernels for 0%

profile of v19, /device:TPU:0, one launch (start us, length us, event | category | flops | bytes accessed | tf_op | source)
XLA Modules:
  0.0 110.5 jit_solution(66099382398229104)
XLA Ops:
  0.0 11.7 %convolution_convert_fusion = bf16[1848,512]{1,0:T(8,128)(2,1)S(1)} fusion(bf16[1848,3696]{1,0:T(8,128)(2,1)} %param.15, bf16[3696,512]{1,0:T(8,128)(2,1)} %param.16), kind=kOutput, calls=%fused_computation.1 | convolution fusion | flops 6995079168 | bytes 19337472 | tf_op jit(solution)/shard_map/dot_general | solution.py:38
  11.7 1.8 %reshape.22 = bf16[8,231,512]{2,1,0:T(8,128)(2,1)} reshape(bf16[1848,512]{1,0:T(8,128)(2,1)S(1)} %convolution_convert_fusion) | data formatting | bytes 3784704 | tf_op jit(solution)/shard_map/reshape | solution.py:8
  13.6 7.9 %all-to-all-start = ((bf16[8,231,512]{2,1,0:T(8,128)(2,1)}), bf16[8,231,512]{2,1,0:T(8,128)(2,1)S(1)}, u32[]{:S(2)}, u32[]{:S(2)}) async-start(bf16[8,231,512]{2,1,0:T(8,128)(2,1)} %reshape.22), calls=%async_computation | async-start | bytes 3801088 | tf_op jit(solution)/shard_map/all_to_all | solution.py:9
  21.4 0.0 copy-start.5
  21.4 3.4 %reshape.21 = bf16[512,8,231]{0,2,1:T(8,128)(2,1)} reshape(bf16[512,1848]{0,1:T(8,128)(2,1)} %param.10) | data formatting | bytes 3784704 | tf_op jit(solution)/shard_map/reshape | solution.py:40
  24.8 20.9 %all-to-all-done = bf16[8,231,512]{2,1,0:T(8,128)(2,1)S(1)} async-done(((bf16[8,231,512]{2,1,0:T(8,128)(2,1)}), bf16[8,231,512]{2,1,0:T(8,128)(2,1)S(1)}, u32[]{:S(2)}, u32[]{:S(2)}) %all-to-all-start) | async-done | bytes 1892384 | tf_op jit(solution)/shard_map/all_to_all | solution.py:9
  45.8 0.3 convert_reduce_fusion
  46.0 0.0 copy-done.5
  46.0 0.4 convolution_convert_fusion.1
  46.4 1.4 %broadcast_in_dim.40 = bf16[8,231,512]{2,1,0:T(8,128)(2,1)} broadcast(bf16[231,512]{1,0:T(8,128)(2,1)S(1)} %convolution_convert_fusion.1), dimensions={1,2} | broadcast | bytes 2128896 | tf_op jit(solution)/shard_map/broadcast_in_dim | solution.py:44
  47.8 0.0 copy-start.2
  47.8 0.0 copy-start.3
  47.8 0.0 copy-start.4
  47.8 0.0 copy-start
  47.8 4.9 %all-to-all-start.1 = ((bf16[8,231,512]{2,1,0:T(8,128)(2,1)}), bf16[8,231,512]{2,1,0:T(8,128)(2,1)}, u32[]{:S(2)}, u32[]{:S(2)}) async-start(bf16[8,231,512]{2,1,0:T(8,128)(2,1)} %broadcast_in_dim.40), calls=%async_computation.1 | async-start | bytes 3801088 | tf_op jit(solution)/shard_map/all_to_all | solution.py:44
  52.7 0.0 copy-done.2
  52.7 0.0 copy-done.3
  52.7 0.2 select_reduce_fusion
  53.0 0.0 copy-done.4
  53.0 0.0 copy-start.1
  53.0 24.3 %all-to-all-done.1 = bf16[8,231,512]{2,1,0:T(8,128)(2,1)} async-done(((bf16[8,231,512]{2,1,0:T(8,128)(2,1)}), bf16[8,231,512]{2,1,0:T(8,128)(2,1)}, u32[]{:S(2)}, u32[]{:S(2)}) %all-to-all-start.1) | async-done | bytes 1892384 | tf_op jit(solution)/shard_map/all_to_all | solution.py:44
  77.3 0.0 copy-done
  77.3 2.8 %convolution_bitcast_fusion = f32[512,512]{0,1:T(8,128)S(1)} fusion(bf16[512,8,231]{0,2,1:T(8,128)(2,1)S(1)} %copy-done, bf16[8,231,512]{2,1,0:T(8,128)(2,1)} %all-to-all-done.1), kind=kOutput, calls=%fused_computation.3 | convolution fusion | flops 968884224 | bytes 4833280 | tf_op jit(solution)/shard_map/dot_general | solution.py:45
  80.1 0.0 copy-done.1
  80.1 1.4 %fusion = f32[1024,512]{0,1:S(1)} fusion(f32[512,512]{0,1:T(8,128)S(1)} %convolution_bitcast_fusion, bf16[512,1024]{1,0:T(8,128)(2,1)S(1)} %copy-done.1, f32[512]{0:T(512)S(1)} %select_multiply_fusion), kind=kOutput, calls=%fused_computation.5 | convolution fusion | flops 1612185600 | bytes 4196352
  81.5 0.2 convert_bitcast_fusion
  81.7 1.1 copy.13
  82.8 1.5 %reshape_reshape.3 = bf16[8,2,2,4,2,2048]{5,4,3,2,1,0:T(2,128)(2,1)S(1)} reshape(bf16[8,1024,64]{2,1,0:T(8,128)(2,1)S(1)} %copy.13) | data formatting | bytes 2097152 | tf_op jit(solution)/shard_map/reshape;reshape | solution.py:59
  84.3 0.5 fusion.3
  84.7 0.1 collective-permute-start
  84.8 1.9 %collective-permute-done = bf16[8,2,4,2,2048]{4,3,2,1,0:T(2,128)(2,1)S(1)} collective-permute-done((bf16[8,2,4,2,2048]{4,3,2,1,0:T(2,128)(2,1)S(1)}, bf16[8,2,4,2,2048]{4,3,2,1,0:T(2,128)(2,1)S(1)}, u32[]{:S(2)}, u32[]{:S(2)}) %collective-permute-start) | collective-permute-done | bytes 524320 | tf_op jit(solution)/shard_map/ppermute | solution.py:62
  86.7 0.7 add_convert_fusion
  87.5 21.8 %all_to_all.15 = bf16[64,2,2048]{2,1,0:T(2,128)(2,1)S(1)} all-to-all(bf16[64,2,2048]{2,1,0:T(2,128)(2,1)S(1)} %bitcast.28), channel_id=1, replica_groups={{0,1,2,3,8,9,10,11,16,17,18,19,24,25,26,27,32,33,34,35,40,41,42,43,48,4..., dimensions={0} | all-to-all | bytes 1048576 | tf_op jit(solution)/shard_map/all_to_all | solution.py:66
  109.2 0.4 convert_reduce_fusion.1
  109.7 0.1 reshape.25
  109.8 0.7 copy.15
  (1 shorter events, 0.0 us)
Async XLA Ops:
  13.6 32.2 %all-to-all-start = ((bf16[8,231,512]{2,1,0:T(8,128)(2,1)}), bf16[8,231,512]{2,1,0:T(8,128)(2,1)S(1)}, u32[]{:S(2)}, u32[]{:S(2)}) async-start(bf16[8,231,512]{2,1,0:T(8,128)(2,1)} %reshape.22), calls=%async_computation | async-start | bytes 3801088 | tf_op jit(solution)/shard_map/all_to_all | solution.py:9
  21.4 24.6 %copy-start.5 = (s32[512]{0:T(512)S(1)}, s32[512]{0:T(512)}, u32[]{:S(2)}) copy-start(s32[512]{0:T(512)} %param.17) | copy-start | bytes 6148
  47.8 4.9 %copy-start.2 = (f32[512]{0:T(512)S(1)}, f32[512]{0:T(512)}, u32[]{:S(2)}) copy-start(f32[512]{0:T(512)} %param.14) | copy-start | bytes 6148
  47.8 4.9 %copy-start.3 = (s32[512]{0:T(512)S(1)}, s32[512]{0:T(512)}, u32[]{:S(2)}) copy-start(s32[512]{0:T(512)} %param.13) | copy-start | bytes 6148
  47.8 5.2 %copy-start.4 = (s32[512]{0:T(512)S(1)}, s32[512]{0:T(512)}, u32[]{:S(2)}) copy-start(s32[512]{0:T(512)} %param.12) | copy-start | bytes 6148
  47.8 29.5 %copy-start = (bf16[512,8,231]{0,2,1:T(8,128)(2,1)S(1)}, bf16[512,8,231]{0,2,1:T(8,128)(2,1)}, u32[]{:S(2)}) copy-start(bf16[512,8,231]{0,2,1:T(8,128)(2,1)} %reshape.21) | copy-start | bytes 5677060
  47.8 29.5 %all-to-all-start.1 = ((bf16[8,231,512]{2,1,0:T(8,128)(2,1)}), bf16[8,231,512]{2,1,0:T(8,128)(2,1)}, u32[]{:S(2)}, u32[]{:S(2)}) async-start(bf16[8,231,512]{2,1,0:T(8,128)(2,1)} %broadcast_in_dim.40), calls=%async_computation.1 | async-start | bytes 3801088 | tf_op jit(solution)/shard_map/all_to_all | solution.py:44
  53.0 27.1 %copy-start.1 = (bf16[512,1024]{1,0:T(8,128)(2,1)S(1)}, bf16[512,1024]{1,0:T(8,128)(2,1)}, u32[]{:S(2)}) copy-start(bf16[512,1024]{1,0:T(8,128)(2,1)} %param.11) | copy-start | bytes 3145732
  84.7 2.0 %collective-permute-start = (bf16[8,2,4,2,2048]{4,3,2,1,0:T(2,128)(2,1)S(1)}, bf16[8,2,4,2,2048]{4,3,2,1,0:T(2,128)(2,1)S(1)}, u32[]{:S(2)}, u32[]{:S(2)}) collective-permute-start(bf16[8,2,4,2,2048]{4,3,2,1,0:T(2,128)(2,1)S(1)} %fusion.3), channel_id=1, source_target_pairs={{0,4},{4,0},{8,12},{12,8},{1,5},{5,1},{9,13},{13,9},{2,6},{6,2},{1... | collective-permute-start | bytes 1572872 | tf_op jit(solution)/shard_map/ppermute | solution.py:62

commit v20 on v17

--- a/solution.py
+++ b/solution.py
@@ -38,8 +38,9 @@
     gram_keys = jnp.dot(inverse_gram, edit_keys, preferred_element_type=jnp.float32)
     gram_keys = reduce_scatter(gram_keys.astype(jnp.bfloat16), "dp", n_dp)
     order = (jnp.arange(edits, dtype=jnp.int32)[:, None] == edit_slots[None, :]).astype(jnp.bfloat16)
-    gram_keys = jnp.dot(gram_keys.astype(jnp.bfloat16), order, preferred_element_type=jnp.float32).astype(jnp.bfloat16)
-    gathered = lax.all_to_all(jnp.broadcast_to(gram_keys[None], (n_dp,) + gram_keys.shape), "dp", 0, 0)
+    copies = jnp.broadcast_to(gram_keys.astype(jnp.bfloat16)[None], (n_dp,) + gram_keys.shape)
+    copies = jnp.dot(copies, order, preferred_element_type=jnp.float32).astype(jnp.bfloat16)
+    gathered = lax.all_to_all(copies, "dp", 0, 0)
     acts = hidden_acts.reshape(hidden_acts.shape[0], n_dp, hidden_acts.shape[1] // n_dp)
     acts_keys = lax.dot_general(acts, gathered, (((1, 2), (0, 1)), ((), ())), preferred_element_type=jnp.float32)
     slots = acts_keys.shape[1]

time: 110 us -> 111 us (level)
  matrix products: 16.3 us -> 18.4 us
  local copies, waits for them, and re-layouts: 9.96 us -> 8.56 us
    dot_general x1, matrix products: 0.38 us -> 2.54 us  [body(): jnp.dot(copies, order, preferred_element_type=jnp.float32)]
    broadcast_in_dim x1 -> x0, local copies, waits for them, and re-layouts: 1.4 us -> none  [body(): jnp.broadcast_to(gram_keys[None], (n_dp,) + gram_keys.shape)]
where the time goes in v20:
time: 111 us
  blocking collectives  56.2 us (51%)
  waiting for transfers between devices  21.1 us (19%)
  matrix products  18.4 us (17%)
  local copies, waits for them, and re-layouts  8.56 us (8%)
  starting transfers between devices  3.68 us (3%)
  other arithmetic  2.36 us (2%)
    all_to_all x1, blocking collectives, reduce_scatter(): got = lax.all_to_all(pieces, axis, 0, 0)  34.5 us
    all_to_all x1, blocking collectives, body(): lax.all_to_all(summed, ('dp', 'row', 'col'), 0, 0, axis_index_groups=groups)  21.8 us
    all_to_all x1, waiting for transfers between devices, body(): gathered = lax.all_to_all(copies, 'dp', 0, 0)  19.2 us
    dot_general x1, matrix products, body(): jnp.dot(inverse_gram, edit_keys, preferred_element_type=jnp.float32)  11.7 us
    all_to_all x1, starting transfers between devices, body(): gathered = lax.all_to_all(copies, 'dp', 0, 0)  3.59 us
    reshape x1, local copies, waits for them, and re-layouts, body(): hidden_acts.reshape(hidden_acts.shape[0], n_dp, hidden_acts.shape[1] // n...  3.33 us
    dot_general x1, matrix products, body(): lax.dot_general(acts, gathered, (((1, 2), (0, 1)), ((), ())), preferred_e...  2.79 us
    dot_general x1, matrix products, body(): jnp.dot(copies, order, preferred_element_type=jnp.float32)  2.54 us
  transfers between devices with their start and end apart: 2, of which 2 were waited for; matrix products, arithmetic and copies ran while one was open for 3% of the time, Pallas kernels for 0%

profile of v20, /device:TPU:0, one launch (start us, length us, event | category | flops | bytes accessed | tf_op | source)
XLA Modules:
  0.0 110.5 jit_solution(8145097872204251795)
XLA Ops:
  0.0 11.7 %convolution_convert_fusion = bf16[1848,512]{1,0:T(8,128)(2,1)S(1)} fusion(bf16[1848,3696]{1,0:T(8,128)(2,1)} %param.15, bf16[3696,512]{1,0:T(8,128)(2,1)} %param.16), kind=kOutput, calls=%fused_computation | convolution fusion | flops 6995079168 | bytes 19337472 | tf_op jit(solution)/shard_map/dot_general | solution.py:38
  11.7 1.8 %reshape.21 = bf16[8,231,512]{2,1,0:T(8,128)(2,1)} reshape(bf16[1848,512]{1,0:T(8,128)(2,1)S(1)} %convolution_convert_fusion) | data formatting | bytes 3784704 | tf_op jit(solution)/shard_map/reshape | solution.py:8
  13.6 0.0 copy-start.4
  13.6 34.5 %all_to_all.15 = bf16[8,231,512]{2,1,0:T(8,128)(2,1)S(1)} all-to-all(bf16[8,231,512]{2,1,0:T(8,128)(2,1)} %reshape.21), channel_id=1, replica_groups=mesh['dp'=8,'row'=4,'col'=4] {'dp'}, dimensions={0} | all-to-all | bytes 3784704 | tf_op jit(solution)/shard_map/all_to_all | solution.py:9
  48.0 0.3 reduce_sum.31
  48.4 0.0 copy-done.4
  48.4 2.5 %convolution_convert_fusion.1 = bf16[8,231,512]{2,1,0:T(8,128)(2,1)} fusion(bf16[231,512]{1,0:T(8,128)(2,1)S(1)} %reduce_sum.31, s32[512]{0:T(512)S(1)} %copy-done.4), kind=kOutput, calls=%fused_computation.2 | convolution fusion | flops 970092544 | bytes 2130944 | tf_op jit(solution)/shard_map/dot_general | solution.py:42
  50.9 3.6 %all-to-all-start.1 = ((bf16[8,231,512]{2,1,0:T(8,128)(2,1)}), bf16[8,231,512]{2,1,0:T(8,128)(2,1)S(1)}, u32[]{:S(2)}, u32[]{:S(2)}) async-start(bf16[8,231,512]{2,1,0:T(8,128)(2,1)} %convolution_convert_fusion.1), calls=%async_computation.1 | async-start | bytes 3801088 | tf_op jit(solution)/shard_map/all_to_all | solution.py:43
  54.5 0.0 copy-start.1
  54.5 0.0 copy-start.2
  54.5 0.0 copy-start.3
  54.6 3.3 %reshape.22 = bf16[512,8,231]{0,2,1:T(8,128)(2,1)} reshape(bf16[512,1848]{0,1:T(8,128)(2,1)} %param.10) | data formatting | bytes 3784704 | tf_op jit(solution)/shard_map/reshape | solution.py:44
  57.9 0.0 copy-done.1
  57.9 0.0 copy-done.2
  57.9 0.2 select_reduce_fusion
  58.2 0.0 copy-done.3
  58.2 0.0 copy-start
  58.2 19.2 %all-to-all-done.1 = bf16[8,231,512]{2,1,0:T(8,128)(2,1)S(1)} async-done(((bf16[8,231,512]{2,1,0:T(8,128)(2,1)}), bf16[8,231,512]{2,1,0:T(8,128)(2,1)S(1)}, u32[]{:S(2)}, u32[]{:S(2)}) %all-to-all-start.1) | async-done | bytes 1892384 | tf_op jit(solution)/shard_map/all_to_all | solution.py:43
  77.4 2.8 %convolution_bitcast_fusion = f32[512,512]{0,1:T(8,128)S(1)} fusion(bf16[8,231,512]{2,1,0:T(8,128)(2,1)S(1)} %all-to-all-done.1, bf16[512,8,231]{0,2,1:T(8,128)(2,1)} %reshape.22), kind=kOutput, calls=%fused_computation.3 | convolution fusion | flops 968884224 | bytes 4833280 | tf_op jit(solution)/shard_map/dot_general | solution.py:45
  80.2 0.0 copy-done
  80.2 1.4 %fusion = f32[1024,512]{0,1:S(1)} fusion(f32[512,512]{0,1:T(8,128)S(1)} %convolution_bitcast_fusion, bf16[512,1024]{1,0:T(8,128)(2,1)S(1)} %copy-done, f32[512]{0:T(512)S(1)} %select_multiply_fusion), kind=kOutput, calls=%fused_computation.4 | convolution fusion | flops 1612185600 | bytes 4196352
  81.6 0.2 convert_bitcast_fusion
  81.7 1.1 copy.13
  82.8 1.5 %reshape_reshape.3 = bf16[8,2,2,4,2,2048]{5,4,3,2,1,0:T(2,128)(2,1)S(1)} reshape(bf16[8,1024,64]{2,1,0:T(8,128)(2,1)S(1)} %copy.13) | data formatting | bytes 2097152 | tf_op jit(solution)/shard_map/reshape;reshape | solution.py:59
  84.3 0.5 fusion.6
  84.8 0.1 collective-permute-start
  84.9 1.9 %collective-permute-done = bf16[8,2,4,2,2048]{4,3,2,1,0:T(2,128)(2,1)S(1)} collective-permute-done((bf16[8,2,4,2,2048]{4,3,2,1,0:T(2,128)(2,1)S(1)}, bf16[8,2,4,2,2048]{4,3,2,1,0:T(2,128)(2,1)S(1)}, u32[]{:S(2)}, u32[]{:S(2)}) %collective-permute-start) | collective-permute-done | bytes 524320 | tf_op jit(solution)/shard_map/ppermute | solution.py:62
  86.8 0.7 add_convert_fusion
  87.5 21.8 %all_to_all.16 = bf16[64,2,2048]{2,1,0:T(2,128)(2,1)S(1)} all-to-all(bf16[64,2,2048]{2,1,0:T(2,128)(2,1)S(1)} %bitcast.32), channel_id=1, replica_groups={{0,1,2,3,8,9,10,11,16,17,18,19,24,25,26,27,32,33,34,35,40,41,42,43,48,4..., dimensions={0} | all-to-all | bytes 1048576 | tf_op jit(solution)/shard_map/all_to_all | solution.py:66
  109.3 0.4 convert_reduce_fusion
  109.7 0.1 reshape.25
  109.8 0.7 copy.15
  (1 shorter events, 0.0 us)
Async XLA Ops:
  13.6 34.8 %copy-start.4 = (s32[512]{0:T(512)S(1)}, s32[512]{0:T(512)}, u32[]{:S(2)}) copy-start(s32[512]{0:T(512)} %param.17) | copy-start | bytes 6148
  50.9 26.5 %all-to-all-start.1 = ((bf16[8,231,512]{2,1,0:T(8,128)(2,1)}), bf16[8,231,512]{2,1,0:T(8,128)(2,1)S(1)}, u32[]{:S(2)}, u32[]{:S(2)}) async-start(bf16[8,231,512]{2,1,0:T(8,128)(2,1)} %convolution_convert_fusion.1), calls=%async_computation.1 | async-start | bytes 3801088 | tf_op jit(solution)/shard_map/all_to_all | solution.py:43
  54.5 3.4 %copy-start.1 = (f32[512]{0:T(512)S(1)}, f32[512]{0:T(512)}, u32[]{:S(2)}) copy-start(f32[512]{0:T(512)} %param.14) | copy-start | bytes 6148
  54.5 3.4 %copy-start.2 = (s32[512]{0:T(512)S(1)}, s32[512]{0:T(512)}, u32[]{:S(2)}) copy-start(s32[512]{0:T(512)} %param.13) | copy-start | bytes 6148
  54.5 3.6 %copy-start.3 = (s32[512]{0:T(512)S(1)}, s32[512]{0:T(512)}, u32[]{:S(2)}) copy-start(s32[512]{0:T(512)} %param.12) | copy-start | bytes 6148
  58.2 22.0 %copy-start = (bf16[512,1024]{1,0:T(8,128)(2,1)S(1)}, bf16[512,1024]{1,0:T(8,128)(2,1)}, u32[]{:S(2)}) copy-start(bf16[512,1024]{1,0:T(8,128)(2,1)} %param.11) | copy-start | bytes 3145732
  84.8 2.0 %collective-permute-start = (bf16[8,2,4,2,2048]{4,3,2,1,0:T(2,128)(2,1)S(1)}, bf16[8,2,4,2,2048]{4,3,2,1,0:T(2,128)(2,1)S(1)}, u32[]{:S(2)}, u32[]{:S(2)}) collective-permute-start(bf16[8,2,4,2,2048]{4,3,2,1,0:T(2,128)(2,1)S(1)} %fusion.6), channel_id=1, source_target_pairs={{0,4},{4,0},{8,12},{12,8},{1,5},{5,1},{9,13},{13,9},{2,6},{6,2},{1... | collective-permute-start | bytes 1572872 | tf_op jit(solution)/shard_map/ppermute | solution.py:62
